TPU v7x, 128 devices: a whole 4x4x4 slice. The times are simulated.
128 devices in a mesh: tm: 4 (over y_hi, core), space: 32 (over x, y_lo, z).
Axes of the slice: x: 4, y: 4 (y_hi: 2, y_lo: 2; y = y_hi * 2 + y_lo), z: 4, core: 2. Of those that a mesh axis runs over, the one named last changes fastest.
Arguments:
- query_rows: bfloat16 [32768, 2560], P(('tm', 'space')), may hold values from -18 to 18
- key_rows: bfloat16 [32768, 2560], P(('tm', 'space')), may hold values from -7 to 7
- value_rows: bfloat16 [32768, 2560], P(('tm', 'space')), may hold values from -12 to 12
- out_cotangent: bfloat16 [32768, 2560], P(('tm', 'space')), may hold values from -12 to 12
- tile_slot: int32 [32768], P(('tm', 'space')), may hold values from 0 to 32767, as said below
- window_reach: int32 [4, 32, 2], P(None, 'space'), may hold values from 0 to 1, as said below
Outputs:
- attended: bfloat16 [32768, 2560], P(('tm', 'space'))
- query_grad: bfloat16 [32768, 2560], P(('tm', 'space'))
- key_grad: bfloat16 [32768, 2560], P(('tm', 'space'))
- value_grad: bfloat16 [32768, 2560], P(('tm', 'space'))
Inputs may be any that keep to these rules, and one draw needn't show every extreme that they name: `tile_slot`: A permutation of the tile-order positions. The raster tokens r * 256 to r * 256 + 256 - 1 (shard r, counted over tm first, then space) take, for every shard d, exactly the 2 positions d * 256 + r * 2 to d * 256 + r * 2 + 1. `window_reach`: entry 0 is 0 in the lowest slab and entry 1 is 0 in the highest slab.
All inputs are finite; a program needn't handle non-finite values.
Results may differ from a plain program's by a relative error of at most 0.0053.
Values may be sent and summed in bfloat16 or wider, within the bound.
No kernel may reach another device: no remote copies, remote signals or barrier semaphores. Data moves between devices by JAX's collectives and lax.ppermute only.
A program may use at most 192 MiB of HBM per device.

v0:
```python
import functools

import jax
import jax.numpy as jnp
from jax import lax
from jax.experimental import pallas as pl
from jax.experimental.pallas import tpu as pltpu
from jax.sharding import PartitionSpec as P

H = 20
HD = 128
TILE = 256
SETS = 5
CHUNKS = 2
NT_DIMS = (((1,), (1,)), ((), ()))


def _attn_kernel(flags_ref, q_ref, g_ref, k_ref, v_ref, kb_ref, ka_ref, kl_ref, kr_ref,
                 o_ref, dq_ref, dko_ref, dvo_ref, nb_b, nb_a, nb_l, nb_r, s_scr, dp_scr):
    scale = HD ** (-0.5)
    q = q_ref[...]
    g = g_ref[...]
    keys = [kb_ref[0], k_ref[...], ka_ref[0], kl_ref[0], kr_ref[0]]
    vals = [kb_ref[1], v_ref[...], ka_ref[1], kl_ref[1], kr_ref[1]]
    nb_out = [nb_b, None, nb_a, nb_l, nb_r]
    vis = [flags_ref[a] > 0 for a in range(SETS)]

    m = jnp.full((TILE, 1), -1e30, jnp.float32)
    for a in range(SETS):
        s = lax.dot_general(q, keys[a], NT_DIMS, preferred_element_type=jnp.float32) * scale
        s = jnp.where(vis[a], s, -1e30)
        s_scr[a] = s
        m = jnp.maximum(m, jnp.max(s, axis=1, keepdims=True))
    l = jnp.zeros((TILE, 1), jnp.float32)
    for a in range(SETS):
        e = jnp.where(vis[a], jnp.exp(s_scr[a] - m), 0.0)
        s_scr[a] = e
        l = l + jnp.sum(e, axis=1, keepdims=True)
    inv = 1.0 / l
    o = jnp.zeros((TILE, HD), jnp.float32)
    rd = jnp.zeros((TILE, 1), jnp.float32)
    for a in range(SETS):
        p = s_scr[a] * inv
        pb = p.astype(jnp.bfloat16)
        o = o + jnp.dot(pb, vals[a], preferred_element_type=jnp.float32)
        dp = lax.dot_general(g, vals[a], NT_DIMS, preferred_element_type=jnp.float32)
        rd = rd + jnp.sum(p * dp, axis=1, keepdims=True)
        s_scr[a] = p
        dp_scr[a] = dp
        dv = jnp.dot(p.T.astype(jnp.bfloat16), g, preferred_element_type=jnp.float32)
        if a == 1:
            dvo_ref[...] = dv
        else:
            nb_out[a][1] = dv.astype(jnp.bfloat16)
    o_ref[...] = o.astype(jnp.bfloat16)
    dq = jnp.zeros((TILE, HD), jnp.float32)
    for a in range(SETS):
        ds = s_scr[a] * (dp_scr[a] - rd) * scale
        dq = dq + jnp.dot(ds.astype(jnp.bfloat16), keys[a], preferred_element_type=jnp.float32)
        dk = jnp.dot(ds.T.astype(jnp.bfloat16), q, preferred_element_type=jnp.float32)
        if a == 1:
            dko_ref[...] = dk
        else:
            nb_out[a][0] = dk.astype(jnp.bfloat16)
    dq_ref[...] = dq.astype(jnp.bfloat16)


def attend_tile(flags, recv, kv_below, kv_above, kv_left, kv_right):
    tokens = recv.shape[0]
    heads = recv.shape[1] // (4 * HD)
    own = lambda part: pl.BlockSpec((tokens, HD), lambda h, f, part=part: (0, part * heads + h))
    pair = pl.BlockSpec((2, tokens, HD), lambda h, f: (0, 0, h))
    head = pl.BlockSpec((tokens, HD), lambda h, f: (0, h))
    flops = 6 * SETS * 2 * tokens * TILE * HD * heads
    bytes_accessed = (4 * 2 + 4 * 4 + 4 * 2 * 2 + 2 * 2 + 2 * 4 + 4 * 2 * 2) * tokens * HD * heads
    out_shape = (
        jax.ShapeDtypeStruct((tokens, heads * HD), jnp.bfloat16),
        jax.ShapeDtypeStruct((tokens, heads * HD), jnp.bfloat16),
        jax.ShapeDtypeStruct((tokens, heads * HD), jnp.float32),
        jax.ShapeDtypeStruct((tokens, heads * HD), jnp.float32),
    ) + tuple(jax.ShapeDtypeStruct((2, tokens, heads * HD), jnp.bfloat16) for _ in range(4))
    return pl.pallas_call(
        _attn_kernel,
        out_shape=out_shape,
        grid_spec=pltpu.PrefetchScalarGridSpec(
            num_scalar_prefetch=1,
            grid=(heads,),
            in_specs=[own(0), own(3), own(1), own(2), pair, pair, pair, pair],
            out_specs=[head, head, head, head, pair, pair, pair, pair],
            scratch_shapes=[
                pltpu.VMEM((SETS, tokens, TILE), jnp.float32),
                pltpu.VMEM((SETS, tokens, TILE), jnp.float32),
            ],
        ),
        compiler_params=pltpu.CompilerParams(dimension_semantics=("arbitrary",)),
        cost_estimate=pl.CostEstimate(
            flops=flops, transcendentals=SETS * tokens * TILE * heads, bytes_accessed=bytes_accessed
        ),
    )(flags, recv, recv, recv, recv, kv_below, kv_above, kv_left, kv_right)


def shifted(block, axis, distance):
    devices = range(lax.axis_size(axis))
    route = [(i - distance, i) for i in devices if i - distance in devices]
    return lax.ppermute(block, axis, route)


def shards(query_rows, key_rows, value_rows, out_cotangent, tile_slot, window_reach):
    tokens_here, channels = query_rows.shape
    tm_count = lax.axis_size("tm")
    space_count = lax.axis_size("space")
    per_peer = tokens_here // (tm_count * space_count)
    own_rank = lax.axis_index("tm") * space_count + lax.axis_index("space")
    landing = tile_slot // tokens_here * per_peer + tile_slot % tokens_here - own_rank * per_peer
    chosen = (
        jnp.zeros((tokens_here,), jnp.int32)
        .at[landing]
        .set(jnp.arange(tokens_here, dtype=jnp.int32))
    )
    gathered = [rows[chosen] for rows in (query_rows, key_rows, value_rows, out_cotangent)]
    slab_index = lax.axis_index("tm")
    column = lax.axis_index("space")
    own_reach = lax.dynamic_index_in_dim(window_reach, slab_index, 0, keepdims=False)[0]
    flags = jnp.stack(
        [own_reach[0] > 0, own_reach[0] >= 0, own_reach[1] > 0, column > 0, column < space_count - 1]
    ).astype(jnp.int32)
    width = channels // CHUNKS
    backs = []
    gate = None
    for chunk in range(CHUNKS):
        cols = slice(chunk * width, (chunk + 1) * width)
        send = jnp.concatenate([rows[:, cols] for rows in gathered], axis=1)
        recv = lax.all_to_all(send, ("tm", "space"), split_axis=0, concat_axis=0, tiled=True)
        kv_own = jnp.stack([recv[:, width:2 * width], recv[:, 2 * width:3 * width]])
        if gate is not None:
            kv_own = lax.optimization_barrier((kv_own,) + gate)[0]
        halo = (
            shifted(kv_own, "tm", 1),
            shifted(kv_own, "tm", -1),
            shifted(kv_own, "space", 1),
            shifted(kv_own, "space", -1),
        )
        attended, query_grad, key_own, value_own, nb_b, nb_a, nb_l, nb_r = attend_tile(
            flags, recv, *halo
        )
        gate = halo
        backs.append((attended, query_grad, key_own, value_own, nb_b, nb_a, nb_l, nb_r))
    outs = []
    prior = None
    for chunk in range(CHUNKS):
        attended, query_grad, key_own, value_own, nb_b, nb_a, nb_l, nb_r = backs[chunk]
        sends = (nb_b, nb_a, nb_l, nb_r)
        if prior is not None:
            sends = lax.optimization_barrier(sends + prior)[:4]
        elif CHUNKS > 1:
            sends = lax.optimization_barrier(sends + gate)[:4]
        nb_b, nb_a, nb_l, nb_r = sends
        received = (
            shifted(nb_b, "tm", -1),
            shifted(nb_a, "tm", 1),
            shifted(nb_l, "space", -1),
            shifted(nb_r, "space", 1),
        )
        prior = received
        terms = sum(part.astype(jnp.float32) for part in received)
        key_grad = (key_own + terms[0]).astype(jnp.bfloat16)
        value_grad = (value_own + terms[1]).astype(jnp.bfloat16)
        out_tile = jnp.concatenate([attended, query_grad, key_grad, value_grad], axis=1)
        outs.append(lax.all_to_all(out_tile, ("tm", "space"), split_axis=0, concat_axis=0, tiled=True))
    return tuple(
        jnp.concatenate([outs[chunk][:, i * width:(i + 1) * width] for chunk in range(CHUNKS)], axis=1)[landing]
        for i in range(4)
    )


def solution(mesh):
    return jax.shard_map(
        shards,
        mesh=mesh,
        in_specs=(
            P(("tm", "space"), None),
            P(("tm", "space"), None),
            P(("tm", "space"), None),
            P(("tm", "space"), None),
            P(("tm", "space")),
            P(None, "space", None),
        ),
        out_specs=(
            P(("tm", "space"), None),
            P(("tm", "space"), None),
            P(("tm", "space"), None),
            P(("tm", "space"), None),
        ),
        check_vma=False,
    )
```

profile of v0, /device:TPU:1, one launch (start us, length us, event | category | flops | bytes accessed | tf_op | source)
XLA Modules:
  0.0 410.5 jit_solution(3502951902792282321)
XLA Ops:
  18.7 11.9 %all-to-all-start = ((bf16[128,2,5120]{2,1,0:T(2,128)(2,1)}), bf16[128,2,5120]{2,1,0:T(2,128)(2,1)}, u32[]{:S(2)}, u32[]{:S(2)}) async-start(bf16[128,2,5120]{2,1,0:T(2,128)(2,1)} %all_to_all.30), calls=%async_computation | async-start | bytes 5242880 | tf_op jit(solution)/shard_map/all_to_all | solution.py:133
  34.7 31.3 %all-to-all-done = bf16[128,2,5120]{2,1,0:T(2,128)(2,1)} async-done(((bf16[128,2,5120]{2,1,0:T(2,128)(2,1)}), bf16[128,2,5120]{2,1,0:T(2,128)(2,1)}, u32[]{:S(2)}, u32[]{:S(2)}) %all-to-all-start) | async-done | bytes 2621472 | tf_op jit(solution)/shard_map/all_to_all | solution.py:133
  65.9 4.6 %all-to-all-start.1 = ((bf16[128,2,5120]{2,1,0:T(2,128)(2,1)}), bf16[128,2,5120]{2,1,0:T(2,128)(2,1)S(1)}, u32[]{:S(2)}, u32[]{:S(2)}) async-start(bf16[128,2,5120]{2,1,0:T(2,128)(2,1)} %all_to_all.33), calls=%async_computation.1 | async-start | bytes 5242880 | tf_op jit(solution)/shard_map/all_to_all | solution.py:133
  70.6 6.5 %all_to_all.32.q_ref.g_ref.k_ref.v_ref = bf16[256,5120]{1,0:T(8,128)(2,1)} reshape(bf16[128,2,5120]{2,1,0:T(2,128)(2,1)} %all-to-all-done) | data formatting | bytes 5242880 | tf_op jit(solution)/shard_map/all_to_all | solution.py:133
  79.6 5.2 %collective-permute-start = (bf16[2,256,1280]{2,1,0:T(8,128)(2,1)}, bf16[2,256,1280]{2,1,0:T(8,128)(2,1)}, u32[]{:S(2)}, u32[]{:S(2)}) collective-permute-start(bf16[2,256,1280]{2,1,0:T(8,128)(2,1)} %pad_maximum_fusion.4), channel_id=1, source_target_pairs={{0,32},{32,64},{64,96},{1,33},{33,65},{65,97},{2,34},{34,66},{66,9... | collective-permute-start | bytes 3932168 | tf_op jit(solution)/shard_map/ppermute | solution.py:105
  86.7 4.4 %collective-permute-start.2 = (bf16[2,256,1280]{2,1,0:T(8,128)(2,1)}, bf16[2,256,1280]{2,1,0:T(8,128)(2,1)}, u32[]{:S(2)}, u32[]{:S(2)}) collective-permute-start(bf16[2,256,1280]{2,1,0:T(8,128)(2,1)} %pad_maximum_fusion.4), channel_id=1, source_target_pairs={{0,1},{1,2},{2,3},{3,4},{4,5},{5,6},{6,7},{7,8},{8,9},{9,10},{10,1... | collective-permute-start | bytes 3932168 | tf_op jit(solution)/shard_map/ppermute | solution.py:105
  92.4 14.1 %all-to-all-done.1 = bf16[128,2,5120]{2,1,0:T(2,128)(2,1)S(1)} async-done(((bf16[128,2,5120]{2,1,0:T(2,128)(2,1)}), bf16[128,2,5120]{2,1,0:T(2,128)(2,1)S(1)}, u32[]{:S(2)}, u32[]{:S(2)}) %all-to-all-start.1) | async-done | bytes 2621472 | tf_op jit(solution)/shard_map/all_to_all | solution.py:133
  110.5 30.4 %collective-permute-done.kb_ref = bf16[2,256,1280]{2,1,0:T(8,128)(2,1)} collective-permute-done((bf16[2,256,1280]{2,1,0:T(8,128)(2,1)}, bf16[2,256,1280]{2,1,0:T(8,128)(2,1)}, u32[]{:S(2)}, u32[]{:S(2)}) %collective-permute-start) | collective-permute-done | bytes 1310752 | tf_op jit(solution)/shard_map/ppermute | solution.py:105
  155.8 23.2 %shard_map.93 = (bf16[256,1280]{1,0:T(8,128)(2,1)}, bf16[256,1280]{1,0:T(8,128)(2,1)}, f32[256,1280]{1,0:T(8,128)}, f32[256,1280]{1,0:T(8,128)}, bf16[2,256,1280...) custom-call(s32[5]{0:T(128)} %convert_element_type.39.flags_ref, ...), custom_call_target="tpu_custom_call" | custom-call | flops 5033164800 | bytes 22282240 | tf_op jit(solution)/shard_map/pallas_call | solution.py:82
  179.0 10.4 %collective-permute-done.4.kb_ref = bf16[2,256,1280]{2,1,0:T(8,128)(2,1)S(1)} collective-permute-done((bf16[2,256,1280]{2,1,0:T(8,128)(2,1)S(1)}, bf16[2,256,1280]{2,1,0:T(8,128)(2,1)S(1)}, u32[]{:S(2)}, u32[]{:S(2)}) %collective-permute-start.4) | collective-permute-done | bytes 1310752 | tf_op jit(solution)/shard_map/ppermute | solution.py:105
  189.4 20.0 %collective-permute-done.5.ka_ref = bf16[2,256,1280]{2,1,0:T(8,128)(2,1)} collective-permute-done((bf16[2,256,1280]{2,1,0:T(8,128)(2,1)S(1)}, bf16[2,256,1280]{2,1,0:T(8,128)(2,1)}, u32[]{:S(2)}, u32[]{:S(2)}) %collective-permute-start.5) | collective-permute-done | bytes 1310752 | tf_op jit(solution)/shard_map/ppermute | solution.py:105
  210.8 4.1 collective-permute-start.11
  216.8 5.1 %collective-permute-start.9 = (bf16[2,256,1280]{2,1,0:T(8,128)(2,1)}, bf16[2,256,1280]{2,1,0:T(8,128)(2,1)}, u32[]{:S(2)}, u32[]{:S(2)}) collective-permute-start(bf16[2,256,1280]{2,1,0:T(8,128)(2,1)} %get-tuple-element.38), channel_id=1, source_target_pairs={{0,32},{32,64},{64,96},{1,33},{33,65},{65,97},{2,34},{34,66},{66,9... | collective-permute-start | bytes 3932168 | tf_op jit(solution)/shard_map/ppermute | solution.py:105
  222.0 23.2 %shard_map.94 = (bf16[256,1280]{1,0:T(8,128)(2,1)}, bf16[256,1280]{1,0:T(8,128)(2,1)}, f32[256,1280]{1,0:T(8,128)}, f32[256,1280]{1,0:T(8,128)}, bf16[2,256,1280...) custom-call(s32[5]{0:T(128)} %convert_element_type.39.flags_ref, ...), custom_call_target="tpu_custom_call" | custom-call | flops 5033164800 | bytes 22282240 | tf_op jit(solution)/shard_map/pallas_call | solution.py:82
  247.3 5.1 %collective-permute-start.13 = (bf16[2,256,1280]{2,1,0:T(8,128)(2,1)}, bf16[2,256,1280]{2,1,0:T(8,128)(2,1)}, u32[]{:S(2)}, u32[]{:S(2)}) collective-permute-start(bf16[2,256,1280]{2,1,0:T(8,128)(2,1)} %get-tuple-element.50), channel_id=1, source_target_pairs={{0,32},{32,64},{64,96},{1,33},{33,65},{65,97},{2,34},{34,66},{66,9... | collective-permute-start | bytes 3932168 | tf_op jit(solution)/shard_map/ppermute | solution.py:105
  253.8 5.1 %collective-permute-start.15 = (bf16[2,256,1280]{2,1,0:T(8,128)(2,1)}, bf16[2,256,1280]{2,1,0:T(8,128)(2,1)}, u32[]{:S(2)}, u32[]{:S(2)}) collective-permute-start(bf16[2,256,1280]{2,1,0:T(8,128)(2,1)} %get-tuple-element.52), channel_id=1, source_target_pairs={{0,1},{1,2},{2,3},{3,4},{4,5},{5,6},{6,7},{7,8},{8,9},{9,10},{10,1... | collective-permute-start | bytes 3932168 | tf_op jit(solution)/shard_map/ppermute | solution.py:105
  265.3 13.2 %all-to-all-start.2 = ((bf16[128,2,5120]{2,1,0:T(2,128)(2,1)}), bf16[128,2,5120]{2,1,0:T(2,128)(2,1)S(1)}, u32[]{:S(2)}, u32[]{:S(2)}) async-start(bf16[128,2,5120]{2,1,0:T(2,128)(2,1)} %all_to_all.36), calls=%async_computation.2 | async-start | bytes 5242880 | tf_op jit(solution)/shard_map/all_to_all | solution.py:169
  278.5 40.7 %collective-permute-done.12 = bf16[2,256,1280]{2,1,0:T(8,128)(2,1)} collective-permute-done((bf16[2,256,1280]{2,1,0:T(8,128)(2,1)}, bf16[2,256,1280]{2,1,0:T(8,128)(2,1)}, u32[]{:S(2)}, u32[]{:S(2)}) %collective-permute-start.12) | collective-permute-done | bytes 1310752 | tf_op jit(solution)/shard_map/ppermute | solution.py:105
  319.2 5.0 %collective-permute-done.13 = bf16[2,256,1280]{2,1,0:T(8,128)(2,1)} collective-permute-done((bf16[2,256,1280]{2,1,0:T(8,128)(2,1)}, bf16[2,256,1280]{2,1,0:T(8,128)(2,1)}, u32[]{:S(2)}, u32[]{:S(2)}) %collective-permute-start.13) | collective-permute-done | bytes 1310752 | tf_op jit(solution)/shard_map/ppermute | solution.py:105
  330.2 6.3 %all_to_all.39 = bf16[128,2,5120]{2,1,0:T(2,128)(2,1)} reshape(bf16[256,5120]{1,0:T(8,128)(2,1)} %pad_maximum_fusion.3) | data formatting | bytes 5242880 | tf_op jit(solution)/shard_map/all_to_all | solution.py:169
  336.5 11.9 %all-to-all-done.2 = bf16[128,2,5120]{2,1,0:T(2,128)(2,1)S(1)} async-done(((bf16[128,2,5120]{2,1,0:T(2,128)(2,1)}), bf16[128,2,5120]{2,1,0:T(2,128)(2,1)S(1)}, u32[]{:S(2)}, u32[]{:S(2)}) %all-to-all-start.2) | async-done | bytes 2621472 | tf_op jit(solution)/shard_map/all_to_all | solution.py:169
  348.4 8.4 %all-to-all-start.3 = ((bf16[128,2,5120]{2,1,0:T(2,128)(2,1)}), bf16[128,2,5120]{2,1,0:T(2,128)(2,1)}, u32[]{:S(2)}, u32[]{:S(2)}) async-start(bf16[128,2,5120]{2,1,0:T(2,128)(2,1)} %all_to_all.39), calls=%async_computation.3 | async-start | bytes 5242880 | tf_op jit(solution)/shard_map/all_to_all | solution.py:169
  362.4 29.9 %all-to-all-done.3 = bf16[128,2,5120]{2,1,0:T(2,128)(2,1)} async-done(((bf16[128,2,5120]{2,1,0:T(2,128)(2,1)}), bf16[128,2,5120]{2,1,0:T(2,128)(2,1)}, u32[]{:S(2)}, u32[]{:S(2)}) %all-to-all-start.3) | async-done | bytes 2621472 | tf_op jit(solution)/shard_map/all_to_all | solution.py:169
  392.3 5.3 %all_to_all.41 = bf16[256,5120]{1,0:T(8,128)(2,1)S(1)} reshape(bf16[128,2,5120]{2,1,0:T(2,128)(2,1)} %all-to-all-done.3) | data formatting | bytes 5242880 | tf_op jit(solution)/shard_map/all_to_all | solution.py:169
  (106 shorter events, 81.9 us)
Async XLA Ops:
  18.7 47.3 %all-to-all-start = ((bf16[128,2,5120]{2,1,0:T(2,128)(2,1)}), bf16[128,2,5120]{2,1,0:T(2,128)(2,1)}, u32[]{:S(2)}, u32[]{:S(2)}) async-start(bf16[128,2,5120]{2,1,0:T(2,128)(2,1)} %all_to_all.30), calls=%async_computation | async-start | bytes 5242880 | tf_op jit(solution)/shard_map/all_to_all | solution.py:133
  65.9 40.6 %all-to-all-start.1 = ((bf16[128,2,5120]{2,1,0:T(2,128)(2,1)}), bf16[128,2,5120]{2,1,0:T(2,128)(2,1)S(1)}, u32[]{:S(2)}, u32[]{:S(2)}) async-start(bf16[128,2,5120]{2,1,0:T(2,128)(2,1)} %all_to_all.33), calls=%async_computation.1 | async-start | bytes 5242880 | tf_op jit(solution)/shard_map/all_to_all | solution.py:133
  79.6 61.3 %collective-permute-start = (bf16[2,256,1280]{2,1,0:T(8,128)(2,1)}, bf16[2,256,1280]{2,1,0:T(8,128)(2,1)}, u32[]{:S(2)}, u32[]{:S(2)}) collective-permute-start(bf16[2,256,1280]{2,1,0:T(8,128)(2,1)} %pad_maximum_fusion.4), channel_id=1, source_target_pairs={{0,32},{32,64},{64,96},{1,33},{33,65},{65,97},{2,34},{34,66},{66,9... | collective-permute-start | bytes 3932168 | tf_op jit(solution)/shard_map/ppermute | solution.py:105
  84.8 59.6 %collective-permute-start.1 = (bf16[2,256,1280]{2,1,0:T(8,128)(2,1)}, bf16[2,256,1280]{2,1,0:T(8,128)(2,1)}, u32[]{:S(2)}, u32[]{:S(2)}) collective-permute-start(bf16[2,256,1280]{2,1,0:T(8,128)(2,1)} %pad_maximum_fusion.4), channel_id=1, source_target_pairs={{32,0},{64,32},{96,64},{33,1},{65,33},{97,65},{34,2},{66,34},{98,6... | collective-permute-start | bytes 3932168 | tf_op jit(solution)/shard_map/ppermute | solution.py:105
  86.7 57.7 %collective-permute-start.2 = (bf16[2,256,1280]{2,1,0:T(8,128)(2,1)}, bf16[2,256,1280]{2,1,0:T(8,128)(2,1)}, u32[]{:S(2)}, u32[]{:S(2)}) collective-permute-start(bf16[2,256,1280]{2,1,0:T(8,128)(2,1)} %pad_maximum_fusion.4), channel_id=1, source_target_pairs={{0,1},{1,2},{2,3},{3,4},{4,5},{5,6},{6,7},{7,8},{8,9},{9,10},{10,1... | collective-permute-start | bytes 3932168 | tf_op jit(solution)/shard_map/ppermute | solution.py:105
  91.1 53.3 %collective-permute-start.3 = (bf16[2,256,1280]{2,1,0:T(8,128)(2,1)}, bf16[2,256,1280]{2,1,0:T(8,128)(2,1)}, u32[]{:S(2)}, u32[]{:S(2)}) collective-permute-start(bf16[2,256,1280]{2,1,0:T(8,128)(2,1)} %pad_maximum_fusion.4), channel_id=1, source_target_pairs={{1,0},{2,1},{3,2},{4,3},{5,4},{6,5},{7,6},{8,7},{9,8},{10,9},{11,1... | collective-permute-start | bytes 3932168 | tf_op jit(solution)/shard_map/ppermute | solution.py:105
  110.4 42.3 %copy-start.19 = (s32[4,1,2]{0,2,1:T(2,128)S(1)}, s32[4,1,2]{0,2,1:T(2,128)}, u32[]{:S(2)}) copy-start(s32[4,1,2]{0,2,1:T(2,128)} %param.11) | copy-start | bytes 100
  144.4 45.1 %collective-permute-start.4 = (bf16[2,256,1280]{2,1,0:T(8,128)(2,1)S(1)}, bf16[2,256,1280]{2,1,0:T(8,128)(2,1)S(1)}, u32[]{:S(2)}, u32[]{:S(2)}) collective-permute-start(bf16[2,256,1280]{2,1,0:T(8,128)(2,1)S(1)} %pad_maximum_fusion.5), channel_id=1, source_target_pairs={{0,32},{32,64},{64,96},{1,33},{33,65},{65,97},{2,34},{34,66},{66,9... | collective-permute-start | bytes 3932168 | tf_op jit(solution)/shard_map/ppermute | solution.py:105
  146.8 62.7 %collective-permute-start.5 = (bf16[2,256,1280]{2,1,0:T(8,128)(2,1)S(1)}, bf16[2,256,1280]{2,1,0:T(8,128)(2,1)}, u32[]{:S(2)}, u32[]{:S(2)}) collective-permute-start(bf16[2,256,1280]{2,1,0:T(8,128)(2,1)S(1)} %pad_maximum_fusion.5), channel_id=1, source_target_pairs={{32,0},{64,32},{96,64},{33,1},{65,33},{97,65},{34,2},{66,34},{98,6... | collective-permute-start | bytes 3932168 | tf_op jit(solution)/shard_map/ppermute | solution.py:105
  148.8 60.7 %collective-permute-start.6 = (bf16[2,256,1280]{2,1,0:T(8,128)(2,1)S(1)}, bf16[2,256,1280]{2,1,0:T(8,128)(2,1)}, u32[]{:S(2)}, u32[]{:S(2)}) collective-permute-start(bf16[2,256,1280]{2,1,0:T(8,128)(2,1)S(1)} %pad_maximum_fusion.5), channel_id=1, source_target_pairs={{0,1},{1,2},{2,3},{3,4},{4,5},{5,6},{6,7},{7,8},{8,9},{9,10},{10,1... | collective-permute-start | bytes 3932168 | tf_op jit(solution)/shard_map/ppermute | solution.py:105
  151.1 58.3 %collective-permute-start.7 = (bf16[2,256,1280]{2,1,0:T(8,128)(2,1)S(1)}, bf16[2,256,1280]{2,1,0:T(8,128)(2,1)}, u32[]{:S(2)}, u32[]{:S(2)}) collective-permute-start(bf16[2,256,1280]{2,1,0:T(8,128)(2,1)S(1)} %pad_maximum_fusion.5), channel_id=1, source_target_pairs={{1,0},{2,1},{3,2},{4,3},{5,4},{6,5},{7,6},{8,7},{9,8},{10,9},{11,1... | collective-permute-start | bytes 3932168 | tf_op jit(solution)/shard_map/ppermute | solution.py:105
  189.4 20.1 %copy-start.20 = (bf16[2,256,1280]{2,1,0:T(8,128)(2,1)}, bf16[2,256,1280]{2,1,0:T(8,128)(2,1)S(1)}, u32[]{:S(2)}) copy-start(bf16[2,256,1280]{2,1,0:T(8,128)(2,1)S(1)} %collective-permute-done.4.kb_ref) | copy-start | bytes 3932164
  209.5 35.7 %collective-permute-start.10 = (bf16[2,256,1280]{2,1,0:T(8,128)(2,1)}, bf16[2,256,1280]{2,1,0:T(8,128)(2,1)S(1)}, u32[]{:S(2)}, u32[]{:S(2)}) collective-permute-start(bf16[2,256,1280]{2,1,0:T(8,128)(2,1)} %get-tuple-element.39), channel_id=1, source_target_pairs={{1,0},{2,1},{3,2},{4,3},{5,4},{6,5},{7,6},{8,7},{9,8},{10,9},{11,1... | collective-permute-start | bytes 3932168 | tf_op jit(solution)/shard_map/ppermute | solution.py:105
  210.8 34.4 %collective-permute-start.11 = (bf16[2,256,1280]{2,1,0:T(8,128)(2,1)}, bf16[2,256,1280]{2,1,0:T(8,128)(2,1)S(1)}, u32[]{:S(2)}, u32[]{:S(2)}) collective-permute-start(bf16[2,256,1280]{2,1,0:T(8,128)(2,1)} %get-tuple-element.40), channel_id=1, source_target_pairs={{0,1},{1,2},{2,3},{3,4},{4,5},{5,6},{6,7},{7,8},{8,9},{9,10},{10,1... | collective-permute-start | bytes 3932168 | tf_op jit(solution)/shard_map/ppermute | solution.py:105
  214.9 30.4 %collective-permute-start.8 = (bf16[2,256,1280]{2,1,0:T(8,128)(2,1)}, bf16[2,256,1280]{2,1,0:T(8,128)(2,1)}, u32[]{:S(2)}, u32[]{:S(2)}) collective-permute-start(bf16[2,256,1280]{2,1,0:T(8,128)(2,1)} %get-tuple-element.37), channel_id=1, source_target_pairs={{32,0},{64,32},{96,64},{33,1},{65,33},{97,65},{34,2},{66,34},{98,6... | collective-permute-start | bytes 3932168 | tf_op jit(solution)/shard_map/ppermute | solution.py:105
  216.8 28.4 %collective-permute-start.9 = (bf16[2,256,1280]{2,1,0:T(8,128)(2,1)}, bf16[2,256,1280]{2,1,0:T(8,128)(2,1)}, u32[]{:S(2)}, u32[]{:S(2)}) collective-permute-start(bf16[2,256,1280]{2,1,0:T(8,128)(2,1)} %get-tuple-element.38), channel_id=1, source_target_pairs={{0,32},{32,64},{64,96},{1,33},{33,65},{65,97},{2,34},{34,66},{66,9... | collective-permute-start | bytes 3932168 | tf_op jit(solution)/shard_map/ppermute | solution.py:105
  245.3 73.9 %collective-permute-start.12 = (bf16[2,256,1280]{2,1,0:T(8,128)(2,1)}, bf16[2,256,1280]{2,1,0:T(8,128)(2,1)}, u32[]{:S(2)}, u32[]{:S(2)}) collective-permute-start(bf16[2,256,1280]{2,1,0:T(8,128)(2,1)} %get-tuple-element.49), channel_id=1, source_target_pairs={{32,0},{64,32},{96,64},{33,1},{65,33},{97,65},{34,2},{66,34},{98,6... | collective-permute-start | bytes 3932168 | tf_op jit(solution)/shard_map/ppermute | solution.py:105
  247.3 76.8 %collective-permute-start.13 = (bf16[2,256,1280]{2,1,0:T(8,128)(2,1)}, bf16[2,256,1280]{2,1,0:T(8,128)(2,1)}, u32[]{:S(2)}, u32[]{:S(2)}) collective-permute-start(bf16[2,256,1280]{2,1,0:T(8,128)(2,1)} %get-tuple-element.50), channel_id=1, source_target_pairs={{0,32},{32,64},{64,96},{1,33},{33,65},{65,97},{2,34},{34,66},{66,9... | collective-permute-start | bytes 3932168 | tf_op jit(solution)/shard_map/ppermute | solution.py:105
  252.5 71.7 %collective-permute-start.14 = (bf16[2,256,1280]{2,1,0:T(8,128)(2,1)}, bf16[2,256,1280]{2,1,0:T(8,128)(2,1)}, u32[]{:S(2)}, u32[]{:S(2)}) collective-permute-start(bf16[2,256,1280]{2,1,0:T(8,128)(2,1)} %get-tuple-element.51), channel_id=1, source_target_pairs={{1,0},{2,1},{3,2},{4,3},{5,4},{6,5},{7,6},{8,7},{9,8},{10,9},{11,1... | collective-permute-start | bytes 3932168 | tf_op jit(solution)/shard_map/ppermute | solution.py:105
  253.8 70.4 %collective-permute-start.15 = (bf16[2,256,1280]{2,1,0:T(8,128)(2,1)}, bf16[2,256,1280]{2,1,0:T(8,128)(2,1)}, u32[]{:S(2)}, u32[]{:S(2)}) collective-permute-start(bf16[2,256,1280]{2,1,0:T(8,128)(2,1)} %get-tuple-element.52), channel_id=1, source_target_pairs={{0,1},{1,2},{2,3},{3,4},{4,5},{5,6},{6,7},{7,8},{8,9},{9,10},{10,1... | collective-permute-start | bytes 3932168 | tf_op jit(solution)/shard_map/ppermute | solution.py:105
  265.3 83.1 %all-to-all-start.2 = ((bf16[128,2,5120]{2,1,0:T(2,128)(2,1)}), bf16[128,2,5120]{2,1,0:T(2,128)(2,1)S(1)}, u32[]{:S(2)}, u32[]{:S(2)}) async-start(bf16[128,2,5120]{2,1,0:T(2,128)(2,1)} %all_to_all.36), calls=%async_computation.2 | async-start | bytes 5242880 | tf_op jit(solution)/shard_map/all_to_all | solution.py:169
  278.5 48.8 %copy-start.13 = (f32[256,1280]{1,0:T(8,128)S(1)}, f32[256,1280]{1,0:T(8,128)}, u32[]{:S(2)}) copy-start(f32[256,1280]{1,0:T(8,128)} %get-tuple-element.44) | copy-start | bytes 3932164
  278.5 48.8 %copy-start.14 = (f32[256,1280]{1,0:T(8,128)S(1)}, f32[256,1280]{1,0:T(8,128)}, u32[]{:S(2)}) copy-start(f32[256,1280]{1,0:T(8,128)} %get-tuple-element.53) | copy-start | bytes 3932164
  348.4 43.8 %all-to-all-start.3 = ((bf16[128,2,5120]{2,1,0:T(2,128)(2,1)}), bf16[128,2,5120]{2,1,0:T(2,128)(2,1)}, u32[]{:S(2)}, u32[]{:S(2)}) async-start(bf16[128,2,5120]{2,1,0:T(2,128)(2,1)} %all_to_all.39), calls=%async_computation.3 | async-start | bytes 5242880 | tf_op jit(solution)/shard_map/all_to_all | solution.py:169
  (17 other events, 63.2 us)
where the time goes:
time: 412 us; the launch traced here: 410 us
  waiting for transfers between devices  197 us (48%)
  starting transfers between devices  85.2 us (21%)
  local copies, waits for them, and re-layouts  64.6 us (16%)
  Pallas kernels  46.5 us (11%)
  other arithmetic  14 us (3%)
    ppermute x16, waiting for transfers between devices, shifted(): return lax.ppermute(block, axis, route)  110 us
    ppermute x16, starting transfers between devices, shifted(): return lax.ppermute(block, axis, route)  47.1 us
    pallas_call x2, Pallas kernels, attend_tile(): pl.pallas_call(_attn_kernel, out_shape=out_shape, grid_spec=pltpu.Prefetc...  46.5 us
    all_to_all x2, waiting for transfers between devices, shards(): lax.all_to_all(send, ('tm', 'space'), split_axis=0, concat_axis=0, tiled=...  45.4 us
    all_to_all x2, waiting for transfers between devices, shards(): lax.all_to_all(out_tile, ('tm', 'space'), split_axis=0, concat_axis=0, ti...  41.8 us
    all_to_all x2, starting transfers between devices, shards(): lax.all_to_all(out_tile, ('tm', 'space'), split_axis=0, concat_axis=0, ti...  21.6 us
    all_to_all x4, local copies, waits for them, and re-layouts, shards(): lax.all_to_all(out_tile, ('tm', 'space'), split_axis=0, concat_axis=0, ti...  16.6 us
    all_to_all x2, starting transfers between devices, shards(): lax.all_to_all(send, ('tm', 'space'), split_axis=0, concat_axis=0, tiled=...  16.5 us
  transfers between devices with their start and end apart: 20, of which 10 were waited for; matrix products, arithmetic and copies ran while one was open for 4% of the time, Pallas kernels for 11%

commit v1 on v0

--- a/solution.py
+++ b/solution.py
@@ -144,11 +144,13 @@
             flags, recv, *halo
         )
         gate = halo
-        backs.append((attended, query_grad, key_own, value_own, nb_b, nb_a, nb_l, nb_r))
+        early = jnp.concatenate([attended, query_grad], axis=1)
+        early = lax.all_to_all(early, ("tm", "space"), split_axis=0, concat_axis=0, tiled=True)
+        backs.append((early, key_own, value_own, nb_b, nb_a, nb_l, nb_r))
     outs = []
     prior = None
     for chunk in range(CHUNKS):
-        attended, query_grad, key_own, value_own, nb_b, nb_a, nb_l, nb_r = backs[chunk]
+        early, key_own, value_own, nb_b, nb_a, nb_l, nb_r = backs[chunk]
         sends = (nb_b, nb_a, nb_l, nb_r)
         if prior is not None:
             sends = lax.optimization_barrier(sends + prior)[:4]
@@ -165,8 +167,9 @@
         terms = sum(part.astype(jnp.float32) for part in received)
         key_grad = (key_own + terms[0]).astype(jnp.bfloat16)
         value_grad = (value_own + terms[1]).astype(jnp.bfloat16)
-        out_tile = jnp.concatenate([attended, query_grad, key_grad, value_grad], axis=1)
-        outs.append(lax.all_to_all(out_tile, ("tm", "space"), split_axis=0, concat_axis=0, tiled=True))
+        late = jnp.concatenate([key_grad, value_grad], axis=1)
+        late = lax.all_to_all(late, ("tm", "space"), split_axis=0, concat_axis=0, tiled=True)
+        outs.append(jnp.concatenate([early, late], axis=1))
     return tuple(
         jnp.concatenate([outs[chunk][:, i * width:(i + 1) * width] for chunk in range(CHUNKS)], axis=1)[landing]
         for i in range(4)

time: 412 us -> 391 us (0.949)
  waiting for transfers between devices: 197 us -> 155 us
  starting transfers between devices: 85.2 us -> 107 us
  local copies, waits for them, and re-layouts: 64.6 us -> 59.9 us
    ppermute x16, waiting for transfers between devices: 110 us -> 74.9 us  [shifted(): return lax.ppermute(block, axis, route)]
    all_to_all x2 -> x4, starting transfers between devices: 21.6 us -> 40.8 us  [the longest x2 23.2 us: shards(): lax.all_to_all(early, ('tm', 'space'), split_axis=0, concat_axis=0, tiled...]
    all_to_all x2 -> x4, waiting for transfers between devices: 41.8 us -> 34.7 us  [the longest x2 21.5 us: shards(): lax.all_to_all(early, ('tm', 'space'), split_axis=0, concat_axis=0, tiled...]
    all_to_all x4 -> x8, local copies, waits for them, and re-layouts: 16.6 us -> 13.7 us  [the longest x4 9.04 us: shards(): lax.all_to_all(late, ('tm', 'space'), split_axis=0, concat_axis=0, tiled=...]
  transfers between devices with their start and end apart: 20 -> 22, of which waited for: 10 -> 8; matrix products, arithmetic and copies ran while one was open for 4% -> 7% of each run, Pallas kernels for 11% -> 12%
where the time goes in v1:
time: 391 us; the launch traced here: 389 us
  waiting for transfers between devices  155 us (40%)
  starting transfers between devices  107 us (27%)
  local copies, waits for them, and re-layouts  59.9 us (15%)
  Pallas kernels  46.5 us (12%)
  other arithmetic  17.9 us (5%)
    ppermute x16, waiting for transfers between devices, shifted(): return lax.ppermute(block, axis, route)  74.9 us
    ppermute x16, starting transfers between devices, shifted(): return lax.ppermute(block, axis, route)  49.5 us
    pallas_call x2, Pallas kernels, attend_tile(): pl.pallas_call(_attn_kernel, out_shape=out_shape, grid_spec=pltpu.Prefetc...  46.5 us
    all_to_all x2, waiting for transfers between devices, shards(): lax.all_to_all(send, ('tm', 'space'), split_axis=0, concat_axis=0, tiled=...  45.3 us
    all_to_all x2, starting transfers between devices, shards(): lax.all_to_all(early, ('tm', 'space'), split_axis=0, concat_axis=0, tiled...  23.2 us
    all_to_all x2, waiting for transfers between devices, shards(): lax.all_to_all(early, ('tm', 'space'), split_axis=0, concat_axis=0, tiled...  21.5 us
    all_to_all x2, starting transfers between devices, shards(): lax.all_to_all(late, ('tm', 'space'), split_axis=0, concat_axis=0, tiled=...  17.6 us
    all_to_all x2, starting transfers between devices, shards(): lax.all_to_all(send, ('tm', 'space'), split_axis=0, concat_axis=0, tiled=...  16.5 us
  transfers between devices with their start and end apart: 22, of which 8 were waited for; matrix products, arithmetic and copies ran while one was open for 7% of the time, Pallas kernels for 12%

profile of v1, /device:TPU:1, one launch (start us, length us, event | category | flops | bytes accessed | tf_op | source)
XLA Modules:
  0.0 389.1 jit_solution(11392263770062146485)
XLA Ops:
  18.7 11.9 %all-to-all-start = ((bf16[128,2,5120]{2,1,0:T(2,128)(2,1)}), bf16[128,2,5120]{2,1,0:T(2,128)(2,1)}, u32[]{:S(2)}, u32[]{:S(2)}) async-start(bf16[128,2,5120]{2,1,0:T(2,128)(2,1)} %all_to_all.46), calls=%async_computation | async-start | bytes 5242880 | tf_op jit(solution)/shard_map/all_to_all | solution.py:133
  34.6 31.3 %all-to-all-done = bf16[128,2,5120]{2,1,0:T(2,128)(2,1)} async-done(((bf16[128,2,5120]{2,1,0:T(2,128)(2,1)}), bf16[128,2,5120]{2,1,0:T(2,128)(2,1)}, u32[]{:S(2)}, u32[]{:S(2)}) %all-to-all-start) | async-done | bytes 2621472 | tf_op jit(solution)/shard_map/all_to_all | solution.py:133
  65.9 4.6 %all-to-all-start.2 = ((bf16[128,2,5120]{2,1,0:T(2,128)(2,1)}), bf16[128,2,5120]{2,1,0:T(2,128)(2,1)S(1)}, u32[]{:S(2)}, u32[]{:S(2)}) async-start(bf16[128,2,5120]{2,1,0:T(2,128)(2,1)} %all_to_all.52), calls=%async_computation.2 | async-start | bytes 5242880 | tf_op jit(solution)/shard_map/all_to_all | solution.py:133
  70.6 6.5 %all_to_all.48.q_ref.g_ref.k_ref.v_ref = bf16[256,5120]{1,0:T(8,128)(2,1)} reshape(bf16[128,2,5120]{2,1,0:T(2,128)(2,1)} %all-to-all-done) | data formatting | bytes 5242880 | tf_op jit(solution)/shard_map/all_to_all | solution.py:133
  79.6 5.2 %collective-permute-start = (bf16[2,256,1280]{2,1,0:T(8,128)(2,1)}, bf16[2,256,1280]{2,1,0:T(8,128)(2,1)}, u32[]{:S(2)}, u32[]{:S(2)}) collective-permute-start(bf16[2,256,1280]{2,1,0:T(8,128)(2,1)} %pad_maximum_fusion.2), channel_id=1, source_target_pairs={{0,32},{32,64},{64,96},{1,33},{33,65},{65,97},{2,34},{34,66},{66,9... | collective-permute-start | bytes 3932168 | tf_op jit(solution)/shard_map/ppermute | solution.py:105
  86.7 4.4 %collective-permute-start.2 = (bf16[2,256,1280]{2,1,0:T(8,128)(2,1)}, bf16[2,256,1280]{2,1,0:T(8,128)(2,1)}, u32[]{:S(2)}, u32[]{:S(2)}) collective-permute-start(bf16[2,256,1280]{2,1,0:T(8,128)(2,1)} %pad_maximum_fusion.2), channel_id=1, source_target_pairs={{0,1},{1,2},{2,3},{3,4},{4,5},{5,6},{6,7},{7,8},{8,9},{9,10},{10,1... | collective-permute-start | bytes 3932168 | tf_op jit(solution)/shard_map/ppermute | solution.py:105
  92.5 14.0 %all-to-all-done.2 = bf16[128,2,5120]{2,1,0:T(2,128)(2,1)S(1)} async-done(((bf16[128,2,5120]{2,1,0:T(2,128)(2,1)}), bf16[128,2,5120]{2,1,0:T(2,128)(2,1)S(1)}, u32[]{:S(2)}, u32[]{:S(2)}) %all-to-all-start.2) | async-done | bytes 2621472 | tf_op jit(solution)/shard_map/all_to_all | solution.py:133
  110.5 30.4 %collective-permute-done.kb_ref = bf16[2,256,1280]{2,1,0:T(8,128)(2,1)} collective-permute-done((bf16[2,256,1280]{2,1,0:T(8,128)(2,1)}, bf16[2,256,1280]{2,1,0:T(8,128)(2,1)}, u32[]{:S(2)}, u32[]{:S(2)}) %collective-permute-start) | collective-permute-done | bytes 1310752 | tf_op jit(solution)/shard_map/ppermute | solution.py:105
  140.9 3.5 collective-permute-done.1.ka_ref
  156.7 23.3 %shard_map.93 = (bf16[256,1280]{1,0:T(8,128)(2,1)}, bf16[256,1280]{1,0:T(8,128)(2,1)}, f32[256,1280]{1,0:T(8,128)}, f32[256,1280]{1,0:T(8,128)}, bf16[2,256,1280...) custom-call(s32[5]{0:T(128)} %convert_element_type.39.flags_ref, ...), custom_call_target="tpu_custom_call" | custom-call | flops 5033164800 | bytes 22282240 | tf_op jit(solution)/shard_map/pallas_call | solution.py:82
  182.8 13.3 %all-to-all-start.1 = ((bf16[128,2,2560]{2,1,0:T(2,128)(2,1)}), bf16[128,2,2560]{2,1,0:T(2,128)(2,1)S(1)}, u32[]{:S(2)}, u32[]{:S(2)}) async-start(bf16[128,2,2560]{2,1,0:T(2,128)(2,1)} %all_to_all.49), calls=%async_computation.1 | async-start | bytes 2621440 | tf_op jit(solution)/shard_map/all_to_all | solution.py:148
  197.4 5.1 %collective-permute-start.11 = (bf16[2,256,1280]{2,1,0:T(8,128)(2,1)}, bf16[2,256,1280]{2,1,0:T(8,128)(2,1)}, u32[]{:S(2)}, u32[]{:S(2)}) collective-permute-start(bf16[2,256,1280]{2,1,0:T(8,128)(2,1)} %get-tuple-element.42), channel_id=1, source_target_pairs={{0,1},{1,2},{2,3},{3,4},{4,5},{5,6},{6,7},{7,8},{8,9},{9,10},{10,1... | collective-permute-start | bytes 3932168 | tf_op jit(solution)/shard_map/ppermute | solution.py:105
  202.5 3.5 collective-permute-start.8
  206.0 4.0 %collective-permute-start.9 = (bf16[2,256,1280]{2,1,0:T(8,128)(2,1)}, bf16[2,256,1280]{2,1,0:T(8,128)(2,1)}, u32[]{:S(2)}, u32[]{:S(2)}) collective-permute-start(bf16[2,256,1280]{2,1,0:T(8,128)(2,1)} %get-tuple-element.40), channel_id=1, source_target_pairs={{0,32},{32,64},{64,96},{1,33},{33,65},{65,97},{2,34},{34,66},{66,9... | collective-permute-start | bytes 3932168 | tf_op jit(solution)/shard_map/ppermute | solution.py:105
  210.0 23.3 %shard_map.94 = (bf16[256,1280]{1,0:T(8,128)(2,1)}, bf16[256,1280]{1,0:T(8,128)(2,1)}, f32[256,1280]{1,0:T(8,128)}, f32[256,1280]{1,0:T(8,128)}, bf16[2,256,1280...) custom-call(s32[5]{0:T(128)} %convert_element_type.39.flags_ref, ...), custom_call_target="tpu_custom_call" | custom-call | flops 5033164800 | bytes 22282240 | tf_op jit(solution)/shard_map/pallas_call | solution.py:82
  236.0 9.9 %all-to-all-start.3 = ((bf16[128,2,2560]{2,1,0:T(2,128)(2,1)}), bf16[128,2,2560]{2,1,0:T(2,128)(2,1)S(1)}, u32[]{:S(2)}, u32[]{:S(2)}) async-start(bf16[128,2,2560]{2,1,0:T(2,128)(2,1)} %all_to_all.55), calls=%async_computation.3 | async-start | bytes 2621440 | tf_op jit(solution)/shard_map/all_to_all | solution.py:148
  249.5 21.5 %all-to-all-done.3 = bf16[128,2,2560]{2,1,0:T(2,128)(2,1)S(1)} async-done(((bf16[128,2,2560]{2,1,0:T(2,128)(2,1)}), bf16[128,2,2560]{2,1,0:T(2,128)(2,1)S(1)}, u32[]{:S(2)}, u32[]{:S(2)}) %all-to-all-start.3) | async-done | bytes 1310752 | tf_op jit(solution)/shard_map/all_to_all | solution.py:148
  275.1 3.8 collective-permute-start.13
  280.1 5.1 %collective-permute-start.15 = (bf16[2,256,1280]{2,1,0:T(8,128)(2,1)}, bf16[2,256,1280]{2,1,0:T(8,128)(2,1)}, u32[]{:S(2)}, u32[]{:S(2)}) collective-permute-start(bf16[2,256,1280]{2,1,0:T(8,128)(2,1)} %get-tuple-element.52), channel_id=1, source_target_pairs={{0,1},{1,2},{2,3},{3,4},{4,5},{5,6},{6,7},{7,8},{8,9},{9,10},{10,1... | collective-permute-start | bytes 3932168 | tf_op jit(solution)/shard_map/ppermute | solution.py:105
  290.2 7.0 %all-to-all-start.4 = ((bf16[128,2,2560]{2,1,0:T(2,128)(2,1)}), bf16[128,2,2560]{2,1,0:T(2,128)(2,1)S(1)}, u32[]{:S(2)}, u32[]{:S(2)}) async-start(bf16[128,2,2560]{2,1,0:T(2,128)(2,1)} %all_to_all.58), calls=%async_computation.4 | async-start | bytes 2621440 | tf_op jit(solution)/shard_map/all_to_all | solution.py:171
  297.2 39.3 %collective-permute-done.12 = bf16[2,256,1280]{2,1,0:T(8,128)(2,1)} collective-permute-done((bf16[2,256,1280]{2,1,0:T(8,128)(2,1)}, bf16[2,256,1280]{2,1,0:T(8,128)(2,1)}, u32[]{:S(2)}, u32[]{:S(2)}) %collective-permute-start.12) | collective-permute-done | bytes 1310752 | tf_op jit(solution)/shard_map/ppermute | solution.py:105
  342.8 4.0 %all_to_all.61 = bf16[128,2,2560]{2,1,0:T(2,128)(2,1)} reshape(bf16[256,2560]{1,0:T(8,128)(2,1)} %pad_maximum_fusion.9) | data formatting | bytes 2621440 | tf_op jit(solution)/shard_map/all_to_all | solution.py:171
  346.8 10.7 %all-to-all-start.5 = ((bf16[128,2,2560]{2,1,0:T(2,128)(2,1)}), bf16[128,2,2560]{2,1,0:T(2,128)(2,1)}, u32[]{:S(2)}, u32[]{:S(2)}) async-start(bf16[128,2,2560]{2,1,0:T(2,128)(2,1)} %all_to_all.61), calls=%async_computation.5 | async-start | bytes 2621440 | tf_op jit(solution)/shard_map/all_to_all | solution.py:171
  365.6 13.1 %all-to-all-done.5 = bf16[128,2,2560]{2,1,0:T(2,128)(2,1)} async-done(((bf16[128,2,2560]{2,1,0:T(2,128)(2,1)}), bf16[128,2,2560]{2,1,0:T(2,128)(2,1)}, u32[]{:S(2)}, u32[]{:S(2)}) %all-to-all-start.5) | async-done | bytes 1310752 | tf_op jit(solution)/shard_map/all_to_all | solution.py:171
  (100 shorter events, 87.5 us)
Async XLA Ops:
  18.7 47.3 %all-to-all-start = ((bf16[128,2,5120]{2,1,0:T(2,128)(2,1)}), bf16[128,2,5120]{2,1,0:T(2,128)(2,1)}, u32[]{:S(2)}, u32[]{:S(2)}) async-start(bf16[128,2,5120]{2,1,0:T(2,128)(2,1)} %all_to_all.46), calls=%async_computation | async-start | bytes 5242880 | tf_op jit(solution)/shard_map/all_to_all | solution.py:133
  65.9 40.6 %all-to-all-start.2 = ((bf16[128,2,5120]{2,1,0:T(2,128)(2,1)}), bf16[128,2,5120]{2,1,0:T(2,128)(2,1)S(1)}, u32[]{:S(2)}, u32[]{:S(2)}) async-start(bf16[128,2,5120]{2,1,0:T(2,128)(2,1)} %all_to_all.52), calls=%async_computation.2 | async-start | bytes 5242880 | tf_op jit(solution)/shard_map/all_to_all | solution.py:133
  79.6 61.3 %collective-permute-start = (bf16[2,256,1280]{2,1,0:T(8,128)(2,1)}, bf16[2,256,1280]{2,1,0:T(8,128)(2,1)}, u32[]{:S(2)}, u32[]{:S(2)}) collective-permute-start(bf16[2,256,1280]{2,1,0:T(8,128)(2,1)} %pad_maximum_fusion.2), channel_id=1, source_target_pairs={{0,32},{32,64},{64,96},{1,33},{33,65},{65,97},{2,34},{34,66},{66,9... | collective-permute-start | bytes 3932168 | tf_op jit(solution)/shard_map/ppermute | solution.py:105
  84.8 59.6 %collective-permute-start.1 = (bf16[2,256,1280]{2,1,0:T(8,128)(2,1)}, bf16[2,256,1280]{2,1,0:T(8,128)(2,1)}, u32[]{:S(2)}, u32[]{:S(2)}) collective-permute-start(bf16[2,256,1280]{2,1,0:T(8,128)(2,1)} %pad_maximum_fusion.2), channel_id=1, source_target_pairs={{32,0},{64,32},{96,64},{33,1},{65,33},{97,65},{34,2},{66,34},{98,6... | collective-permute-start | bytes 3932168 | tf_op jit(solution)/shard_map/ppermute | solution.py:105
  86.7 57.7 %collective-permute-start.2 = (bf16[2,256,1280]{2,1,0:T(8,128)(2,1)}, bf16[2,256,1280]{2,1,0:T(8,128)(2,1)}, u32[]{:S(2)}, u32[]{:S(2)}) collective-permute-start(bf16[2,256,1280]{2,1,0:T(8,128)(2,1)} %pad_maximum_fusion.2), channel_id=1, source_target_pairs={{0,1},{1,2},{2,3},{3,4},{4,5},{5,6},{6,7},{7,8},{8,9},{9,10},{10,1... | collective-permute-start | bytes 3932168 | tf_op jit(solution)/shard_map/ppermute | solution.py:105
  91.2 53.2 %collective-permute-start.3 = (bf16[2,256,1280]{2,1,0:T(8,128)(2,1)}, bf16[2,256,1280]{2,1,0:T(8,128)(2,1)}, u32[]{:S(2)}, u32[]{:S(2)}) collective-permute-start(bf16[2,256,1280]{2,1,0:T(8,128)(2,1)} %pad_maximum_fusion.2), channel_id=1, source_target_pairs={{1,0},{2,1},{3,2},{4,3},{5,4},{6,5},{7,6},{8,7},{9,8},{10,9},{11,1... | collective-permute-start | bytes 3932168 | tf_op jit(solution)/shard_map/ppermute | solution.py:105
  144.4 51.7 %collective-permute-start.4 = (bf16[2,256,1280]{2,1,0:T(8,128)(2,1)S(1)}, bf16[2,256,1280]{2,1,0:T(8,128)(2,1)}, u32[]{:S(2)}, u32[]{:S(2)}) collective-permute-start(bf16[2,256,1280]{2,1,0:T(8,128)(2,1)S(1)} %pad_maximum_fusion.4), channel_id=1, source_target_pairs={{0,32},{32,64},{64,96},{1,33},{33,65},{65,97},{2,34},{34,66},{66,9... | collective-permute-start | bytes 3932168 | tf_op jit(solution)/shard_map/ppermute | solution.py:105
  146.8 49.3 %collective-permute-start.5 = (bf16[2,256,1280]{2,1,0:T(8,128)(2,1)S(1)}, bf16[2,256,1280]{2,1,0:T(8,128)(2,1)}, u32[]{:S(2)}, u32[]{:S(2)}) collective-permute-start(bf16[2,256,1280]{2,1,0:T(8,128)(2,1)S(1)} %pad_maximum_fusion.4), channel_id=1, source_target_pairs={{32,0},{64,32},{96,64},{33,1},{65,33},{97,65},{34,2},{66,34},{98,6... | collective-permute-start | bytes 3932168 | tf_op jit(solution)/shard_map/ppermute | solution.py:105
  149.8 46.3 %collective-permute-start.6 = (bf16[2,256,1280]{2,1,0:T(8,128)(2,1)S(1)}, bf16[2,256,1280]{2,1,0:T(8,128)(2,1)}, u32[]{:S(2)}, u32[]{:S(2)}) collective-permute-start(bf16[2,256,1280]{2,1,0:T(8,128)(2,1)S(1)} %pad_maximum_fusion.4), channel_id=1, source_target_pairs={{0,1},{1,2},{2,3},{3,4},{4,5},{5,6},{6,7},{7,8},{8,9},{9,10},{10,1... | collective-permute-start | bytes 3932168 | tf_op jit(solution)/shard_map/ppermute | solution.py:105
  152.2 43.9 %collective-permute-start.7 = (bf16[2,256,1280]{2,1,0:T(8,128)(2,1)S(1)}, bf16[2,256,1280]{2,1,0:T(8,128)(2,1)}, u32[]{:S(2)}, u32[]{:S(2)}) collective-permute-start(bf16[2,256,1280]{2,1,0:T(8,128)(2,1)S(1)} %pad_maximum_fusion.4), channel_id=1, source_target_pairs={{1,0},{2,1},{3,2},{4,3},{5,4},{6,5},{7,6},{8,7},{9,8},{10,9},{11,1... | collective-permute-start | bytes 3932168 | tf_op jit(solution)/shard_map/ppermute | solution.py:105
  182.8 53.2 %all-to-all-start.1 = ((bf16[128,2,2560]{2,1,0:T(2,128)(2,1)}), bf16[128,2,2560]{2,1,0:T(2,128)(2,1)S(1)}, u32[]{:S(2)}, u32[]{:S(2)}) async-start(bf16[128,2,2560]{2,1,0:T(2,128)(2,1)} %all_to_all.49), calls=%async_computation.1 | async-start | bytes 2621440 | tf_op jit(solution)/shard_map/all_to_all | solution.py:148
  196.1 75.4 %collective-permute-start.10 = (bf16[2,256,1280]{2,1,0:T(8,128)(2,1)}, bf16[2,256,1280]{2,1,0:T(8,128)(2,1)}, u32[]{:S(2)}, u32[]{:S(2)}) collective-permute-start(bf16[2,256,1280]{2,1,0:T(8,128)(2,1)} %get-tuple-element.41), channel_id=1, source_target_pairs={{1,0},{2,1},{3,2},{4,3},{5,4},{6,5},{7,6},{8,7},{9,8},{10,9},{11,1... | collective-permute-start | bytes 3932168 | tf_op jit(solution)/shard_map/ppermute | solution.py:105
  197.4 74.2 %collective-permute-start.11 = (bf16[2,256,1280]{2,1,0:T(8,128)(2,1)}, bf16[2,256,1280]{2,1,0:T(8,128)(2,1)}, u32[]{:S(2)}, u32[]{:S(2)}) collective-permute-start(bf16[2,256,1280]{2,1,0:T(8,128)(2,1)} %get-tuple-element.42), channel_id=1, source_target_pairs={{0,1},{1,2},{2,3},{3,4},{4,5},{5,6},{6,7},{7,8},{8,9},{9,10},{10,1... | collective-permute-start | bytes 3932168 | tf_op jit(solution)/shard_map/ppermute | solution.py:105
  202.5 69.1 %collective-permute-start.8 = (bf16[2,256,1280]{2,1,0:T(8,128)(2,1)}, bf16[2,256,1280]{2,1,0:T(8,128)(2,1)}, u32[]{:S(2)}, u32[]{:S(2)}) collective-permute-start(bf16[2,256,1280]{2,1,0:T(8,128)(2,1)} %get-tuple-element.39), channel_id=1, source_target_pairs={{32,0},{64,32},{96,64},{33,1},{65,33},{97,65},{34,2},{66,34},{98,6... | collective-permute-start | bytes 3932168 | tf_op jit(solution)/shard_map/ppermute | solution.py:105
  206.0 65.6 %collective-permute-start.9 = (bf16[2,256,1280]{2,1,0:T(8,128)(2,1)}, bf16[2,256,1280]{2,1,0:T(8,128)(2,1)}, u32[]{:S(2)}, u32[]{:S(2)}) collective-permute-start(bf16[2,256,1280]{2,1,0:T(8,128)(2,1)} %get-tuple-element.40), channel_id=1, source_target_pairs={{0,32},{32,64},{64,96},{1,33},{33,65},{65,97},{2,34},{34,66},{66,9... | collective-permute-start | bytes 3932168 | tf_op jit(solution)/shard_map/ppermute | solution.py:105
  236.0 35.0 %all-to-all-start.3 = ((bf16[128,2,2560]{2,1,0:T(2,128)(2,1)}), bf16[128,2,2560]{2,1,0:T(2,128)(2,1)S(1)}, u32[]{:S(2)}, u32[]{:S(2)}) async-start(bf16[128,2,2560]{2,1,0:T(2,128)(2,1)} %all_to_all.55), calls=%async_computation.3 | async-start | bytes 2621440 | tf_op jit(solution)/shard_map/all_to_all | solution.py:148
  271.6 64.9 %collective-permute-start.12 = (bf16[2,256,1280]{2,1,0:T(8,128)(2,1)}, bf16[2,256,1280]{2,1,0:T(8,128)(2,1)}, u32[]{:S(2)}, u32[]{:S(2)}) collective-permute-start(bf16[2,256,1280]{2,1,0:T(8,128)(2,1)} %get-tuple-element.49), channel_id=1, source_target_pairs={{32,0},{64,32},{96,64},{33,1},{65,33},{97,65},{34,2},{66,34},{98,6... | collective-permute-start | bytes 3932168 | tf_op jit(solution)/shard_map/ppermute | solution.py:105
  275.1 63.1 %collective-permute-start.13 = (bf16[2,256,1280]{2,1,0:T(8,128)(2,1)}, bf16[2,256,1280]{2,1,0:T(8,128)(2,1)}, u32[]{:S(2)}, u32[]{:S(2)}) collective-permute-start(bf16[2,256,1280]{2,1,0:T(8,128)(2,1)} %get-tuple-element.50), channel_id=1, source_target_pairs={{0,32},{32,64},{64,96},{1,33},{33,65},{65,97},{2,34},{34,66},{66,9... | collective-permute-start | bytes 3932168 | tf_op jit(solution)/shard_map/ppermute | solution.py:105
  278.8 59.3 %collective-permute-start.14 = (bf16[2,256,1280]{2,1,0:T(8,128)(2,1)}, bf16[2,256,1280]{2,1,0:T(8,128)(2,1)}, u32[]{:S(2)}, u32[]{:S(2)}) collective-permute-start(bf16[2,256,1280]{2,1,0:T(8,128)(2,1)} %get-tuple-element.51), channel_id=1, source_target_pairs={{1,0},{2,1},{3,2},{4,3},{5,4},{6,5},{7,6},{8,7},{9,8},{10,9},{11,1... | collective-permute-start | bytes 3932168 | tf_op jit(solution)/shard_map/ppermute | solution.py:105
  280.1 58.0 %collective-permute-start.15 = (bf16[2,256,1280]{2,1,0:T(8,128)(2,1)}, bf16[2,256,1280]{2,1,0:T(8,128)(2,1)}, u32[]{:S(2)}, u32[]{:S(2)}) collective-permute-start(bf16[2,256,1280]{2,1,0:T(8,128)(2,1)} %get-tuple-element.52), channel_id=1, source_target_pairs={{0,1},{1,2},{2,3},{3,4},{4,5},{5,6},{6,7},{7,8},{8,9},{9,10},{10,1... | collective-permute-start | bytes 3932168 | tf_op jit(solution)/shard_map/ppermute | solution.py:105
  290.2 56.5 %all-to-all-start.4 = ((bf16[128,2,2560]{2,1,0:T(2,128)(2,1)}), bf16[128,2,2560]{2,1,0:T(2,128)(2,1)S(1)}, u32[]{:S(2)}, u32[]{:S(2)}) async-start(bf16[128,2,2560]{2,1,0:T(2,128)(2,1)} %all_to_all.58), calls=%async_computation.4 | async-start | bytes 2621440 | tf_op jit(solution)/shard_map/all_to_all | solution.py:171
  297.2 44.1 %copy-start.9 = (f32[256,1280]{1,0:T(8,128)S(1)}, f32[256,1280]{1,0:T(8,128)}, u32[]{:S(2)}) copy-start(f32[256,1280]{1,0:T(8,128)} %get-tuple-element.44) | copy-start | bytes 3932164
  297.2 44.1 %copy-start.10 = (f32[256,1280]{1,0:T(8,128)S(1)}, f32[256,1280]{1,0:T(8,128)}, u32[]{:S(2)}) copy-start(f32[256,1280]{1,0:T(8,128)} %get-tuple-element.53) | copy-start | bytes 3932164
  346.8 32.0 %all-to-all-start.5 = ((bf16[128,2,2560]{2,1,0:T(2,128)(2,1)}), bf16[128,2,2560]{2,1,0:T(2,128)(2,1)}, u32[]{:S(2)}, u32[]{:S(2)}) async-start(bf16[128,2,2560]{2,1,0:T(2,128)(2,1)} %all_to_all.61), calls=%async_computation.5 | async-start | bytes 2621440 | tf_op jit(solution)/shard_map/all_to_all | solution.py:171
  (10 other events, 63.8 us)

commit v2 on v1

--- a/solution.py
+++ b/solution.py
@@ -65,9 +65,9 @@
     dq_ref[...] = dq.astype(jnp.bfloat16)
 
 
-def attend_tile(flags, recv, kv_below, kv_above, kv_left, kv_right):
-    tokens = recv.shape[0]
-    heads = recv.shape[1] // (4 * HD)
+def attend_tile(flags, qg, kv, kv_below, kv_above, kv_left, kv_right):
+    tokens = qg.shape[0]
+    heads = qg.shape[1] // (2 * HD)
     own = lambda part: pl.BlockSpec((tokens, HD), lambda h, f, part=part: (0, part * heads + h))
     pair = pl.BlockSpec((2, tokens, HD), lambda h, f: (0, 0, h))
     head = pl.BlockSpec((tokens, HD), lambda h, f: (0, h))
@@ -85,7 +85,7 @@
         grid_spec=pltpu.PrefetchScalarGridSpec(
             num_scalar_prefetch=1,
             grid=(heads,),
-            in_specs=[own(0), own(3), own(1), own(2), pair, pair, pair, pair],
+            in_specs=[own(0), own(1), own(0), own(1), pair, pair, pair, pair],
             out_specs=[head, head, head, head, pair, pair, pair, pair],
             scratch_shapes=[
                 pltpu.VMEM((SETS, tokens, TILE), jnp.float32),
@@ -96,7 +96,7 @@
         cost_estimate=pl.CostEstimate(
             flops=flops, transcendentals=SETS * tokens * TILE * heads, bytes_accessed=bytes_accessed
         ),
-    )(flags, recv, recv, recv, recv, kv_below, kv_above, kv_left, kv_right)
+    )(flags, qg, qg, kv, kv, kv_below, kv_above, kv_left, kv_right)
 
 
 def shifted(block, axis, distance):
@@ -129,9 +129,9 @@
     gate = None
     for chunk in range(CHUNKS):
         cols = slice(chunk * width, (chunk + 1) * width)
-        send = jnp.concatenate([rows[:, cols] for rows in gathered], axis=1)
-        recv = lax.all_to_all(send, ("tm", "space"), split_axis=0, concat_axis=0, tiled=True)
-        kv_own = jnp.stack([recv[:, width:2 * width], recv[:, 2 * width:3 * width]])
+        send_kv = jnp.concatenate([gathered[1][:, cols], gathered[2][:, cols]], axis=1)
+        kv = lax.all_to_all(send_kv, ("tm", "space"), split_axis=0, concat_axis=0, tiled=True)
+        kv_own = jnp.stack([kv[:, :width], kv[:, width:]])
         if gate is not None:
             kv_own = lax.optimization_barrier((kv_own,) + gate)[0]
         halo = (
@@ -140,8 +140,10 @@
             shifted(kv_own, "space", 1),
             shifted(kv_own, "space", -1),
         )
+        send_qg = jnp.concatenate([gathered[0][:, cols], gathered[3][:, cols]], axis=1)
+        qg = lax.all_to_all(send_qg, ("tm", "space"), split_axis=0, concat_axis=0, tiled=True)
         attended, query_grad, key_own, value_own, nb_b, nb_a, nb_l, nb_r = attend_tile(
-            flags, recv, *halo
+            flags, qg, kv, *halo
         )
         gate = halo
         early = jnp.concatenate([attended, query_grad], axis=1)

time: 391 us -> 403 us (1.031)
  starting transfers between devices: 107 us -> 128 us
  waiting for transfers between devices: 155 us -> 144 us
    all_to_all x2 -> x4, starting transfers between devices: 16.5 us -> 39.6 us  [the longest x2 22.4 us: shards(): lax.all_to_all(send_qg, ('tm', 'space'), split_axis=0, concat_axis=0, til...]
    all_to_all x2 -> x4, waiting for transfers between devices: 45.3 us -> 33.8 us  [the longest x2 31 us: shards(): lax.all_to_all(send_kv, ('tm', 'space'), split_axis=0, concat_axis=0, til...]
    all_to_all x4 -> x8, local copies, waits for them, and re-layouts: 13.9 us -> 14.6 us  [the longest x4 8.15 us: shards(): lax.all_to_all(send_qg, ('tm', 'space'), split_axis=0, concat_axis=0, til...]
  transfers between devices with their start and end apart: 22 -> 24, of which waited for: 8 -> 9; matrix products, arithmetic and copies ran while one was open for 7% -> 8% of each run, Pallas kernels for 12% -> 11%
where the time goes in v2:
time: 403 us; the launch traced here: 402 us
  waiting for transfers between devices  144 us (36%)
  starting transfers between devices  128 us (32%)
  local copies, waits for them, and re-layouts  61.6 us (15%)
  Pallas kernels  46.2 us (11%)
  other arithmetic  18.6 us (5%)
    ppermute x16, waiting for transfers between devices, shifted(): return lax.ppermute(block, axis, route)  74.9 us
    ppermute x16, starting transfers between devices, shifted(): return lax.ppermute(block, axis, route)  49.5 us
    pallas_call x2, Pallas kernels, attend_tile(): pl.pallas_call(_attn_kernel, out_shape=out_shape, grid_spec=pltpu.Prefetc...  46.2 us
    all_to_all x2, waiting for transfers between devices, shards(): lax.all_to_all(send_kv, ('tm', 'space'), split_axis=0, concat_axis=0, til...  31 us
    all_to_all x2, starting transfers between devices, shards(): lax.all_to_all(send_qg, ('tm', 'space'), split_axis=0, concat_axis=0, til...  22.4 us
    all_to_all x2, waiting for transfers between devices, shards(): lax.all_to_all(early, ('tm', 'space'), split_axis=0, concat_axis=0, tiled...  22.2 us
    all_to_all x2, starting transfers between devices, shards(): lax.all_to_all(early, ('tm', 'space'), split_axis=0, concat_axis=0, tiled...  21.9 us
    all_to_all x2, starting transfers between devices, shards(): lax.all_to_all(late, ('tm', 'space'), split_axis=0, concat_axis=0, tiled=...  17.3 us
  transfers between devices with their start and end apart: 24, of which 9 were waited for; matrix products, arithmetic and copies ran while one was open for 8% of the time, Pallas kernels for 11%

profile of v2, /device:TPU:1, one launch (start us, length us, event | category | flops | bytes accessed | tf_op | source)
XLA Modules:
  0.0 401.7 jit_solution(11653313703614152882)
XLA Ops:
  11.7 11.5 %all-to-all-start.1 = ((bf16[128,2,2560]{2,1,0:T(2,128)(2,1)}), bf16[128,2,2560]{2,1,0:T(2,128)(2,1)S(1)}, u32[]{:S(2)}, u32[]{:S(2)}) async-start(bf16[128,2,2560]{2,1,0:T(2,128)(2,1)} %all_to_all.63), calls=%async_computation.1 | async-start | bytes 2621440 | tf_op jit(solution)/shard_map/all_to_all | solution.py:133
  25.7 19.1 %all-to-all-done.1 = bf16[128,2,2560]{2,1,0:T(2,128)(2,1)S(1)} async-done(((bf16[128,2,2560]{2,1,0:T(2,128)(2,1)}), bf16[128,2,2560]{2,1,0:T(2,128)(2,1)S(1)}, u32[]{:S(2)}, u32[]{:S(2)}) %all-to-all-start.1) | async-done | bytes 1310752 | tf_op jit(solution)/shard_map/all_to_all | solution.py:133
  45.9 5.7 %all-to-all-start.4 = ((bf16[128,2,2560]{2,1,0:T(2,128)(2,1)}), bf16[128,2,2560]{2,1,0:T(2,128)(2,1)}, u32[]{:S(2)}, u32[]{:S(2)}) async-start(bf16[128,2,2560]{2,1,0:T(2,128)(2,1)} %all_to_all.72), calls=%async_computation.4 | async-start | bytes 2621440 | tf_op jit(solution)/shard_map/all_to_all | solution.py:133
  61.1 11.9 %all-to-all-done.4 = bf16[128,2,2560]{2,1,0:T(2,128)(2,1)} async-done(((bf16[128,2,2560]{2,1,0:T(2,128)(2,1)}), bf16[128,2,2560]{2,1,0:T(2,128)(2,1)}, u32[]{:S(2)}, u32[]{:S(2)}) %all-to-all-start.4) | async-done | bytes 1310752 | tf_op jit(solution)/shard_map/all_to_all | solution.py:133
  73.1 5.7 %all-to-all-start = ((bf16[128,2,2560]{2,1,0:T(2,128)(2,1)}), bf16[128,2,2560]{2,1,0:T(2,128)(2,1)}, u32[]{:S(2)}, u32[]{:S(2)}) async-start(bf16[128,2,2560]{2,1,0:T(2,128)(2,1)} %all_to_all.60), calls=%async_computation | async-start | bytes 2621440 | tf_op jit(solution)/shard_map/all_to_all | solution.py:144
  80.1 5.2 %collective-permute-start = (bf16[2,256,1280]{2,1,0:T(8,128)(2,1)}, bf16[2,256,1280]{2,1,0:T(8,128)(2,1)}, u32[]{:S(2)}, u32[]{:S(2)}) collective-permute-start(bf16[2,256,1280]{2,1,0:T(8,128)(2,1)} %pad_maximum_fusion.2), channel_id=1, source_target_pairs={{0,32},{32,64},{64,96},{1,33},{33,65},{65,97},{2,34},{34,66},{66,9... | collective-permute-start | bytes 3932168 | tf_op jit(solution)/shard_map/ppermute | solution.py:105
  87.2 4.4 %collective-permute-start.2 = (bf16[2,256,1280]{2,1,0:T(8,128)(2,1)}, bf16[2,256,1280]{2,1,0:T(8,128)(2,1)}, u32[]{:S(2)}, u32[]{:S(2)}) collective-permute-start(bf16[2,256,1280]{2,1,0:T(8,128)(2,1)} %pad_maximum_fusion.2), channel_id=1, source_target_pairs={{0,1},{1,2},{2,3},{3,4},{4,5},{5,6},{6,7},{7,8},{8,9},{9,10},{10,1... | collective-permute-start | bytes 3932168 | tf_op jit(solution)/shard_map/ppermute | solution.py:105
  100.4 16.6 %all-to-all-start.3 = ((bf16[128,2,2560]{2,1,0:T(2,128)(2,1)}), bf16[128,2,2560]{2,1,0:T(2,128)(2,1)S(1)}, u32[]{:S(2)}, u32[]{:S(2)}) async-start(bf16[128,2,2560]{2,1,0:T(2,128)(2,1)} %all_to_all.69), calls=%async_computation.3 | async-start | bytes 2621440 | tf_op jit(solution)/shard_map/all_to_all | solution.py:144
  118.3 30.0 %collective-permute-done.kb_ref = bf16[2,256,1280]{2,1,0:T(8,128)(2,1)} collective-permute-done((bf16[2,256,1280]{2,1,0:T(8,128)(2,1)}, bf16[2,256,1280]{2,1,0:T(8,128)(2,1)}, u32[]{:S(2)}, u32[]{:S(2)}) %collective-permute-start) | collective-permute-done | bytes 1310752 | tf_op jit(solution)/shard_map/ppermute | solution.py:105
  148.3 3.8 collective-permute-done.1.ka_ref
  164.4 4.1 %all_to_all.62.q_ref.g_ref = bf16[256,2560]{1,0:T(8,128)(2,1)} reshape(bf16[128,2,2560]{2,1,0:T(2,128)(2,1)} %all-to-all-done) | data formatting | bytes 2621440 | tf_op jit(solution)/shard_map/all_to_all | solution.py:144
  168.4 23.1 %shard_map.93 = (bf16[256,1280]{1,0:T(8,128)(2,1)}, bf16[256,1280]{1,0:T(8,128)(2,1)}, f32[256,1280]{1,0:T(8,128)}, f32[256,1280]{1,0:T(8,128)}, bf16[2,256,1280...) custom-call(s32[5]{0:T(128)} %convert_element_type.39.flags_ref, ...), custom_call_target="tpu_custom_call" | custom-call | flops 5033164800 | bytes 22282240 | tf_op jit(solution)/shard_map/pallas_call | solution.py:82
  194.3 11.7 %all-to-all-start.2 = ((bf16[128,2,2560]{2,1,0:T(2,128)(2,1)}), bf16[128,2,2560]{2,1,0:T(2,128)(2,1)S(1)}, u32[]{:S(2)}, u32[]{:S(2)}) async-start(bf16[128,2,2560]{2,1,0:T(2,128)(2,1)} %all_to_all.66), calls=%async_computation.2 | async-start | bytes 2621440 | tf_op jit(solution)/shard_map/all_to_all | solution.py:150
  208.7 5.1 %collective-permute-start.11 = (bf16[2,256,1280]{2,1,0:T(8,128)(2,1)}, bf16[2,256,1280]{2,1,0:T(8,128)(2,1)}, u32[]{:S(2)}, u32[]{:S(2)}) collective-permute-start(bf16[2,256,1280]{2,1,0:T(8,128)(2,1)} %get-tuple-element.42), channel_id=1, source_target_pairs={{0,1},{1,2},{2,3},{3,4},{4,5},{5,6},{6,7},{7,8},{8,9},{9,10},{10,1... | collective-permute-start | bytes 3932168 | tf_op jit(solution)/shard_map/ppermute | solution.py:105
  217.4 4.0 collective-permute-start.9
  221.4 23.1 %shard_map.94 = (bf16[256,1280]{1,0:T(8,128)(2,1)}, bf16[256,1280]{1,0:T(8,128)(2,1)}, f32[256,1280]{1,0:T(8,128)}, f32[256,1280]{1,0:T(8,128)}, bf16[2,256,1280...) custom-call(s32[5]{0:T(128)} %convert_element_type.39.flags_ref, ...), custom_call_target="tpu_custom_call" | custom-call | flops 5033164800 | bytes 22282240 | tf_op jit(solution)/shard_map/pallas_call | solution.py:82
  247.2 10.2 %all-to-all-start.5 = ((bf16[128,2,2560]{2,1,0:T(2,128)(2,1)}), bf16[128,2,2560]{2,1,0:T(2,128)(2,1)}, u32[]{:S(2)}, u32[]{:S(2)}) async-start(bf16[128,2,2560]{2,1,0:T(2,128)(2,1)} %all_to_all.75), calls=%async_computation.5 | async-start | bytes 2621440 | tf_op jit(solution)/shard_map/all_to_all | solution.py:150
  259.0 22.2 %all-to-all-done.5 = bf16[128,2,2560]{2,1,0:T(2,128)(2,1)} async-done(((bf16[128,2,2560]{2,1,0:T(2,128)(2,1)}), bf16[128,2,2560]{2,1,0:T(2,128)(2,1)}, u32[]{:S(2)}, u32[]{:S(2)}) %all-to-all-start.5) | async-done | bytes 1310752 | tf_op jit(solution)/shard_map/all_to_all | solution.py:150
  293.0 5.1 %collective-permute-start.15 = (bf16[2,256,1280]{2,1,0:T(8,128)(2,1)}, bf16[2,256,1280]{2,1,0:T(8,128)(2,1)}, u32[]{:S(2)}, u32[]{:S(2)}) collective-permute-start(bf16[2,256,1280]{2,1,0:T(8,128)(2,1)} %get-tuple-element.52), channel_id=1, source_target_pairs={{0,1},{1,2},{2,3},{3,4},{4,5},{5,6},{6,7},{7,8},{8,9},{9,10},{10,1... | collective-permute-start | bytes 3932168 | tf_op jit(solution)/shard_map/ppermute | solution.py:105
  303.0 7.0 %all-to-all-start.6 = ((bf16[128,2,2560]{2,1,0:T(2,128)(2,1)}), bf16[128,2,2560]{2,1,0:T(2,128)(2,1)S(1)}, u32[]{:S(2)}, u32[]{:S(2)}) async-start(bf16[128,2,2560]{2,1,0:T(2,128)(2,1)} %all_to_all.78), calls=%async_computation.6 | async-start | bytes 2621440 | tf_op jit(solution)/shard_map/all_to_all | solution.py:173
  310.0 39.4 %collective-permute-done.12 = bf16[2,256,1280]{2,1,0:T(8,128)(2,1)} collective-permute-done((bf16[2,256,1280]{2,1,0:T(8,128)(2,1)}, bf16[2,256,1280]{2,1,0:T(8,128)(2,1)}, u32[]{:S(2)}, u32[]{:S(2)}) %collective-permute-start.12) | collective-permute-done | bytes 1310752 | tf_op jit(solution)/shard_map/ppermute | solution.py:105
  355.6 4.0 all_to_all.81
  359.6 10.4 %all-to-all-start.7 = ((bf16[128,2,2560]{2,1,0:T(2,128)(2,1)}), bf16[128,2,2560]{2,1,0:T(2,128)(2,1)}, u32[]{:S(2)}, u32[]{:S(2)}) async-start(bf16[128,2,2560]{2,1,0:T(2,128)(2,1)} %all_to_all.81), calls=%async_computation.7 | async-start | bytes 2621440 | tf_op jit(solution)/shard_map/all_to_all | solution.py:173
  378.1 13.1 %all-to-all-done.7 = bf16[128,2,2560]{2,1,0:T(2,128)(2,1)} async-done(((bf16[128,2,2560]{2,1,0:T(2,128)(2,1)}), bf16[128,2,2560]{2,1,0:T(2,128)(2,1)}, u32[]{:S(2)}, u32[]{:S(2)}) %all-to-all-start.7) | async-done | bytes 1310752 | tf_op jit(solution)/shard_map/all_to_all | solution.py:173
  (122 shorter events, 102.2 us)
Async XLA Ops:
  11.7 33.1 %all-to-all-start.1 = ((bf16[128,2,2560]{2,1,0:T(2,128)(2,1)}), bf16[128,2,2560]{2,1,0:T(2,128)(2,1)S(1)}, u32[]{:S(2)}, u32[]{:S(2)}) async-start(bf16[128,2,2560]{2,1,0:T(2,128)(2,1)} %all_to_all.63), calls=%async_computation.1 | async-start | bytes 2621440 | tf_op jit(solution)/shard_map/all_to_all | solution.py:133
  45.9 27.2 %all-to-all-start.4 = ((bf16[128,2,2560]{2,1,0:T(2,128)(2,1)}), bf16[128,2,2560]{2,1,0:T(2,128)(2,1)}, u32[]{:S(2)}, u32[]{:S(2)}) async-start(bf16[128,2,2560]{2,1,0:T(2,128)(2,1)} %all_to_all.72), calls=%async_computation.4 | async-start | bytes 2621440 | tf_op jit(solution)/shard_map/all_to_all | solution.py:133
  73.1 27.4 %all-to-all-start = ((bf16[128,2,2560]{2,1,0:T(2,128)(2,1)}), bf16[128,2,2560]{2,1,0:T(2,128)(2,1)}, u32[]{:S(2)}, u32[]{:S(2)}) async-start(bf16[128,2,2560]{2,1,0:T(2,128)(2,1)} %all_to_all.60), calls=%async_computation | async-start | bytes 2621440 | tf_op jit(solution)/shard_map/all_to_all | solution.py:144
  80.1 68.2 %collective-permute-start = (bf16[2,256,1280]{2,1,0:T(8,128)(2,1)}, bf16[2,256,1280]{2,1,0:T(8,128)(2,1)}, u32[]{:S(2)}, u32[]{:S(2)}) collective-permute-start(bf16[2,256,1280]{2,1,0:T(8,128)(2,1)} %pad_maximum_fusion.2), channel_id=1, source_target_pairs={{0,32},{32,64},{64,96},{1,33},{33,65},{65,97},{2,34},{34,66},{66,9... | collective-permute-start | bytes 3932168 | tf_op jit(solution)/shard_map/ppermute | solution.py:105
  85.3 66.9 %collective-permute-start.1 = (bf16[2,256,1280]{2,1,0:T(8,128)(2,1)}, bf16[2,256,1280]{2,1,0:T(8,128)(2,1)}, u32[]{:S(2)}, u32[]{:S(2)}) collective-permute-start(bf16[2,256,1280]{2,1,0:T(8,128)(2,1)} %pad_maximum_fusion.2), channel_id=1, source_target_pairs={{32,0},{64,32},{96,64},{33,1},{65,33},{97,65},{34,2},{66,34},{98,6... | collective-permute-start | bytes 3932168 | tf_op jit(solution)/shard_map/ppermute | solution.py:105
  87.2 65.0 %collective-permute-start.2 = (bf16[2,256,1280]{2,1,0:T(8,128)(2,1)}, bf16[2,256,1280]{2,1,0:T(8,128)(2,1)}, u32[]{:S(2)}, u32[]{:S(2)}) collective-permute-start(bf16[2,256,1280]{2,1,0:T(8,128)(2,1)} %pad_maximum_fusion.2), channel_id=1, source_target_pairs={{0,1},{1,2},{2,3},{3,4},{4,5},{5,6},{6,7},{7,8},{8,9},{9,10},{10,1... | collective-permute-start | bytes 3932168 | tf_op jit(solution)/shard_map/ppermute | solution.py:105
  91.6 60.5 %collective-permute-start.3 = (bf16[2,256,1280]{2,1,0:T(8,128)(2,1)}, bf16[2,256,1280]{2,1,0:T(8,128)(2,1)}, u32[]{:S(2)}, u32[]{:S(2)}) collective-permute-start(bf16[2,256,1280]{2,1,0:T(8,128)(2,1)} %pad_maximum_fusion.2), channel_id=1, source_target_pairs={{1,0},{2,1},{3,2},{4,3},{5,4},{6,5},{7,6},{8,7},{9,8},{10,9},{11,1... | collective-permute-start | bytes 3932168 | tf_op jit(solution)/shard_map/ppermute | solution.py:105
  100.4 93.9 %all-to-all-start.3 = ((bf16[128,2,2560]{2,1,0:T(2,128)(2,1)}), bf16[128,2,2560]{2,1,0:T(2,128)(2,1)S(1)}, u32[]{:S(2)}, u32[]{:S(2)}) async-start(bf16[128,2,2560]{2,1,0:T(2,128)(2,1)} %all_to_all.69), calls=%async_computation.3 | async-start | bytes 2621440 | tf_op jit(solution)/shard_map/all_to_all | solution.py:144
  152.1 55.3 %collective-permute-start.4 = (bf16[2,256,1280]{2,1,0:T(8,128)(2,1)}, bf16[2,256,1280]{2,1,0:T(8,128)(2,1)}, u32[]{:S(2)}, u32[]{:S(2)}) collective-permute-start(bf16[2,256,1280]{2,1,0:T(8,128)(2,1)} %pad_maximum_fusion.6), channel_id=1, source_target_pairs={{0,32},{32,64},{64,96},{1,33},{33,65},{65,97},{2,34},{34,66},{66,9... | collective-permute-start | bytes 3932168 | tf_op jit(solution)/shard_map/ppermute | solution.py:105
  154.2 53.2 %collective-permute-start.5 = (bf16[2,256,1280]{2,1,0:T(8,128)(2,1)}, bf16[2,256,1280]{2,1,0:T(8,128)(2,1)}, u32[]{:S(2)}, u32[]{:S(2)}) collective-permute-start(bf16[2,256,1280]{2,1,0:T(8,128)(2,1)} %pad_maximum_fusion.6), channel_id=1, source_target_pairs={{32,0},{64,32},{96,64},{33,1},{65,33},{97,65},{34,2},{66,34},{98,6... | collective-permute-start | bytes 3932168 | tf_op jit(solution)/shard_map/ppermute | solution.py:105
  157.7 49.7 %collective-permute-start.6 = (bf16[2,256,1280]{2,1,0:T(8,128)(2,1)}, bf16[2,256,1280]{2,1,0:T(8,128)(2,1)}, u32[]{:S(2)}, u32[]{:S(2)}) collective-permute-start(bf16[2,256,1280]{2,1,0:T(8,128)(2,1)} %pad_maximum_fusion.6), channel_id=1, source_target_pairs={{0,1},{1,2},{2,3},{3,4},{4,5},{5,6},{6,7},{7,8},{8,9},{9,10},{10,1... | collective-permute-start | bytes 3932168 | tf_op jit(solution)/shard_map/ppermute | solution.py:105
  160.1 47.3 %collective-permute-start.7 = (bf16[2,256,1280]{2,1,0:T(8,128)(2,1)}, bf16[2,256,1280]{2,1,0:T(8,128)(2,1)}, u32[]{:S(2)}, u32[]{:S(2)}) collective-permute-start(bf16[2,256,1280]{2,1,0:T(8,128)(2,1)} %pad_maximum_fusion.6), channel_id=1, source_target_pairs={{1,0},{2,1},{3,2},{4,3},{5,4},{6,5},{7,6},{8,7},{9,8},{10,9},{11,1... | collective-permute-start | bytes 3932168 | tf_op jit(solution)/shard_map/ppermute | solution.py:105
  194.3 52.9 %all-to-all-start.2 = ((bf16[128,2,2560]{2,1,0:T(2,128)(2,1)}), bf16[128,2,2560]{2,1,0:T(2,128)(2,1)S(1)}, u32[]{:S(2)}, u32[]{:S(2)}) async-start(bf16[128,2,2560]{2,1,0:T(2,128)(2,1)} %all_to_all.66), calls=%async_computation.2 | async-start | bytes 2621440 | tf_op jit(solution)/shard_map/all_to_all | solution.py:150
  207.4 77.0 %collective-permute-start.10 = (bf16[2,256,1280]{2,1,0:T(8,128)(2,1)}, bf16[2,256,1280]{2,1,0:T(8,128)(2,1)}, u32[]{:S(2)}, u32[]{:S(2)}) collective-permute-start(bf16[2,256,1280]{2,1,0:T(8,128)(2,1)} %get-tuple-element.41), channel_id=1, source_target_pairs={{1,0},{2,1},{3,2},{4,3},{5,4},{6,5},{7,6},{8,7},{9,8},{10,9},{11,1... | collective-permute-start | bytes 3932168 | tf_op jit(solution)/shard_map/ppermute | solution.py:105
  208.7 75.7 %collective-permute-start.11 = (bf16[2,256,1280]{2,1,0:T(8,128)(2,1)}, bf16[2,256,1280]{2,1,0:T(8,128)(2,1)}, u32[]{:S(2)}, u32[]{:S(2)}) collective-permute-start(bf16[2,256,1280]{2,1,0:T(8,128)(2,1)} %get-tuple-element.42), channel_id=1, source_target_pairs={{0,1},{1,2},{2,3},{3,4},{4,5},{5,6},{6,7},{7,8},{8,9},{9,10},{10,1... | collective-permute-start | bytes 3932168 | tf_op jit(solution)/shard_map/ppermute | solution.py:105
  213.9 70.6 %collective-permute-start.8 = (bf16[2,256,1280]{2,1,0:T(8,128)(2,1)}, bf16[2,256,1280]{2,1,0:T(8,128)(2,1)}, u32[]{:S(2)}, u32[]{:S(2)}) collective-permute-start(bf16[2,256,1280]{2,1,0:T(8,128)(2,1)} %get-tuple-element.39), channel_id=1, source_target_pairs={{32,0},{64,32},{96,64},{33,1},{65,33},{97,65},{34,2},{66,34},{98,6... | collective-permute-start | bytes 3932168 | tf_op jit(solution)/shard_map/ppermute | solution.py:105
  217.4 67.1 %collective-permute-start.9 = (bf16[2,256,1280]{2,1,0:T(8,128)(2,1)}, bf16[2,256,1280]{2,1,0:T(8,128)(2,1)}, u32[]{:S(2)}, u32[]{:S(2)}) collective-permute-start(bf16[2,256,1280]{2,1,0:T(8,128)(2,1)} %get-tuple-element.40), channel_id=1, source_target_pairs={{0,32},{32,64},{64,96},{1,33},{33,65},{65,97},{2,34},{34,66},{66,9... | collective-permute-start | bytes 3932168 | tf_op jit(solution)/shard_map/ppermute | solution.py:105
  247.2 34.0 %all-to-all-start.5 = ((bf16[128,2,2560]{2,1,0:T(2,128)(2,1)}), bf16[128,2,2560]{2,1,0:T(2,128)(2,1)}, u32[]{:S(2)}, u32[]{:S(2)}) async-start(bf16[128,2,2560]{2,1,0:T(2,128)(2,1)} %all_to_all.75), calls=%async_computation.5 | async-start | bytes 2621440 | tf_op jit(solution)/shard_map/all_to_all | solution.py:150
  284.5 64.9 %collective-permute-start.12 = (bf16[2,256,1280]{2,1,0:T(8,128)(2,1)}, bf16[2,256,1280]{2,1,0:T(8,128)(2,1)}, u32[]{:S(2)}, u32[]{:S(2)}) collective-permute-start(bf16[2,256,1280]{2,1,0:T(8,128)(2,1)} %get-tuple-element.49), channel_id=1, source_target_pairs={{32,0},{64,32},{96,64},{33,1},{65,33},{97,65},{34,2},{66,34},{98,6... | collective-permute-start | bytes 3932168 | tf_op jit(solution)/shard_map/ppermute | solution.py:105
  287.9 63.1 %collective-permute-start.13 = (bf16[2,256,1280]{2,1,0:T(8,128)(2,1)}, bf16[2,256,1280]{2,1,0:T(8,128)(2,1)}, u32[]{:S(2)}, u32[]{:S(2)}) collective-permute-start(bf16[2,256,1280]{2,1,0:T(8,128)(2,1)} %get-tuple-element.50), channel_id=1, source_target_pairs={{0,32},{32,64},{64,96},{1,33},{33,65},{65,97},{2,34},{34,66},{66,9... | collective-permute-start | bytes 3932168 | tf_op jit(solution)/shard_map/ppermute | solution.py:105
  291.7 59.3 %collective-permute-start.14 = (bf16[2,256,1280]{2,1,0:T(8,128)(2,1)}, bf16[2,256,1280]{2,1,0:T(8,128)(2,1)}, u32[]{:S(2)}, u32[]{:S(2)}) collective-permute-start(bf16[2,256,1280]{2,1,0:T(8,128)(2,1)} %get-tuple-element.51), channel_id=1, source_target_pairs={{1,0},{2,1},{3,2},{4,3},{5,4},{6,5},{7,6},{8,7},{9,8},{10,9},{11,1... | collective-permute-start | bytes 3932168 | tf_op jit(solution)/shard_map/ppermute | solution.py:105
  293.0 58.0 %collective-permute-start.15 = (bf16[2,256,1280]{2,1,0:T(8,128)(2,1)}, bf16[2,256,1280]{2,1,0:T(8,128)(2,1)}, u32[]{:S(2)}, u32[]{:S(2)}) collective-permute-start(bf16[2,256,1280]{2,1,0:T(8,128)(2,1)} %get-tuple-element.52), channel_id=1, source_target_pairs={{0,1},{1,2},{2,3},{3,4},{4,5},{5,6},{6,7},{7,8},{8,9},{9,10},{10,1... | collective-permute-start | bytes 3932168 | tf_op jit(solution)/shard_map/ppermute | solution.py:105
  303.0 56.6 %all-to-all-start.6 = ((bf16[128,2,2560]{2,1,0:T(2,128)(2,1)}), bf16[128,2,2560]{2,1,0:T(2,128)(2,1)S(1)}, u32[]{:S(2)}, u32[]{:S(2)}) async-start(bf16[128,2,2560]{2,1,0:T(2,128)(2,1)} %all_to_all.78), calls=%async_computation.6 | async-start | bytes 2621440 | tf_op jit(solution)/shard_map/all_to_all | solution.py:173
  359.6 31.7 %all-to-all-start.7 = ((bf16[128,2,2560]{2,1,0:T(2,128)(2,1)}), bf16[128,2,2560]{2,1,0:T(2,128)(2,1)}, u32[]{:S(2)}, u32[]{:S(2)}) async-start(bf16[128,2,2560]{2,1,0:T(2,128)(2,1)} %all_to_all.81), calls=%async_computation.7 | async-start | bytes 2621440 | tf_op jit(solution)/shard_map/all_to_all | solution.py:173
  (18 other events, 218.9 us)

commit v3 on v1

--- a/solution.py
+++ b/solution.py
@@ -145,7 +145,8 @@
         )
         gate = halo
         early = jnp.concatenate([attended, query_grad], axis=1)
-        early = lax.all_to_all(early, ("tm", "space"), split_axis=0, concat_axis=0, tiled=True)
+        if chunk + 1 < CHUNKS:
+            early = lax.all_to_all(early, ("tm", "space"), split_axis=0, concat_axis=0, tiled=True)
         backs.append((early, key_own, value_own, nb_b, nb_a, nb_l, nb_r))
     outs = []
     prior = None
@@ -167,9 +168,13 @@
         terms = sum(part.astype(jnp.float32) for part in received)
         key_grad = (key_own + terms[0]).astype(jnp.bfloat16)
         value_grad = (value_own + terms[1]).astype(jnp.bfloat16)
-        late = jnp.concatenate([key_grad, value_grad], axis=1)
-        late = lax.all_to_all(late, ("tm", "space"), split_axis=0, concat_axis=0, tiled=True)
-        outs.append(jnp.concatenate([early, late], axis=1))
+        if chunk + 1 < CHUNKS:
+            late = jnp.concatenate([key_grad, value_grad], axis=1)
+            late = lax.all_to_all(late, ("tm", "space"), split_axis=0, concat_axis=0, tiled=True)
+            outs.append(jnp.concatenate([early, late], axis=1))
+        else:
+            late = jnp.concatenate([early, key_grad, value_grad], axis=1)
+            outs.append(lax.all_to_all(late, ("tm", "space"), split_axis=0, concat_axis=0, tiled=True))
     return tuple(
         jnp.concatenate([outs[chunk][:, i * width:(i + 1) * width] for chunk in range(CHUNKS)], axis=1)[landing]
         for i in range(4)

time: 391 us -> 402 us (1.028)
  waiting for transfers between devices: 155 us -> 171 us
  starting transfers between devices: 107 us -> 97.9 us
  local copies, waits for them, and re-layouts: 59.9 us -> 67.2 us
    ppermute x16, waiting for transfers between devices: 74.9 us -> 98.9 us  [shifted(): return lax.ppermute(block, axis, route)]
    all_to_all x2 -> x1, waiting for transfers between devices: 21.5 us -> 0.01 us  [shards(): lax.all_to_all(early, ('tm', 'space'), split_axis=0, concat_axis=0, tiled...]
    all_to_all x2 -> x1, starting transfers between devices: 23.2 us -> 9.5 us  [shards(): lax.all_to_all(early, ('tm', 'space'), split_axis=0, concat_axis=0, tiled...]
    all_to_all x2, waiting for transfers between devices: 13.1 us -> 26.5 us  [shards(): lax.all_to_all(late, ('tm', 'space'), split_axis=0, concat_axis=0, tiled=...]
    all_to_all x2, starting transfers between devices: 17.6 us -> 23.9 us  [shards(): lax.all_to_all(late, ('tm', 'space'), split_axis=0, concat_axis=0, tiled=...]
  transfers between devices with their start and end apart: 22 -> 21, of which waited for: 8 -> 10; matrix products, arithmetic and copies ran while one was open for 7% -> 5% of each run, Pallas kernels for 12% -> 12%
where the time goes in v3:
time: 402 us; the launch traced here: 401 us
  waiting for transfers between devices  171 us (43%)
  starting transfers between devices  97.9 us (24%)
  local copies, waits for them, and re-layouts  67.2 us (17%)
  Pallas kernels  46.5 us (12%)
  other arithmetic  15.3 us (4%)
    ppermute x16, waiting for transfers between devices, shifted(): return lax.ppermute(block, axis, route)  98.9 us
    ppermute x16, starting transfers between devices, shifted(): return lax.ppermute(block, axis, route)  48.1 us
    pallas_call x2, Pallas kernels, attend_tile(): pl.pallas_call(_attn_kernel, out_shape=out_shape, grid_spec=pltpu.Prefetc...  46.5 us
    all_to_all x2, waiting for transfers between devices, shards(): lax.all_to_all(send, ('tm', 'space'), split_axis=0, concat_axis=0, tiled=...  45.4 us
    all_to_all x2, waiting for transfers between devices, shards(): lax.all_to_all(late, ('tm', 'space'), split_axis=0, concat_axis=0, tiled=...  26.5 us
    all_to_all x2, starting transfers between devices, shards(): lax.all_to_all(late, ('tm', 'space'), split_axis=0, concat_axis=0, tiled=...  23.9 us
    all_to_all x2, starting transfers between devices, shards(): lax.all_to_all(send, ('tm', 'space'), split_axis=0, concat_axis=0, tiled=...  16.5 us
    all_to_all x4, local copies, waits for them, and re-layouts, shards(): lax.all_to_all(send, ('tm', 'space'), split_axis=0, concat_axis=0, tiled=...  13.9 us
  transfers between devices with their start and end apart: 21, of which 10 were waited for; matrix products, arithmetic and copies ran while one was open for 5% of the time, Pallas kernels for 12%

profile of v3, /device:TPU:1, one launch (start us, length us, event | category | flops | bytes accessed | tf_op | source)
XLA Modules:
  0.0 400.7 jit_solution(13467325243510647187)
XLA Ops:
  18.6 11.9 %all-to-all-start = ((bf16[128,2,5120]{2,1,0:T(2,128)(2,1)}), bf16[128,2,5120]{2,1,0:T(2,128)(2,1)}, u32[]{:S(2)}, u32[]{:S(2)}) async-start(bf16[128,2,5120]{2,1,0:T(2,128)(2,1)} %all_to_all.38), calls=%async_computation | async-start | bytes 5242880 | tf_op jit(solution)/shard_map/all_to_all | solution.py:133
  34.7 31.3 %all-to-all-done = bf16[128,2,5120]{2,1,0:T(2,128)(2,1)} async-done(((bf16[128,2,5120]{2,1,0:T(2,128)(2,1)}), bf16[128,2,5120]{2,1,0:T(2,128)(2,1)}, u32[]{:S(2)}, u32[]{:S(2)}) %all-to-all-start) | async-done | bytes 2621472 | tf_op jit(solution)/shard_map/all_to_all | solution.py:133
  65.9 4.6 %all-to-all-start.2 = ((bf16[128,2,5120]{2,1,0:T(2,128)(2,1)}), bf16[128,2,5120]{2,1,0:T(2,128)(2,1)S(1)}, u32[]{:S(2)}, u32[]{:S(2)}) async-start(bf16[128,2,5120]{2,1,0:T(2,128)(2,1)} %all_to_all.44), calls=%async_computation.2 | async-start | bytes 5242880 | tf_op jit(solution)/shard_map/all_to_all | solution.py:133
  70.6 6.5 %all_to_all.40.q_ref.g_ref.k_ref.v_ref = bf16[256,5120]{1,0:T(8,128)(2,1)} reshape(bf16[128,2,5120]{2,1,0:T(2,128)(2,1)} %all-to-all-done) | data formatting | bytes 5242880 | tf_op jit(solution)/shard_map/all_to_all | solution.py:133
  79.6 5.2 %collective-permute-start = (bf16[2,256,1280]{2,1,0:T(8,128)(2,1)}, bf16[2,256,1280]{2,1,0:T(8,128)(2,1)}, u32[]{:S(2)}, u32[]{:S(2)}) collective-permute-start(bf16[2,256,1280]{2,1,0:T(8,128)(2,1)} %pad_maximum_fusion.3), channel_id=1, source_target_pairs={{0,32},{32,64},{64,96},{1,33},{33,65},{65,97},{2,34},{34,66},{66,9... | collective-permute-start | bytes 3932168 | tf_op jit(solution)/shard_map/ppermute | solution.py:105
  86.7 4.4 %collective-permute-start.2 = (bf16[2,256,1280]{2,1,0:T(8,128)(2,1)}, bf16[2,256,1280]{2,1,0:T(8,128)(2,1)}, u32[]{:S(2)}, u32[]{:S(2)}) collective-permute-start(bf16[2,256,1280]{2,1,0:T(8,128)(2,1)} %pad_maximum_fusion.3), channel_id=1, source_target_pairs={{0,1},{1,2},{2,3},{3,4},{4,5},{5,6},{6,7},{7,8},{8,9},{9,10},{10,1... | collective-permute-start | bytes 3932168 | tf_op jit(solution)/shard_map/ppermute | solution.py:105
  92.4 14.1 %all-to-all-done.2 = bf16[128,2,5120]{2,1,0:T(2,128)(2,1)S(1)} async-done(((bf16[128,2,5120]{2,1,0:T(2,128)(2,1)}), bf16[128,2,5120]{2,1,0:T(2,128)(2,1)S(1)}, u32[]{:S(2)}, u32[]{:S(2)}) %all-to-all-start.2) | async-done | bytes 2621472 | tf_op jit(solution)/shard_map/all_to_all | solution.py:133
  110.5 30.4 %collective-permute-done.kb_ref = bf16[2,256,1280]{2,1,0:T(8,128)(2,1)} collective-permute-done((bf16[2,256,1280]{2,1,0:T(8,128)(2,1)}, bf16[2,256,1280]{2,1,0:T(8,128)(2,1)}, u32[]{:S(2)}, u32[]{:S(2)}) %collective-permute-start) | collective-permute-done | bytes 1310752 | tf_op jit(solution)/shard_map/ppermute | solution.py:105
  155.8 23.2 %shard_map.93 = (bf16[256,1280]{1,0:T(8,128)(2,1)}, bf16[256,1280]{1,0:T(8,128)(2,1)}, f32[256,1280]{1,0:T(8,128)}, f32[256,1280]{1,0:T(8,128)}, bf16[2,256,1280...) custom-call(s32[5]{0:T(128)} %convert_element_type.39.flags_ref, ...), custom_call_target="tpu_custom_call" | custom-call | flops 5033164800 | bytes 22282240 | tf_op jit(solution)/shard_map/pallas_call | solution.py:82
  179.0 10.4 %collective-permute-done.4.kb_ref = bf16[2,256,1280]{2,1,0:T(8,128)(2,1)S(1)} collective-permute-done((bf16[2,256,1280]{2,1,0:T(8,128)(2,1)S(1)}, bf16[2,256,1280]{2,1,0:T(8,128)(2,1)S(1)}, u32[]{:S(2)}, u32[]{:S(2)}) %collective-permute-start.4) | collective-permute-done | bytes 1310752 | tf_op jit(solution)/shard_map/ppermute | solution.py:105
  189.4 20.0 %collective-permute-done.5.ka_ref = bf16[2,256,1280]{2,1,0:T(8,128)(2,1)} collective-permute-done((bf16[2,256,1280]{2,1,0:T(8,128)(2,1)S(1)}, bf16[2,256,1280]{2,1,0:T(8,128)(2,1)}, u32[]{:S(2)}, u32[]{:S(2)}) %collective-permute-start.5) | collective-permute-done | bytes 1310752 | tf_op jit(solution)/shard_map/ppermute | solution.py:105
  210.8 5.1 %collective-permute-start.11 = (bf16[2,256,1280]{2,1,0:T(8,128)(2,1)}, bf16[2,256,1280]{2,1,0:T(8,128)(2,1)}, u32[]{:S(2)}, u32[]{:S(2)}) collective-permute-start(bf16[2,256,1280]{2,1,0:T(8,128)(2,1)} %get-tuple-element.46), channel_id=1, source_target_pairs={{0,1},{1,2},{2,3},{3,4},{4,5},{5,6},{6,7},{7,8},{8,9},{9,10},{10,1... | collective-permute-start | bytes 3932168 | tf_op jit(solution)/shard_map/ppermute | solution.py:105
  217.8 5.1 %collective-permute-start.9 = (bf16[2,256,1280]{2,1,0:T(8,128)(2,1)}, bf16[2,256,1280]{2,1,0:T(8,128)(2,1)}, u32[]{:S(2)}, u32[]{:S(2)}) collective-permute-start(bf16[2,256,1280]{2,1,0:T(8,128)(2,1)} %get-tuple-element.44), channel_id=1, source_target_pairs={{0,32},{32,64},{64,96},{1,33},{33,65},{65,97},{2,34},{34,66},{66,9... | collective-permute-start | bytes 3932168 | tf_op jit(solution)/shard_map/ppermute | solution.py:105
  225.7 9.5 %all-to-all-start.1 = ((bf16[128,2,2560]{2,1,0:T(2,128)(2,1)}), bf16[128,2,2560]{2,1,0:T(2,128)(2,1)S(1)}, u32[]{:S(2)}, u32[]{:S(2)}) async-start(bf16[128,2,2560]{2,1,0:T(2,128)(2,1)} %all_to_all.41), calls=%async_computation.1 | async-start | bytes 2621440 | tf_op jit(solution)/shard_map/all_to_all | solution.py:149
  235.2 23.3 %shard_map.94 = (bf16[256,1280]{1,0:T(8,128)(2,1)}, bf16[256,1280]{1,0:T(8,128)(2,1)}, f32[256,1280]{1,0:T(8,128)}, f32[256,1280]{1,0:T(8,128)}, bf16[2,256,1280...) custom-call(s32[5]{0:T(128)} %convert_element_type.39.flags_ref, ...), custom_call_target="tpu_custom_call" | custom-call | flops 5033164800 | bytes 22282240 | tf_op jit(solution)/shard_map/pallas_call | solution.py:82
  261.6 4.1 %collective-permute-start.13 = (bf16[2,256,1280]{2,1,0:T(8,128)(2,1)}, bf16[2,256,1280]{2,1,0:T(8,128)(2,1)}, u32[]{:S(2)}, u32[]{:S(2)}) collective-permute-start(bf16[2,256,1280]{2,1,0:T(8,128)(2,1)} %get-tuple-element.48), channel_id=1, source_target_pairs={{0,32},{32,64},{64,96},{1,33},{33,65},{65,97},{2,34},{34,66},{66,9... | collective-permute-start | bytes 3932168 | tf_op jit(solution)/shard_map/ppermute | solution.py:105
  267.0 5.1 %collective-permute-start.15 = (bf16[2,256,1280]{2,1,0:T(8,128)(2,1)}, bf16[2,256,1280]{2,1,0:T(8,128)(2,1)}, u32[]{:S(2)}, u32[]{:S(2)}) collective-permute-start(bf16[2,256,1280]{2,1,0:T(8,128)(2,1)} %get-tuple-element.50), channel_id=1, source_target_pairs={{0,1},{1,2},{2,3},{3,4},{4,5},{5,6},{6,7},{7,8},{8,9},{9,10},{10,1... | collective-permute-start | bytes 3932168 | tf_op jit(solution)/shard_map/ppermute | solution.py:105
  277.8 12.7 %all-to-all-start.4 = ((bf16[128,2,2560]{2,1,0:T(2,128)(2,1)}), bf16[128,2,2560]{2,1,0:T(2,128)(2,1)}, u32[]{:S(2)}, u32[]{:S(2)}) async-start(bf16[128,2,2560]{2,1,0:T(2,128)(2,1)} %all_to_all.50), calls=%async_computation.4 | async-start | bytes 2621440 | tf_op jit(solution)/shard_map/all_to_all | solution.py:173
  290.5 31.7 %collective-permute-done.12 = bf16[2,256,1280]{2,1,0:T(8,128)(2,1)} collective-permute-done((bf16[2,256,1280]{2,1,0:T(8,128)(2,1)}, bf16[2,256,1280]{2,1,0:T(8,128)(2,1)}, u32[]{:S(2)}, u32[]{:S(2)}) %collective-permute-start.12) | collective-permute-done | bytes 1310752 | tf_op jit(solution)/shard_map/ppermute | solution.py:105
  332.3 3.6 all-to-all-done.4
  335.9 11.2 %all-to-all-start.3 = ((bf16[128,2,5120]{2,1,0:T(2,128)(2,1)}), bf16[128,2,5120]{2,1,0:T(2,128)(2,1)S(1)}, u32[]{:S(2)}, u32[]{:S(2)}) async-start(bf16[128,2,5120]{2,1,0:T(2,128)(2,1)} %all_to_all.47), calls=%async_computation.3 | async-start | bytes 5242880 | tf_op jit(solution)/shard_map/all_to_all | solution.py:177
  347.1 4.1 %all_to_all.43 = bf16[256,2560]{1,0:T(8,128)(2,1)} reshape(bf16[128,2,2560]{2,1,0:T(2,128)(2,1)} %copy-done.6) | data formatting | bytes 2621440 | tf_op jit(solution)/shard_map/all_to_all | solution.py:149
  353.3 4.1 %all_to_all.52 = bf16[256,2560]{1,0:T(8,128)(2,1)} reshape(bf16[128,2,2560]{2,1,0:T(2,128)(2,1)} %all-to-all-done.4) | data formatting | bytes 2621440 | tf_op jit(solution)/shard_map/all_to_all | solution.py:173
  359.8 22.9 %all-to-all-done.3 = bf16[128,2,5120]{2,1,0:T(2,128)(2,1)S(1)} async-done(((bf16[128,2,5120]{2,1,0:T(2,128)(2,1)}), bf16[128,2,5120]{2,1,0:T(2,128)(2,1)S(1)}, u32[]{:S(2)}, u32[]{:S(2)}) %all-to-all-start.3) | async-done | bytes 2621472 | tf_op jit(solution)/shard_map/all_to_all | solution.py:177
  (106 shorter events, 93.2 us)
Async XLA Ops:
  18.6 47.3 %all-to-all-start = ((bf16[128,2,5120]{2,1,0:T(2,128)(2,1)}), bf16[128,2,5120]{2,1,0:T(2,128)(2,1)}, u32[]{:S(2)}, u32[]{:S(2)}) async-start(bf16[128,2,5120]{2,1,0:T(2,128)(2,1)} %all_to_all.38), calls=%async_computation | async-start | bytes 5242880 | tf_op jit(solution)/shard_map/all_to_all | solution.py:133
  65.9 40.6 %all-to-all-start.2 = ((bf16[128,2,5120]{2,1,0:T(2,128)(2,1)}), bf16[128,2,5120]{2,1,0:T(2,128)(2,1)S(1)}, u32[]{:S(2)}, u32[]{:S(2)}) async-start(bf16[128,2,5120]{2,1,0:T(2,128)(2,1)} %all_to_all.44), calls=%async_computation.2 | async-start | bytes 5242880 | tf_op jit(solution)/shard_map/all_to_all | solution.py:133
  79.6 61.3 %collective-permute-start = (bf16[2,256,1280]{2,1,0:T(8,128)(2,1)}, bf16[2,256,1280]{2,1,0:T(8,128)(2,1)}, u32[]{:S(2)}, u32[]{:S(2)}) collective-permute-start(bf16[2,256,1280]{2,1,0:T(8,128)(2,1)} %pad_maximum_fusion.3), channel_id=1, source_target_pairs={{0,32},{32,64},{64,96},{1,33},{33,65},{65,97},{2,34},{34,66},{66,9... | collective-permute-start | bytes 3932168 | tf_op jit(solution)/shard_map/ppermute | solution.py:105
  84.8 59.6 %collective-permute-start.1 = (bf16[2,256,1280]{2,1,0:T(8,128)(2,1)}, bf16[2,256,1280]{2,1,0:T(8,128)(2,1)}, u32[]{:S(2)}, u32[]{:S(2)}) collective-permute-start(bf16[2,256,1280]{2,1,0:T(8,128)(2,1)} %pad_maximum_fusion.3), channel_id=1, source_target_pairs={{32,0},{64,32},{96,64},{33,1},{65,33},{97,65},{34,2},{66,34},{98,6... | collective-permute-start | bytes 3932168 | tf_op jit(solution)/shard_map/ppermute | solution.py:105
  86.7 57.7 %collective-permute-start.2 = (bf16[2,256,1280]{2,1,0:T(8,128)(2,1)}, bf16[2,256,1280]{2,1,0:T(8,128)(2,1)}, u32[]{:S(2)}, u32[]{:S(2)}) collective-permute-start(bf16[2,256,1280]{2,1,0:T(8,128)(2,1)} %pad_maximum_fusion.3), channel_id=1, source_target_pairs={{0,1},{1,2},{2,3},{3,4},{4,5},{5,6},{6,7},{7,8},{8,9},{9,10},{10,1... | collective-permute-start | bytes 3932168 | tf_op jit(solution)/shard_map/ppermute | solution.py:105
  91.1 53.3 %collective-permute-start.3 = (bf16[2,256,1280]{2,1,0:T(8,128)(2,1)}, bf16[2,256,1280]{2,1,0:T(8,128)(2,1)}, u32[]{:S(2)}, u32[]{:S(2)}) collective-permute-start(bf16[2,256,1280]{2,1,0:T(8,128)(2,1)} %pad_maximum_fusion.3), channel_id=1, source_target_pairs={{1,0},{2,1},{3,2},{4,3},{5,4},{6,5},{7,6},{8,7},{9,8},{10,9},{11,1... | collective-permute-start | bytes 3932168 | tf_op jit(solution)/shard_map/ppermute | solution.py:105
  110.4 42.3 %copy-start.16 = (s32[4,1,2]{0,2,1:T(2,128)S(1)}, s32[4,1,2]{0,2,1:T(2,128)}, u32[]{:S(2)}) copy-start(s32[4,1,2]{0,2,1:T(2,128)} %param.11) | copy-start | bytes 100
  144.4 45.1 %collective-permute-start.4 = (bf16[2,256,1280]{2,1,0:T(8,128)(2,1)S(1)}, bf16[2,256,1280]{2,1,0:T(8,128)(2,1)S(1)}, u32[]{:S(2)}, u32[]{:S(2)}) collective-permute-start(bf16[2,256,1280]{2,1,0:T(8,128)(2,1)S(1)} %pad_maximum_fusion.5), channel_id=1, source_target_pairs={{0,32},{32,64},{64,96},{1,33},{33,65},{65,97},{2,34},{34,66},{66,9... | collective-permute-start | bytes 3932168 | tf_op jit(solution)/shard_map/ppermute | solution.py:105
  146.8 62.7 %collective-permute-start.5 = (bf16[2,256,1280]{2,1,0:T(8,128)(2,1)S(1)}, bf16[2,256,1280]{2,1,0:T(8,128)(2,1)}, u32[]{:S(2)}, u32[]{:S(2)}) collective-permute-start(bf16[2,256,1280]{2,1,0:T(8,128)(2,1)S(1)} %pad_maximum_fusion.5), channel_id=1, source_target_pairs={{32,0},{64,32},{96,64},{33,1},{65,33},{97,65},{34,2},{66,34},{98,6... | collective-permute-start | bytes 3932168 | tf_op jit(solution)/shard_map/ppermute | solution.py:105
  148.8 60.7 %collective-permute-start.6 = (bf16[2,256,1280]{2,1,0:T(8,128)(2,1)S(1)}, bf16[2,256,1280]{2,1,0:T(8,128)(2,1)}, u32[]{:S(2)}, u32[]{:S(2)}) collective-permute-start(bf16[2,256,1280]{2,1,0:T(8,128)(2,1)S(1)} %pad_maximum_fusion.5), channel_id=1, source_target_pairs={{0,1},{1,2},{2,3},{3,4},{4,5},{5,6},{6,7},{7,8},{8,9},{9,10},{10,1... | collective-permute-start | bytes 3932168 | tf_op jit(solution)/shard_map/ppermute | solution.py:105
  151.2 58.3 %collective-permute-start.7 = (bf16[2,256,1280]{2,1,0:T(8,128)(2,1)S(1)}, bf16[2,256,1280]{2,1,0:T(8,128)(2,1)}, u32[]{:S(2)}, u32[]{:S(2)}) collective-permute-start(bf16[2,256,1280]{2,1,0:T(8,128)(2,1)S(1)} %pad_maximum_fusion.5), channel_id=1, source_target_pairs={{1,0},{2,1},{3,2},{4,3},{5,4},{6,5},{7,6},{8,7},{9,8},{10,9},{11,1... | collective-permute-start | bytes 3932168 | tf_op jit(solution)/shard_map/ppermute | solution.py:105
  209.5 48.9 %collective-permute-start.10 = (bf16[2,256,1280]{2,1,0:T(8,128)(2,1)}, bf16[2,256,1280]{2,1,0:T(8,128)(2,1)S(1)}, u32[]{:S(2)}, u32[]{:S(2)}) collective-permute-start(bf16[2,256,1280]{2,1,0:T(8,128)(2,1)} %get-tuple-element.45), channel_id=1, source_target_pairs={{1,0},{2,1},{3,2},{4,3},{5,4},{6,5},{7,6},{8,7},{9,8},{10,9},{11,1... | collective-permute-start | bytes 3932168 | tf_op jit(solution)/shard_map/ppermute | solution.py:105
  210.8 47.7 %collective-permute-start.11 = (bf16[2,256,1280]{2,1,0:T(8,128)(2,1)}, bf16[2,256,1280]{2,1,0:T(8,128)(2,1)}, u32[]{:S(2)}, u32[]{:S(2)}) collective-permute-start(bf16[2,256,1280]{2,1,0:T(8,128)(2,1)} %get-tuple-element.46), channel_id=1, source_target_pairs={{0,1},{1,2},{2,3},{3,4},{4,5},{5,6},{6,7},{7,8},{8,9},{9,10},{10,1... | collective-permute-start | bytes 3932168 | tf_op jit(solution)/shard_map/ppermute | solution.py:105
  215.9 42.6 %collective-permute-start.8 = (bf16[2,256,1280]{2,1,0:T(8,128)(2,1)}, bf16[2,256,1280]{2,1,0:T(8,128)(2,1)}, u32[]{:S(2)}, u32[]{:S(2)}) collective-permute-start(bf16[2,256,1280]{2,1,0:T(8,128)(2,1)} %get-tuple-element.43), channel_id=1, source_target_pairs={{32,0},{64,32},{96,64},{33,1},{65,33},{97,65},{34,2},{66,34},{98,6... | collective-permute-start | bytes 3932168 | tf_op jit(solution)/shard_map/ppermute | solution.py:105
  217.8 40.7 %collective-permute-start.9 = (bf16[2,256,1280]{2,1,0:T(8,128)(2,1)}, bf16[2,256,1280]{2,1,0:T(8,128)(2,1)}, u32[]{:S(2)}, u32[]{:S(2)}) collective-permute-start(bf16[2,256,1280]{2,1,0:T(8,128)(2,1)} %get-tuple-element.44), channel_id=1, source_target_pairs={{0,32},{32,64},{64,96},{1,33},{33,65},{65,97},{2,34},{34,66},{66,9... | collective-permute-start | bytes 3932168 | tf_op jit(solution)/shard_map/ppermute | solution.py:105
  225.7 51.0 %all-to-all-start.1 = ((bf16[128,2,2560]{2,1,0:T(2,128)(2,1)}), bf16[128,2,2560]{2,1,0:T(2,128)(2,1)S(1)}, u32[]{:S(2)}, u32[]{:S(2)}) async-start(bf16[128,2,2560]{2,1,0:T(2,128)(2,1)} %all_to_all.41), calls=%async_computation.1 | async-start | bytes 2621440 | tf_op jit(solution)/shard_map/all_to_all | solution.py:149
  258.5 63.7 %collective-permute-start.12 = (bf16[2,256,1280]{2,1,0:T(8,128)(2,1)}, bf16[2,256,1280]{2,1,0:T(8,128)(2,1)}, u32[]{:S(2)}, u32[]{:S(2)}) collective-permute-start(bf16[2,256,1280]{2,1,0:T(8,128)(2,1)} %get-tuple-element.47), channel_id=1, source_target_pairs={{32,0},{64,32},{96,64},{33,1},{65,33},{97,65},{34,2},{66,34},{98,6... | collective-permute-start | bytes 3932168 | tf_op jit(solution)/shard_map/ppermute | solution.py:105
  261.6 63.5 %collective-permute-start.13 = (bf16[2,256,1280]{2,1,0:T(8,128)(2,1)}, bf16[2,256,1280]{2,1,0:T(8,128)(2,1)}, u32[]{:S(2)}, u32[]{:S(2)}) collective-permute-start(bf16[2,256,1280]{2,1,0:T(8,128)(2,1)} %get-tuple-element.48), channel_id=1, source_target_pairs={{0,32},{32,64},{64,96},{1,33},{33,65},{65,97},{2,34},{34,66},{66,9... | collective-permute-start | bytes 3932168 | tf_op jit(solution)/shard_map/ppermute | solution.py:105
  265.7 59.4 %collective-permute-start.14 = (bf16[2,256,1280]{2,1,0:T(8,128)(2,1)}, bf16[2,256,1280]{2,1,0:T(8,128)(2,1)}, u32[]{:S(2)}, u32[]{:S(2)}) collective-permute-start(bf16[2,256,1280]{2,1,0:T(8,128)(2,1)} %get-tuple-element.49), channel_id=1, source_target_pairs={{1,0},{2,1},{3,2},{4,3},{5,4},{6,5},{7,6},{8,7},{9,8},{10,9},{11,1... | collective-permute-start | bytes 3932168 | tf_op jit(solution)/shard_map/ppermute | solution.py:105
  267.0 58.1 %collective-permute-start.15 = (bf16[2,256,1280]{2,1,0:T(8,128)(2,1)}, bf16[2,256,1280]{2,1,0:T(8,128)(2,1)}, u32[]{:S(2)}, u32[]{:S(2)}) collective-permute-start(bf16[2,256,1280]{2,1,0:T(8,128)(2,1)} %get-tuple-element.50), channel_id=1, source_target_pairs={{0,1},{1,2},{2,3},{3,4},{4,5},{5,6},{6,7},{7,8},{8,9},{9,10},{10,1... | collective-permute-start | bytes 3932168 | tf_op jit(solution)/shard_map/ppermute | solution.py:105
  277.8 58.1 %all-to-all-start.4 = ((bf16[128,2,2560]{2,1,0:T(2,128)(2,1)}), bf16[128,2,2560]{2,1,0:T(2,128)(2,1)}, u32[]{:S(2)}, u32[]{:S(2)}) async-start(bf16[128,2,2560]{2,1,0:T(2,128)(2,1)} %all_to_all.50), calls=%async_computation.4 | async-start | bytes 2621440 | tf_op jit(solution)/shard_map/all_to_all | solution.py:173
  290.5 37.7 %copy-start.12 = (f32[256,1280]{1,0:T(8,128)S(1)}, f32[256,1280]{1,0:T(8,128)}, u32[]{:S(2)}) copy-start(f32[256,1280]{1,0:T(8,128)} %get-tuple-element.34) | copy-start | bytes 3932164
  290.5 37.7 %copy-start.13 = (f32[256,1280]{1,0:T(8,128)S(1)}, f32[256,1280]{1,0:T(8,128)}, u32[]{:S(2)}) copy-start(f32[256,1280]{1,0:T(8,128)} %get-tuple-element.51) | copy-start | bytes 3932164
  335.9 46.8 %all-to-all-start.3 = ((bf16[128,2,5120]{2,1,0:T(2,128)(2,1)}), bf16[128,2,5120]{2,1,0:T(2,128)(2,1)S(1)}, u32[]{:S(2)}, u32[]{:S(2)}) async-start(bf16[128,2,5120]{2,1,0:T(2,128)(2,1)} %all_to_all.47), calls=%async_computation.3 | async-start | bytes 5242880 | tf_op jit(solution)/shard_map/all_to_all | solution.py:177
  (15 other events, 79.3 us)

commit v4 on v1

--- a/solution.py
+++ b/solution.py
@@ -152,9 +152,7 @@
     for chunk in range(CHUNKS):
         early, key_own, value_own, nb_b, nb_a, nb_l, nb_r = backs[chunk]
         sends = (nb_b, nb_a, nb_l, nb_r)
-        if prior is not None:
-            sends = lax.optimization_barrier(sends + prior)[:4]
-        elif CHUNKS > 1:
+        if prior is None and CHUNKS > 1:
             sends = lax.optimization_barrier(sends + gate)[:4]
         nb_b, nb_a, nb_l, nb_r = sends
         received = (

time: 391 us -> 387 us (0.990)
  no operation moved by 1% of the time
where the time goes in v4:
time: 387 us; the launch traced here: 385 us
  waiting for transfers between devices  153 us (40%)
  starting transfers between devices  105 us (27%)
  local copies, waits for them, and re-layouts  59.9 us (15%)
  Pallas kernels  46.5 us (12%)
  other arithmetic  17.9 us (5%)
    ppermute x16, waiting for transfers between devices, shifted(): return lax.ppermute(block, axis, route)  75.6 us
    ppermute x16, starting transfers between devices, shifted(): return lax.ppermute(block, axis, route)  50.1 us
    pallas_call x2, Pallas kernels, attend_tile(): pl.pallas_call(_attn_kernel, out_shape=out_shape, grid_spec=pltpu.Prefetc...  46.5 us
    all_to_all x2, waiting for transfers between devices, shards(): lax.all_to_all(send, ('tm', 'space'), split_axis=0, concat_axis=0, tiled=...  45.3 us
    all_to_all x2, starting transfers between devices, shards(): lax.all_to_all(early, ('tm', 'space'), split_axis=0, concat_axis=0, tiled...  23.1 us
    all_to_all x2, waiting for transfers between devices, shards(): lax.all_to_all(early, ('tm', 'space'), split_axis=0, concat_axis=0, tiled...  18.5 us
    all_to_all x2, starting transfers between devices, shards(): lax.all_to_all(send, ('tm', 'space'), split_axis=0, concat_axis=0, tiled=...  16.5 us
    all_to_all x2, starting transfers between devices, shards(): lax.all_to_all(late, ('tm', 'space'), split_axis=0, concat_axis=0, tiled=...  15.5 us
  transfers between devices with their start and end apart: 22, of which 8 were waited for; matrix products, arithmetic and copies ran while one was open for 7% of the time, Pallas kernels for 12%

profile of v4, /device:TPU:1, one launch (start us, length us, event | category | flops | bytes accessed | tf_op | source)
XLA Modules:
  0.0 385.4 jit_solution(13351657746349091271)
XLA Ops:
  18.7 11.9 %all-to-all-start = ((bf16[128,2,5120]{2,1,0:T(2,128)(2,1)}), bf16[128,2,5120]{2,1,0:T(2,128)(2,1)}, u32[]{:S(2)}, u32[]{:S(2)}) async-start(bf16[128,2,5120]{2,1,0:T(2,128)(2,1)} %all_to_all.46), calls=%async_computation | async-start | bytes 5242880 | tf_op jit(solution)/shard_map/all_to_all | solution.py:133
  34.6 31.3 %all-to-all-done = bf16[128,2,5120]{2,1,0:T(2,128)(2,1)} async-done(((bf16[128,2,5120]{2,1,0:T(2,128)(2,1)}), bf16[128,2,5120]{2,1,0:T(2,128)(2,1)}, u32[]{:S(2)}, u32[]{:S(2)}) %all-to-all-start) | async-done | bytes 2621472 | tf_op jit(solution)/shard_map/all_to_all | solution.py:133
  65.9 4.6 %all-to-all-start.2 = ((bf16[128,2,5120]{2,1,0:T(2,128)(2,1)}), bf16[128,2,5120]{2,1,0:T(2,128)(2,1)S(1)}, u32[]{:S(2)}, u32[]{:S(2)}) async-start(bf16[128,2,5120]{2,1,0:T(2,128)(2,1)} %all_to_all.52), calls=%async_computation.2 | async-start | bytes 5242880 | tf_op jit(solution)/shard_map/all_to_all | solution.py:133
  70.6 6.5 %all_to_all.48.q_ref.g_ref.k_ref.v_ref = bf16[256,5120]{1,0:T(8,128)(2,1)} reshape(bf16[128,2,5120]{2,1,0:T(2,128)(2,1)} %all-to-all-done) | data formatting | bytes 5242880 | tf_op jit(solution)/shard_map/all_to_all | solution.py:133
  79.6 5.2 %collective-permute-start = (bf16[2,256,1280]{2,1,0:T(8,128)(2,1)}, bf16[2,256,1280]{2,1,0:T(8,128)(2,1)}, u32[]{:S(2)}, u32[]{:S(2)}) collective-permute-start(bf16[2,256,1280]{2,1,0:T(8,128)(2,1)} %pad_maximum_fusion.2), channel_id=1, source_target_pairs={{0,32},{32,64},{64,96},{1,33},{33,65},{65,97},{2,34},{34,66},{66,9... | collective-permute-start | bytes 3932168 | tf_op jit(solution)/shard_map/ppermute | solution.py:105
  86.7 4.4 %collective-permute-start.2 = (bf16[2,256,1280]{2,1,0:T(8,128)(2,1)}, bf16[2,256,1280]{2,1,0:T(8,128)(2,1)}, u32[]{:S(2)}, u32[]{:S(2)}) collective-permute-start(bf16[2,256,1280]{2,1,0:T(8,128)(2,1)} %pad_maximum_fusion.2), channel_id=1, source_target_pairs={{0,1},{1,2},{2,3},{3,4},{4,5},{5,6},{6,7},{7,8},{8,9},{9,10},{10,1... | collective-permute-start | bytes 3932168 | tf_op jit(solution)/shard_map/ppermute | solution.py:105
  92.5 14.0 %all-to-all-done.2 = bf16[128,2,5120]{2,1,0:T(2,128)(2,1)S(1)} async-done(((bf16[128,2,5120]{2,1,0:T(2,128)(2,1)}), bf16[128,2,5120]{2,1,0:T(2,128)(2,1)S(1)}, u32[]{:S(2)}, u32[]{:S(2)}) %all-to-all-start.2) | async-done | bytes 2621472 | tf_op jit(solution)/shard_map/all_to_all | solution.py:133
  110.5 30.4 %collective-permute-done.kb_ref = bf16[2,256,1280]{2,1,0:T(8,128)(2,1)} collective-permute-done((bf16[2,256,1280]{2,1,0:T(8,128)(2,1)}, bf16[2,256,1280]{2,1,0:T(8,128)(2,1)}, u32[]{:S(2)}, u32[]{:S(2)}) %collective-permute-start) | collective-permute-done | bytes 1310752 | tf_op jit(solution)/shard_map/ppermute | solution.py:105
  156.7 23.2 %shard_map.93 = (bf16[256,1280]{1,0:T(8,128)(2,1)}, bf16[256,1280]{1,0:T(8,128)(2,1)}, f32[256,1280]{1,0:T(8,128)}, f32[256,1280]{1,0:T(8,128)}, bf16[2,256,1280...) custom-call(s32[5]{0:T(128)} %convert_element_type.39.flags_ref, ...), custom_call_target="tpu_custom_call" | custom-call | flops 5033164800 | bytes 22282240 | tf_op jit(solution)/shard_map/pallas_call | solution.py:82
  182.8 13.3 %all-to-all-start.1 = ((bf16[128,2,2560]{2,1,0:T(2,128)(2,1)}), bf16[128,2,2560]{2,1,0:T(2,128)(2,1)S(1)}, u32[]{:S(2)}, u32[]{:S(2)}) async-start(bf16[128,2,2560]{2,1,0:T(2,128)(2,1)} %all_to_all.49), calls=%async_computation.1 | async-start | bytes 2621440 | tf_op jit(solution)/shard_map/all_to_all | solution.py:148
  197.4 5.1 %collective-permute-start.11 = (bf16[2,256,1280]{2,1,0:T(8,128)(2,1)}, bf16[2,256,1280]{2,1,0:T(8,128)(2,1)}, u32[]{:S(2)}, u32[]{:S(2)}) collective-permute-start(bf16[2,256,1280]{2,1,0:T(8,128)(2,1)} %get-tuple-element.38), channel_id=1, source_target_pairs={{0,1},{1,2},{2,3},{3,4},{4,5},{5,6},{6,7},{7,8},{8,9},{9,10},{10,1... | collective-permute-start | bytes 3932168 | tf_op jit(solution)/shard_map/ppermute | solution.py:105
  202.5 3.5 collective-permute-start.8
  206.0 4.0 %collective-permute-start.9 = (bf16[2,256,1280]{2,1,0:T(8,128)(2,1)}, bf16[2,256,1280]{2,1,0:T(8,128)(2,1)}, u32[]{:S(2)}, u32[]{:S(2)}) collective-permute-start(bf16[2,256,1280]{2,1,0:T(8,128)(2,1)} %get-tuple-element.36), channel_id=1, source_target_pairs={{0,32},{32,64},{64,96},{1,33},{33,65},{65,97},{2,34},{34,66},{66,9... | collective-permute-start | bytes 3932168 | tf_op jit(solution)/shard_map/ppermute | solution.py:105
  210.0 23.3 %shard_map.94 = (bf16[256,1280]{1,0:T(8,128)(2,1)}, bf16[256,1280]{1,0:T(8,128)(2,1)}, f32[256,1280]{1,0:T(8,128)}, f32[256,1280]{1,0:T(8,128)}, bf16[2,256,1280...) custom-call(s32[5]{0:T(128)} %convert_element_type.39.flags_ref, ...), custom_call_target="tpu_custom_call" | custom-call | flops 5033164800 | bytes 22282240 | tf_op jit(solution)/shard_map/pallas_call | solution.py:82
  236.0 9.9 %all-to-all-start.3 = ((bf16[128,2,2560]{2,1,0:T(2,128)(2,1)}), bf16[128,2,2560]{2,1,0:T(2,128)(2,1)S(1)}, u32[]{:S(2)}, u32[]{:S(2)}) async-start(bf16[128,2,2560]{2,1,0:T(2,128)(2,1)} %all_to_all.55), calls=%async_computation.3 | async-start | bytes 2621440 | tf_op jit(solution)/shard_map/all_to_all | solution.py:148
  252.5 18.5 %all-to-all-done.3 = bf16[128,2,2560]{2,1,0:T(2,128)(2,1)S(1)} async-done(((bf16[128,2,2560]{2,1,0:T(2,128)(2,1)}), bf16[128,2,2560]{2,1,0:T(2,128)(2,1)S(1)}, u32[]{:S(2)}, u32[]{:S(2)}) %all-to-all-start.3) | async-done | bytes 1310752 | tf_op jit(solution)/shard_map/all_to_all | solution.py:148
  271.5 4.8 %collective-permute-start.13 = (bf16[2,256,1280]{2,1,0:T(8,128)(2,1)}, bf16[2,256,1280]{2,1,0:T(8,128)(2,1)}, u32[]{:S(2)}, u32[]{:S(2)}) collective-permute-start(bf16[2,256,1280]{2,1,0:T(8,128)(2,1)} %get-tuple-element.42), channel_id=1, source_target_pairs={{0,32},{32,64},{64,96},{1,33},{33,65},{65,97},{2,34},{34,66},{66,9... | collective-permute-start | bytes 3932168 | tf_op jit(solution)/shard_map/ppermute | solution.py:105
  277.7 5.2 %collective-permute-start.15 = (bf16[2,256,1280]{2,1,0:T(8,128)(2,1)}, bf16[2,256,1280]{2,1,0:T(8,128)(2,1)}, u32[]{:S(2)}, u32[]{:S(2)}) collective-permute-start(bf16[2,256,1280]{2,1,0:T(8,128)(2,1)} %get-tuple-element.44), channel_id=1, source_target_pairs={{0,1},{1,2},{2,3},{3,4},{4,5},{5,6},{6,7},{7,8},{8,9},{9,10},{10,1... | collective-permute-start | bytes 3932168 | tf_op jit(solution)/shard_map/ppermute | solution.py:105
  287.8 6.2 %all-to-all-start.4 = ((bf16[128,2,2560]{2,1,0:T(2,128)(2,1)}), bf16[128,2,2560]{2,1,0:T(2,128)(2,1)S(1)}, u32[]{:S(2)}, u32[]{:S(2)}) async-start(bf16[128,2,2560]{2,1,0:T(2,128)(2,1)} %all_to_all.58), calls=%async_computation.4 | async-start | bytes 2621440 | tf_op jit(solution)/shard_map/all_to_all | solution.py:169
  294.1 32.8 %collective-permute-done.12 = bf16[2,256,1280]{2,1,0:T(8,128)(2,1)} collective-permute-done((bf16[2,256,1280]{2,1,0:T(8,128)(2,1)}, bf16[2,256,1280]{2,1,0:T(8,128)(2,1)}, u32[]{:S(2)}, u32[]{:S(2)}) %collective-permute-start.12) | collective-permute-done | bytes 1310752 | tf_op jit(solution)/shard_map/ppermute | solution.py:105
  326.8 8.9 %collective-permute-done.13 = bf16[2,256,1280]{2,1,0:T(8,128)(2,1)} collective-permute-done((bf16[2,256,1280]{2,1,0:T(8,128)(2,1)}, bf16[2,256,1280]{2,1,0:T(8,128)(2,1)}, u32[]{:S(2)}, u32[]{:S(2)}) %collective-permute-start.13) | collective-permute-done | bytes 1310752 | tf_op jit(solution)/shard_map/ppermute | solution.py:105
  340.4 4.0 %all_to_all.61 = bf16[128,2,2560]{2,1,0:T(2,128)(2,1)} reshape(bf16[256,2560]{1,0:T(8,128)(2,1)} %pad_maximum_fusion.9) | data formatting | bytes 2621440 | tf_op jit(solution)/shard_map/all_to_all | solution.py:169
  344.3 9.3 %all-to-all-start.5 = ((bf16[128,2,2560]{2,1,0:T(2,128)(2,1)}), bf16[128,2,2560]{2,1,0:T(2,128)(2,1)}, u32[]{:S(2)}, u32[]{:S(2)}) async-start(bf16[128,2,2560]{2,1,0:T(2,128)(2,1)} %all_to_all.61), calls=%async_computation.5 | async-start | bytes 2621440 | tf_op jit(solution)/shard_map/all_to_all | solution.py:169
  361.8 13.1 %all-to-all-done.5 = bf16[128,2,2560]{2,1,0:T(2,128)(2,1)} async-done(((bf16[128,2,2560]{2,1,0:T(2,128)(2,1)}), bf16[128,2,2560]{2,1,0:T(2,128)(2,1)}, u32[]{:S(2)}, u32[]{:S(2)}) %all-to-all-start.5) | async-done | bytes 1310752 | tf_op jit(solution)/shard_map/all_to_all | solution.py:169
  (100 shorter events, 88.9 us)
Async XLA Ops:
  18.7 47.3 %all-to-all-start = ((bf16[128,2,5120]{2,1,0:T(2,128)(2,1)}), bf16[128,2,5120]{2,1,0:T(2,128)(2,1)}, u32[]{:S(2)}, u32[]{:S(2)}) async-start(bf16[128,2,5120]{2,1,0:T(2,128)(2,1)} %all_to_all.46), calls=%async_computation | async-start | bytes 5242880 | tf_op jit(solution)/shard_map/all_to_all | solution.py:133
  65.9 40.6 %all-to-all-start.2 = ((bf16[128,2,5120]{2,1,0:T(2,128)(2,1)}), bf16[128,2,5120]{2,1,0:T(2,128)(2,1)S(1)}, u32[]{:S(2)}, u32[]{:S(2)}) async-start(bf16[128,2,5120]{2,1,0:T(2,128)(2,1)} %all_to_all.52), calls=%async_computation.2 | async-start | bytes 5242880 | tf_op jit(solution)/shard_map/all_to_all | solution.py:133
  79.6 61.3 %collective-permute-start = (bf16[2,256,1280]{2,1,0:T(8,128)(2,1)}, bf16[2,256,1280]{2,1,0:T(8,128)(2,1)}, u32[]{:S(2)}, u32[]{:S(2)}) collective-permute-start(bf16[2,256,1280]{2,1,0:T(8,128)(2,1)} %pad_maximum_fusion.2), channel_id=1, source_target_pairs={{0,32},{32,64},{64,96},{1,33},{33,65},{65,97},{2,34},{34,66},{66,9... | collective-permute-start | bytes 3932168 | tf_op jit(solution)/shard_map/ppermute | solution.py:105
  84.8 59.6 %collective-permute-start.1 = (bf16[2,256,1280]{2,1,0:T(8,128)(2,1)}, bf16[2,256,1280]{2,1,0:T(8,128)(2,1)}, u32[]{:S(2)}, u32[]{:S(2)}) collective-permute-start(bf16[2,256,1280]{2,1,0:T(8,128)(2,1)} %pad_maximum_fusion.2), channel_id=1, source_target_pairs={{32,0},{64,32},{96,64},{33,1},{65,33},{97,65},{34,2},{66,34},{98,6... | collective-permute-start | bytes 3932168 | tf_op jit(solution)/shard_map/ppermute | solution.py:105
  86.7 57.7 %collective-permute-start.2 = (bf16[2,256,1280]{2,1,0:T(8,128)(2,1)}, bf16[2,256,1280]{2,1,0:T(8,128)(2,1)}, u32[]{:S(2)}, u32[]{:S(2)}) collective-permute-start(bf16[2,256,1280]{2,1,0:T(8,128)(2,1)} %pad_maximum_fusion.2), channel_id=1, source_target_pairs={{0,1},{1,2},{2,3},{3,4},{4,5},{5,6},{6,7},{7,8},{8,9},{9,10},{10,1... | collective-permute-start | bytes 3932168 | tf_op jit(solution)/shard_map/ppermute | solution.py:105
  91.1 53.2 %collective-permute-start.3 = (bf16[2,256,1280]{2,1,0:T(8,128)(2,1)}, bf16[2,256,1280]{2,1,0:T(8,128)(2,1)}, u32[]{:S(2)}, u32[]{:S(2)}) collective-permute-start(bf16[2,256,1280]{2,1,0:T(8,128)(2,1)} %pad_maximum_fusion.2), channel_id=1, source_target_pairs={{1,0},{2,1},{3,2},{4,3},{5,4},{6,5},{7,6},{8,7},{9,8},{10,9},{11,1... | collective-permute-start | bytes 3932168 | tf_op jit(solution)/shard_map/ppermute | solution.py:105
  144.4 51.6 %collective-permute-start.4 = (bf16[2,256,1280]{2,1,0:T(8,128)(2,1)S(1)}, bf16[2,256,1280]{2,1,0:T(8,128)(2,1)}, u32[]{:S(2)}, u32[]{:S(2)}) collective-permute-start(bf16[2,256,1280]{2,1,0:T(8,128)(2,1)S(1)} %pad_maximum_fusion.4), channel_id=1, source_target_pairs={{0,32},{32,64},{64,96},{1,33},{33,65},{65,97},{2,34},{34,66},{66,9... | collective-permute-start | bytes 3932168 | tf_op jit(solution)/shard_map/ppermute | solution.py:105
  146.8 49.2 %collective-permute-start.5 = (bf16[2,256,1280]{2,1,0:T(8,128)(2,1)S(1)}, bf16[2,256,1280]{2,1,0:T(8,128)(2,1)}, u32[]{:S(2)}, u32[]{:S(2)}) collective-permute-start(bf16[2,256,1280]{2,1,0:T(8,128)(2,1)S(1)} %pad_maximum_fusion.4), channel_id=1, source_target_pairs={{32,0},{64,32},{96,64},{33,1},{65,33},{97,65},{34,2},{66,34},{98,6... | collective-permute-start | bytes 3932168 | tf_op jit(solution)/shard_map/ppermute | solution.py:105
  149.8 46.3 %collective-permute-start.6 = (bf16[2,256,1280]{2,1,0:T(8,128)(2,1)S(1)}, bf16[2,256,1280]{2,1,0:T(8,128)(2,1)}, u32[]{:S(2)}, u32[]{:S(2)}) collective-permute-start(bf16[2,256,1280]{2,1,0:T(8,128)(2,1)S(1)} %pad_maximum_fusion.4), channel_id=1, source_target_pairs={{0,1},{1,2},{2,3},{3,4},{4,5},{5,6},{6,7},{7,8},{8,9},{9,10},{10,1... | collective-permute-start | bytes 3932168 | tf_op jit(solution)/shard_map/ppermute | solution.py:105
  152.2 43.9 %collective-permute-start.7 = (bf16[2,256,1280]{2,1,0:T(8,128)(2,1)S(1)}, bf16[2,256,1280]{2,1,0:T(8,128)(2,1)}, u32[]{:S(2)}, u32[]{:S(2)}) collective-permute-start(bf16[2,256,1280]{2,1,0:T(8,128)(2,1)S(1)} %pad_maximum_fusion.4), channel_id=1, source_target_pairs={{1,0},{2,1},{3,2},{4,3},{5,4},{6,5},{7,6},{8,7},{9,8},{10,9},{11,1... | collective-permute-start | bytes 3932168 | tf_op jit(solution)/shard_map/ppermute | solution.py:105
  182.8 53.2 %all-to-all-start.1 = ((bf16[128,2,2560]{2,1,0:T(2,128)(2,1)}), bf16[128,2,2560]{2,1,0:T(2,128)(2,1)S(1)}, u32[]{:S(2)}, u32[]{:S(2)}) async-start(bf16[128,2,2560]{2,1,0:T(2,128)(2,1)} %all_to_all.49), calls=%async_computation.1 | async-start | bytes 2621440 | tf_op jit(solution)/shard_map/all_to_all | solution.py:148
  196.1 75.4 %collective-permute-start.10 = (bf16[2,256,1280]{2,1,0:T(8,128)(2,1)}, bf16[2,256,1280]{2,1,0:T(8,128)(2,1)}, u32[]{:S(2)}, u32[]{:S(2)}) collective-permute-start(bf16[2,256,1280]{2,1,0:T(8,128)(2,1)} %get-tuple-element.37), channel_id=1, source_target_pairs={{1,0},{2,1},{3,2},{4,3},{5,4},{6,5},{7,6},{8,7},{9,8},{10,9},{11,1... | collective-permute-start | bytes 3932168 | tf_op jit(solution)/shard_map/ppermute | solution.py:105
  197.4 78.9 %collective-permute-start.11 = (bf16[2,256,1280]{2,1,0:T(8,128)(2,1)}, bf16[2,256,1280]{2,1,0:T(8,128)(2,1)}, u32[]{:S(2)}, u32[]{:S(2)}) collective-permute-start(bf16[2,256,1280]{2,1,0:T(8,128)(2,1)} %get-tuple-element.38), channel_id=1, source_target_pairs={{0,1},{1,2},{2,3},{3,4},{4,5},{5,6},{6,7},{7,8},{8,9},{9,10},{10,1... | collective-permute-start | bytes 3932168 | tf_op jit(solution)/shard_map/ppermute | solution.py:105
  202.5 75.2 %collective-permute-start.8 = (bf16[2,256,1280]{2,1,0:T(8,128)(2,1)}, bf16[2,256,1280]{2,1,0:T(8,128)(2,1)}, u32[]{:S(2)}, u32[]{:S(2)}) collective-permute-start(bf16[2,256,1280]{2,1,0:T(8,128)(2,1)} %get-tuple-element.35), channel_id=1, source_target_pairs={{32,0},{64,32},{96,64},{33,1},{65,33},{97,65},{34,2},{66,34},{98,6... | collective-permute-start | bytes 3932168 | tf_op jit(solution)/shard_map/ppermute | solution.py:105
  206.0 76.9 %collective-permute-start.9 = (bf16[2,256,1280]{2,1,0:T(8,128)(2,1)}, bf16[2,256,1280]{2,1,0:T(8,128)(2,1)}, u32[]{:S(2)}, u32[]{:S(2)}) collective-permute-start(bf16[2,256,1280]{2,1,0:T(8,128)(2,1)} %get-tuple-element.36), channel_id=1, source_target_pairs={{0,32},{32,64},{64,96},{1,33},{33,65},{65,97},{2,34},{34,66},{66,9... | collective-permute-start | bytes 3932168 | tf_op jit(solution)/shard_map/ppermute | solution.py:105
  236.0 35.0 %all-to-all-start.3 = ((bf16[128,2,2560]{2,1,0:T(2,128)(2,1)}), bf16[128,2,2560]{2,1,0:T(2,128)(2,1)S(1)}, u32[]{:S(2)}, u32[]{:S(2)}) async-start(bf16[128,2,2560]{2,1,0:T(2,128)(2,1)} %all_to_all.55), calls=%async_computation.3 | async-start | bytes 2621440 | tf_op jit(solution)/shard_map/all_to_all | solution.py:148
  249.5 77.4 %collective-permute-start.12 = (bf16[2,256,1280]{2,1,0:T(8,128)(2,1)}, bf16[2,256,1280]{2,1,0:T(8,128)(2,1)}, u32[]{:S(2)}, u32[]{:S(2)}) collective-permute-start(bf16[2,256,1280]{2,1,0:T(8,128)(2,1)} %get-tuple-element.41), channel_id=1, source_target_pairs={{32,0},{64,32},{96,64},{33,1},{65,33},{97,65},{34,2},{66,34},{98,6... | collective-permute-start | bytes 3932168 | tf_op jit(solution)/shard_map/ppermute | solution.py:105
  271.5 64.2 %collective-permute-start.13 = (bf16[2,256,1280]{2,1,0:T(8,128)(2,1)}, bf16[2,256,1280]{2,1,0:T(8,128)(2,1)}, u32[]{:S(2)}, u32[]{:S(2)}) collective-permute-start(bf16[2,256,1280]{2,1,0:T(8,128)(2,1)} %get-tuple-element.42), channel_id=1, source_target_pairs={{0,32},{32,64},{64,96},{1,33},{33,65},{65,97},{2,34},{34,66},{66,9... | collective-permute-start | bytes 3932168 | tf_op jit(solution)/shard_map/ppermute | solution.py:105
  276.3 59.4 %collective-permute-start.14 = (bf16[2,256,1280]{2,1,0:T(8,128)(2,1)}, bf16[2,256,1280]{2,1,0:T(8,128)(2,1)}, u32[]{:S(2)}, u32[]{:S(2)}) collective-permute-start(bf16[2,256,1280]{2,1,0:T(8,128)(2,1)} %get-tuple-element.43), channel_id=1, source_target_pairs={{1,0},{2,1},{3,2},{4,3},{5,4},{6,5},{7,6},{8,7},{9,8},{10,9},{11,1... | collective-permute-start | bytes 3932168 | tf_op jit(solution)/shard_map/ppermute | solution.py:105
  277.7 58.1 %collective-permute-start.15 = (bf16[2,256,1280]{2,1,0:T(8,128)(2,1)}, bf16[2,256,1280]{2,1,0:T(8,128)(2,1)}, u32[]{:S(2)}, u32[]{:S(2)}) collective-permute-start(bf16[2,256,1280]{2,1,0:T(8,128)(2,1)} %get-tuple-element.44), channel_id=1, source_target_pairs={{0,1},{1,2},{2,3},{3,4},{4,5},{5,6},{6,7},{7,8},{8,9},{9,10},{10,1... | collective-permute-start | bytes 3932168 | tf_op jit(solution)/shard_map/ppermute | solution.py:105
  287.8 56.5 %all-to-all-start.4 = ((bf16[128,2,2560]{2,1,0:T(2,128)(2,1)}), bf16[128,2,2560]{2,1,0:T(2,128)(2,1)S(1)}, u32[]{:S(2)}, u32[]{:S(2)}) async-start(bf16[128,2,2560]{2,1,0:T(2,128)(2,1)} %all_to_all.58), calls=%async_computation.4 | async-start | bytes 2621440 | tf_op jit(solution)/shard_map/all_to_all | solution.py:169
  294.0 44.8 %copy-start.9 = (f32[256,1280]{1,0:T(8,128)S(1)}, f32[256,1280]{1,0:T(8,128)}, u32[]{:S(2)}) copy-start(f32[256,1280]{1,0:T(8,128)} %get-tuple-element.40) | copy-start | bytes 3932164
  294.1 44.8 %copy-start.10 = (f32[256,1280]{1,0:T(8,128)S(1)}, f32[256,1280]{1,0:T(8,128)}, u32[]{:S(2)}) copy-start(f32[256,1280]{1,0:T(8,128)} %get-tuple-element.45) | copy-start | bytes 3932164
  344.3 30.6 %all-to-all-start.5 = ((bf16[128,2,2560]{2,1,0:T(2,128)(2,1)}), bf16[128,2,2560]{2,1,0:T(2,128)(2,1)}, u32[]{:S(2)}, u32[]{:S(2)}) async-start(bf16[128,2,2560]{2,1,0:T(2,128)(2,1)} %all_to_all.61), calls=%async_computation.5 | async-start | bytes 2621440 | tf_op jit(solution)/shard_map/all_to_all | solution.py:169
  (10 other events, 47.0 us)

commit v5 on v4

--- a/solution.py
+++ b/solution.py
@@ -13,6 +13,7 @@
 SETS = 5
 CHUNKS = 2
 NT_DIMS = (((1,), (1,)), ((), ()))
+TN_DIMS = (((0,), (0,)), ((), ()))
 
 
 def _attn_kernel(flags_ref, q_ref, g_ref, k_ref, v_ref, kb_ref, ka_ref, kl_ref, kr_ref,
@@ -33,7 +34,7 @@
         m = jnp.maximum(m, jnp.max(s, axis=1, keepdims=True))
     l = jnp.zeros((TILE, 1), jnp.float32)
     for a in range(SETS):
-        e = jnp.where(vis[a], jnp.exp(s_scr[a] - m), 0.0)
+        e = jnp.exp(s_scr[a] - m)
         s_scr[a] = e
         l = l + jnp.sum(e, axis=1, keepdims=True)
     inv = 1.0 / l
@@ -47,7 +48,7 @@
         rd = rd + jnp.sum(p * dp, axis=1, keepdims=True)
         s_scr[a] = p
         dp_scr[a] = dp
-        dv = jnp.dot(p.T.astype(jnp.bfloat16), g, preferred_element_type=jnp.float32)
+        dv = lax.dot_general(pb, g, TN_DIMS, preferred_element_type=jnp.float32)
         if a == 1:
             dvo_ref[...] = dv
         else:
@@ -55,9 +56,9 @@
     o_ref[...] = o.astype(jnp.bfloat16)
     dq = jnp.zeros((TILE, HD), jnp.float32)
     for a in range(SETS):
-        ds = s_scr[a] * (dp_scr[a] - rd) * scale
-        dq = dq + jnp.dot(ds.astype(jnp.bfloat16), keys[a], preferred_element_type=jnp.float32)
-        dk = jnp.dot(ds.T.astype(jnp.bfloat16), q, preferred_element_type=jnp.float32)
+        ds = (s_scr[a] * (dp_scr[a] - rd) * scale).astype(jnp.bfloat16)
+        dq = dq + jnp.dot(ds, keys[a], preferred_element_type=jnp.float32)
+        dk = lax.dot_general(ds, q, TN_DIMS, preferred_element_type=jnp.float32)
         if a == 1:
             dko_ref[...] = dk
         else:

time: 387 us -> 386 us (level)
  transfers between devices with their start and end apart: 22 -> 22, of which waited for: 8 -> 9; matrix products, arithmetic and copies ran while one was open for 7% -> 7% of each run, Pallas kernels for 12% -> 12%
where the time goes in v5:
time: 386 us; the launch traced here: 384 us
  waiting for transfers between devices  152 us (39%)
  starting transfers between devices  107 us (28%)
  local copies, waits for them, and re-layouts  59.9 us (16%)
  Pallas kernels  44.9 us (12%)
  other arithmetic  17.9 us (5%)
    ppermute x16, waiting for transfers between devices, shifted(): return lax.ppermute(block, axis, route)  75.7 us
    ppermute x16, starting transfers between devices, shifted(): return lax.ppermute(block, axis, route)  49.9 us
    all_to_all x2, waiting for transfers between devices, shards(): lax.all_to_all(send, ('tm', 'space'), split_axis=0, concat_axis=0, tiled=...  45.3 us
    pallas_call x2, Pallas kernels, attend_tile(): pl.pallas_call(_attn_kernel, out_shape=out_shape, grid_spec=pltpu.Prefetc...  44.9 us
    all_to_all x2, starting transfers between devices, shards(): lax.all_to_all(early, ('tm', 'space'), split_axis=0, concat_axis=0, tiled...  25 us
    all_to_all x2, waiting for transfers between devices, shards(): lax.all_to_all(early, ('tm', 'space'), split_axis=0, concat_axis=0, tiled...  17.5 us
    all_to_all x2, starting transfers between devices, shards(): lax.all_to_all(send, ('tm', 'space'), split_axis=0, concat_axis=0, tiled=...  16.5 us
    all_to_all x2, starting transfers between devices, shards(): lax.all_to_all(late, ('tm', 'space'), split_axis=0, concat_axis=0, tiled=...  15.6 us
  transfers between devices with their start and end apart: 22, of which 9 were waited for; matrix products, arithmetic and copies ran while one was open for 7% of the time, Pallas kernels for 12%

profile of v5, /device:TPU:1, one launch (start us, length us, event | category | flops | bytes accessed | tf_op | source)
XLA Modules:
  0.0 384.5 jit_solution(12767097887407729149)
XLA Ops:
  18.7 11.9 %all-to-all-start = ((bf16[128,2,5120]{2,1,0:T(2,128)(2,1)}), bf16[128,2,5120]{2,1,0:T(2,128)(2,1)}, u32[]{:S(2)}, u32[]{:S(2)}) async-start(bf16[128,2,5120]{2,1,0:T(2,128)(2,1)} %all_to_all.46), calls=%async_computation | async-start | bytes 5242880 | tf_op jit(solution)/shard_map/all_to_all | solution.py:134
  34.6 31.3 %all-to-all-done = bf16[128,2,5120]{2,1,0:T(2,128)(2,1)} async-done(((bf16[128,2,5120]{2,1,0:T(2,128)(2,1)}), bf16[128,2,5120]{2,1,0:T(2,128)(2,1)}, u32[]{:S(2)}, u32[]{:S(2)}) %all-to-all-start) | async-done | bytes 2621472 | tf_op jit(solution)/shard_map/all_to_all | solution.py:134
  65.9 4.6 %all-to-all-start.2 = ((bf16[128,2,5120]{2,1,0:T(2,128)(2,1)}), bf16[128,2,5120]{2,1,0:T(2,128)(2,1)S(1)}, u32[]{:S(2)}, u32[]{:S(2)}) async-start(bf16[128,2,5120]{2,1,0:T(2,128)(2,1)} %all_to_all.52), calls=%async_computation.2 | async-start | bytes 5242880 | tf_op jit(solution)/shard_map/all_to_all | solution.py:134
  70.6 6.5 %all_to_all.48.q_ref.g_ref.k_ref.v_ref = bf16[256,5120]{1,0:T(8,128)(2,1)} reshape(bf16[128,2,5120]{2,1,0:T(2,128)(2,1)} %all-to-all-done) | data formatting | bytes 5242880 | tf_op jit(solution)/shard_map/all_to_all | solution.py:134
  79.6 5.2 %collective-permute-start = (bf16[2,256,1280]{2,1,0:T(8,128)(2,1)}, bf16[2,256,1280]{2,1,0:T(8,128)(2,1)}, u32[]{:S(2)}, u32[]{:S(2)}) collective-permute-start(bf16[2,256,1280]{2,1,0:T(8,128)(2,1)} %pad_maximum_fusion.2), channel_id=1, source_target_pairs={{0,32},{32,64},{64,96},{1,33},{33,65},{65,97},{2,34},{34,66},{66,9... | collective-permute-start | bytes 3932168 | tf_op jit(solution)/shard_map/ppermute | solution.py:106
  86.7 4.4 %collective-permute-start.2 = (bf16[2,256,1280]{2,1,0:T(8,128)(2,1)}, bf16[2,256,1280]{2,1,0:T(8,128)(2,1)}, u32[]{:S(2)}, u32[]{:S(2)}) collective-permute-start(bf16[2,256,1280]{2,1,0:T(8,128)(2,1)} %pad_maximum_fusion.2), channel_id=1, source_target_pairs={{0,1},{1,2},{2,3},{3,4},{4,5},{5,6},{6,7},{7,8},{8,9},{9,10},{10,1... | collective-permute-start | bytes 3932168 | tf_op jit(solution)/shard_map/ppermute | solution.py:106
  92.5 14.0 %all-to-all-done.2 = bf16[128,2,5120]{2,1,0:T(2,128)(2,1)S(1)} async-done(((bf16[128,2,5120]{2,1,0:T(2,128)(2,1)}), bf16[128,2,5120]{2,1,0:T(2,128)(2,1)S(1)}, u32[]{:S(2)}, u32[]{:S(2)}) %all-to-all-start.2) | async-done | bytes 2621472 | tf_op jit(solution)/shard_map/all_to_all | solution.py:134
  110.5 30.4 %collective-permute-done.kb_ref = bf16[2,256,1280]{2,1,0:T(8,128)(2,1)} collective-permute-done((bf16[2,256,1280]{2,1,0:T(8,128)(2,1)}, bf16[2,256,1280]{2,1,0:T(8,128)(2,1)}, u32[]{:S(2)}, u32[]{:S(2)}) %collective-permute-start) | collective-permute-done | bytes 1310752 | tf_op jit(solution)/shard_map/ppermute | solution.py:106
  140.9 3.5 collective-permute-done.1.ka_ref
  156.7 22.4 %shard_map.93 = (bf16[256,1280]{1,0:T(8,128)(2,1)}, bf16[256,1280]{1,0:T(8,128)(2,1)}, f32[256,1280]{1,0:T(8,128)}, f32[256,1280]{1,0:T(8,128)}, bf16[2,256,1280...) custom-call(s32[5]{0:T(128)} %convert_element_type.39.flags_ref, ...), custom_call_target="tpu_custom_call" | custom-call | flops 5033164800 | bytes 22282240 | tf_op jit(solution)/shard_map/pallas_call | solution.py:83
  182.0 13.3 %all-to-all-start.1 = ((bf16[128,2,2560]{2,1,0:T(2,128)(2,1)}), bf16[128,2,2560]{2,1,0:T(2,128)(2,1)S(1)}, u32[]{:S(2)}, u32[]{:S(2)}) async-start(bf16[128,2,2560]{2,1,0:T(2,128)(2,1)} %all_to_all.49), calls=%async_computation.1 | async-start | bytes 2621440 | tf_op jit(solution)/shard_map/all_to_all | solution.py:149
  196.7 5.1 %collective-permute-start.11 = (bf16[2,256,1280]{2,1,0:T(8,128)(2,1)}, bf16[2,256,1280]{2,1,0:T(8,128)(2,1)}, u32[]{:S(2)}, u32[]{:S(2)}) collective-permute-start(bf16[2,256,1280]{2,1,0:T(8,128)(2,1)} %get-tuple-element.38), channel_id=1, source_target_pairs={{0,1},{1,2},{2,3},{3,4},{4,5},{5,6},{6,7},{7,8},{8,9},{9,10},{10,1... | collective-permute-start | bytes 3932168 | tf_op jit(solution)/shard_map/ppermute | solution.py:106
  205.2 4.0 %collective-permute-start.9 = (bf16[2,256,1280]{2,1,0:T(8,128)(2,1)}, bf16[2,256,1280]{2,1,0:T(8,128)(2,1)}, u32[]{:S(2)}, u32[]{:S(2)}) collective-permute-start(bf16[2,256,1280]{2,1,0:T(8,128)(2,1)} %get-tuple-element.36), channel_id=1, source_target_pairs={{0,32},{32,64},{64,96},{1,33},{33,65},{65,97},{2,34},{34,66},{66,9... | collective-permute-start | bytes 3932168 | tf_op jit(solution)/shard_map/ppermute | solution.py:106
  209.2 22.5 %shard_map.94 = (bf16[256,1280]{1,0:T(8,128)(2,1)}, bf16[256,1280]{1,0:T(8,128)(2,1)}, f32[256,1280]{1,0:T(8,128)}, f32[256,1280]{1,0:T(8,128)}, bf16[2,256,1280...) custom-call(s32[5]{0:T(128)} %convert_element_type.39.flags_ref, ...), custom_call_target="tpu_custom_call" | custom-call | flops 5033164800 | bytes 22282240 | tf_op jit(solution)/shard_map/pallas_call | solution.py:83
  234.4 11.7 %all-to-all-start.3 = ((bf16[128,2,2560]{2,1,0:T(2,128)(2,1)}), bf16[128,2,2560]{2,1,0:T(2,128)(2,1)S(1)}, u32[]{:S(2)}, u32[]{:S(2)}) async-start(bf16[128,2,2560]{2,1,0:T(2,128)(2,1)} %all_to_all.55), calls=%async_computation.3 | async-start | bytes 2621440 | tf_op jit(solution)/shard_map/all_to_all | solution.py:149
  252.7 17.5 %all-to-all-done.3 = bf16[128,2,2560]{2,1,0:T(2,128)(2,1)S(1)} async-done(((bf16[128,2,2560]{2,1,0:T(2,128)(2,1)}), bf16[128,2,2560]{2,1,0:T(2,128)(2,1)S(1)}, u32[]{:S(2)}, u32[]{:S(2)}) %all-to-all-start.3) | async-done | bytes 1310752 | tf_op jit(solution)/shard_map/all_to_all | solution.py:149
  270.7 4.8 %collective-permute-start.13 = (bf16[2,256,1280]{2,1,0:T(8,128)(2,1)}, bf16[2,256,1280]{2,1,0:T(8,128)(2,1)}, u32[]{:S(2)}, u32[]{:S(2)}) collective-permute-start(bf16[2,256,1280]{2,1,0:T(8,128)(2,1)} %get-tuple-element.42), channel_id=1, source_target_pairs={{0,32},{32,64},{64,96},{1,33},{33,65},{65,97},{2,34},{34,66},{66,9... | collective-permute-start | bytes 3932168 | tf_op jit(solution)/shard_map/ppermute | solution.py:106
  276.9 5.2 %collective-permute-start.15 = (bf16[2,256,1280]{2,1,0:T(8,128)(2,1)}, bf16[2,256,1280]{2,1,0:T(8,128)(2,1)}, u32[]{:S(2)}, u32[]{:S(2)}) collective-permute-start(bf16[2,256,1280]{2,1,0:T(8,128)(2,1)} %get-tuple-element.44), channel_id=1, source_target_pairs={{0,1},{1,2},{2,3},{3,4},{4,5},{5,6},{6,7},{7,8},{8,9},{9,10},{10,1... | collective-permute-start | bytes 3932168 | tf_op jit(solution)/shard_map/ppermute | solution.py:106
  287.0 6.4 %all-to-all-start.4 = ((bf16[128,2,2560]{2,1,0:T(2,128)(2,1)}), bf16[128,2,2560]{2,1,0:T(2,128)(2,1)S(1)}, u32[]{:S(2)}, u32[]{:S(2)}) async-start(bf16[128,2,2560]{2,1,0:T(2,128)(2,1)} %all_to_all.58), calls=%async_computation.4 | async-start | bytes 2621440 | tf_op jit(solution)/shard_map/all_to_all | solution.py:170
  293.4 32.6 %collective-permute-done.12 = bf16[2,256,1280]{2,1,0:T(8,128)(2,1)} collective-permute-done((bf16[2,256,1280]{2,1,0:T(8,128)(2,1)}, bf16[2,256,1280]{2,1,0:T(8,128)(2,1)}, u32[]{:S(2)}, u32[]{:S(2)}) %collective-permute-start.12) | collective-permute-done | bytes 1310752 | tf_op jit(solution)/shard_map/ppermute | solution.py:106
  326.1 8.9 %collective-permute-done.13 = bf16[2,256,1280]{2,1,0:T(8,128)(2,1)} collective-permute-done((bf16[2,256,1280]{2,1,0:T(8,128)(2,1)}, bf16[2,256,1280]{2,1,0:T(8,128)(2,1)}, u32[]{:S(2)}, u32[]{:S(2)}) %collective-permute-start.13) | collective-permute-done | bytes 1310752 | tf_op jit(solution)/shard_map/ppermute | solution.py:106
  339.6 4.0 %all_to_all.61 = bf16[128,2,2560]{2,1,0:T(2,128)(2,1)} reshape(bf16[256,2560]{1,0:T(8,128)(2,1)} %pad_maximum_fusion.9) | data formatting | bytes 2621440 | tf_op jit(solution)/shard_map/all_to_all | solution.py:170
  343.6 9.2 %all-to-all-start.5 = ((bf16[128,2,2560]{2,1,0:T(2,128)(2,1)}), bf16[128,2,2560]{2,1,0:T(2,128)(2,1)}, u32[]{:S(2)}, u32[]{:S(2)}) async-start(bf16[128,2,2560]{2,1,0:T(2,128)(2,1)} %all_to_all.61), calls=%async_computation.5 | async-start | bytes 2621440 | tf_op jit(solution)/shard_map/all_to_all | solution.py:170
  360.9 13.1 %all-to-all-done.5 = bf16[128,2,2560]{2,1,0:T(2,128)(2,1)} async-done(((bf16[128,2,2560]{2,1,0:T(2,128)(2,1)}), bf16[128,2,2560]{2,1,0:T(2,128)(2,1)}, u32[]{:S(2)}, u32[]{:S(2)}) %all-to-all-start.5) | async-done | bytes 1310752 | tf_op jit(solution)/shard_map/all_to_all | solution.py:170
  (100 shorter events, 88.9 us)
Async XLA Ops:
  18.7 47.3 %all-to-all-start = ((bf16[128,2,5120]{2,1,0:T(2,128)(2,1)}), bf16[128,2,5120]{2,1,0:T(2,128)(2,1)}, u32[]{:S(2)}, u32[]{:S(2)}) async-start(bf16[128,2,5120]{2,1,0:T(2,128)(2,1)} %all_to_all.46), calls=%async_computation | async-start | bytes 5242880 | tf_op jit(solution)/shard_map/all_to_all | solution.py:134
  65.9 40.6 %all-to-all-start.2 = ((bf16[128,2,5120]{2,1,0:T(2,128)(2,1)}), bf16[128,2,5120]{2,1,0:T(2,128)(2,1)S(1)}, u32[]{:S(2)}, u32[]{:S(2)}) async-start(bf16[128,2,5120]{2,1,0:T(2,128)(2,1)} %all_to_all.52), calls=%async_computation.2 | async-start | bytes 5242880 | tf_op jit(solution)/shard_map/all_to_all | solution.py:134
  79.6 61.3 %collective-permute-start = (bf16[2,256,1280]{2,1,0:T(8,128)(2,1)}, bf16[2,256,1280]{2,1,0:T(8,128)(2,1)}, u32[]{:S(2)}, u32[]{:S(2)}) collective-permute-start(bf16[2,256,1280]{2,1,0:T(8,128)(2,1)} %pad_maximum_fusion.2), channel_id=1, source_target_pairs={{0,32},{32,64},{64,96},{1,33},{33,65},{65,97},{2,34},{34,66},{66,9... | collective-permute-start | bytes 3932168 | tf_op jit(solution)/shard_map/ppermute | solution.py:106
  84.8 59.6 %collective-permute-start.1 = (bf16[2,256,1280]{2,1,0:T(8,128)(2,1)}, bf16[2,256,1280]{2,1,0:T(8,128)(2,1)}, u32[]{:S(2)}, u32[]{:S(2)}) collective-permute-start(bf16[2,256,1280]{2,1,0:T(8,128)(2,1)} %pad_maximum_fusion.2), channel_id=1, source_target_pairs={{32,0},{64,32},{96,64},{33,1},{65,33},{97,65},{34,2},{66,34},{98,6... | collective-permute-start | bytes 3932168 | tf_op jit(solution)/shard_map/ppermute | solution.py:106
  86.7 57.7 %collective-permute-start.2 = (bf16[2,256,1280]{2,1,0:T(8,128)(2,1)}, bf16[2,256,1280]{2,1,0:T(8,128)(2,1)}, u32[]{:S(2)}, u32[]{:S(2)}) collective-permute-start(bf16[2,256,1280]{2,1,0:T(8,128)(2,1)} %pad_maximum_fusion.2), channel_id=1, source_target_pairs={{0,1},{1,2},{2,3},{3,4},{4,5},{5,6},{6,7},{7,8},{8,9},{9,10},{10,1... | collective-permute-start | bytes 3932168 | tf_op jit(solution)/shard_map/ppermute | solution.py:106
  91.1 53.2 %collective-permute-start.3 = (bf16[2,256,1280]{2,1,0:T(8,128)(2,1)}, bf16[2,256,1280]{2,1,0:T(8,128)(2,1)}, u32[]{:S(2)}, u32[]{:S(2)}) collective-permute-start(bf16[2,256,1280]{2,1,0:T(8,128)(2,1)} %pad_maximum_fusion.2), channel_id=1, source_target_pairs={{1,0},{2,1},{3,2},{4,3},{5,4},{6,5},{7,6},{8,7},{9,8},{10,9},{11,1... | collective-permute-start | bytes 3932168 | tf_op jit(solution)/shard_map/ppermute | solution.py:106
  144.4 50.9 %collective-permute-start.4 = (bf16[2,256,1280]{2,1,0:T(8,128)(2,1)S(1)}, bf16[2,256,1280]{2,1,0:T(8,128)(2,1)}, u32[]{:S(2)}, u32[]{:S(2)}) collective-permute-start(bf16[2,256,1280]{2,1,0:T(8,128)(2,1)S(1)} %pad_maximum_fusion.4), channel_id=1, source_target_pairs={{0,32},{32,64},{64,96},{1,33},{33,65},{65,97},{2,34},{34,66},{66,9... | collective-permute-start | bytes 3932168 | tf_op jit(solution)/shard_map/ppermute | solution.py:106
  146.8 48.6 %collective-permute-start.5 = (bf16[2,256,1280]{2,1,0:T(8,128)(2,1)S(1)}, bf16[2,256,1280]{2,1,0:T(8,128)(2,1)}, u32[]{:S(2)}, u32[]{:S(2)}) collective-permute-start(bf16[2,256,1280]{2,1,0:T(8,128)(2,1)S(1)} %pad_maximum_fusion.4), channel_id=1, source_target_pairs={{32,0},{64,32},{96,64},{33,1},{65,33},{97,65},{34,2},{66,34},{98,6... | collective-permute-start | bytes 3932168 | tf_op jit(solution)/shard_map/ppermute | solution.py:106
  149.8 45.7 %collective-permute-start.6 = (bf16[2,256,1280]{2,1,0:T(8,128)(2,1)S(1)}, bf16[2,256,1280]{2,1,0:T(8,128)(2,1)}, u32[]{:S(2)}, u32[]{:S(2)}) collective-permute-start(bf16[2,256,1280]{2,1,0:T(8,128)(2,1)S(1)} %pad_maximum_fusion.4), channel_id=1, source_target_pairs={{0,1},{1,2},{2,3},{3,4},{4,5},{5,6},{6,7},{7,8},{8,9},{9,10},{10,1... | collective-permute-start | bytes 3932168 | tf_op jit(solution)/shard_map/ppermute | solution.py:106
  152.2 43.3 %collective-permute-start.7 = (bf16[2,256,1280]{2,1,0:T(8,128)(2,1)S(1)}, bf16[2,256,1280]{2,1,0:T(8,128)(2,1)}, u32[]{:S(2)}, u32[]{:S(2)}) collective-permute-start(bf16[2,256,1280]{2,1,0:T(8,128)(2,1)S(1)} %pad_maximum_fusion.4), channel_id=1, source_target_pairs={{1,0},{2,1},{3,2},{4,3},{5,4},{6,5},{7,6},{8,7},{9,8},{10,9},{11,1... | collective-permute-start | bytes 3932168 | tf_op jit(solution)/shard_map/ppermute | solution.py:106
  182.0 52.4 %all-to-all-start.1 = ((bf16[128,2,2560]{2,1,0:T(2,128)(2,1)}), bf16[128,2,2560]{2,1,0:T(2,128)(2,1)S(1)}, u32[]{:S(2)}, u32[]{:S(2)}) async-start(bf16[128,2,2560]{2,1,0:T(2,128)(2,1)} %all_to_all.49), calls=%async_computation.1 | async-start | bytes 2621440 | tf_op jit(solution)/shard_map/all_to_all | solution.py:149
  195.5 75.3 %collective-permute-start.10 = (bf16[2,256,1280]{2,1,0:T(8,128)(2,1)}, bf16[2,256,1280]{2,1,0:T(8,128)(2,1)}, u32[]{:S(2)}, u32[]{:S(2)}) collective-permute-start(bf16[2,256,1280]{2,1,0:T(8,128)(2,1)} %get-tuple-element.37), channel_id=1, source_target_pairs={{1,0},{2,1},{3,2},{4,3},{5,4},{6,5},{7,6},{8,7},{9,8},{10,9},{11,1... | collective-permute-start | bytes 3932168 | tf_op jit(solution)/shard_map/ppermute | solution.py:106
  196.7 78.8 %collective-permute-start.11 = (bf16[2,256,1280]{2,1,0:T(8,128)(2,1)}, bf16[2,256,1280]{2,1,0:T(8,128)(2,1)}, u32[]{:S(2)}, u32[]{:S(2)}) collective-permute-start(bf16[2,256,1280]{2,1,0:T(8,128)(2,1)} %get-tuple-element.38), channel_id=1, source_target_pairs={{0,1},{1,2},{2,3},{3,4},{4,5},{5,6},{6,7},{7,8},{8,9},{9,10},{10,1... | collective-permute-start | bytes 3932168 | tf_op jit(solution)/shard_map/ppermute | solution.py:106
  201.8 75.0 %collective-permute-start.8 = (bf16[2,256,1280]{2,1,0:T(8,128)(2,1)}, bf16[2,256,1280]{2,1,0:T(8,128)(2,1)}, u32[]{:S(2)}, u32[]{:S(2)}) collective-permute-start(bf16[2,256,1280]{2,1,0:T(8,128)(2,1)} %get-tuple-element.35), channel_id=1, source_target_pairs={{32,0},{64,32},{96,64},{33,1},{65,33},{97,65},{34,2},{66,34},{98,6... | collective-permute-start | bytes 3932168 | tf_op jit(solution)/shard_map/ppermute | solution.py:106
  205.2 76.9 %collective-permute-start.9 = (bf16[2,256,1280]{2,1,0:T(8,128)(2,1)}, bf16[2,256,1280]{2,1,0:T(8,128)(2,1)}, u32[]{:S(2)}, u32[]{:S(2)}) collective-permute-start(bf16[2,256,1280]{2,1,0:T(8,128)(2,1)} %get-tuple-element.36), channel_id=1, source_target_pairs={{0,32},{32,64},{64,96},{1,33},{33,65},{65,97},{2,34},{34,66},{66,9... | collective-permute-start | bytes 3932168 | tf_op jit(solution)/shard_map/ppermute | solution.py:106
  234.4 35.8 %all-to-all-start.3 = ((bf16[128,2,2560]{2,1,0:T(2,128)(2,1)}), bf16[128,2,2560]{2,1,0:T(2,128)(2,1)S(1)}, u32[]{:S(2)}, u32[]{:S(2)}) async-start(bf16[128,2,2560]{2,1,0:T(2,128)(2,1)} %all_to_all.55), calls=%async_computation.3 | async-start | bytes 2621440 | tf_op jit(solution)/shard_map/all_to_all | solution.py:149
  249.7 76.4 %collective-permute-start.12 = (bf16[2,256,1280]{2,1,0:T(8,128)(2,1)}, bf16[2,256,1280]{2,1,0:T(8,128)(2,1)}, u32[]{:S(2)}, u32[]{:S(2)}) collective-permute-start(bf16[2,256,1280]{2,1,0:T(8,128)(2,1)} %get-tuple-element.41), channel_id=1, source_target_pairs={{32,0},{64,32},{96,64},{33,1},{65,33},{97,65},{34,2},{66,34},{98,6... | collective-permute-start | bytes 3932168 | tf_op jit(solution)/shard_map/ppermute | solution.py:106
  270.7 64.2 %collective-permute-start.13 = (bf16[2,256,1280]{2,1,0:T(8,128)(2,1)}, bf16[2,256,1280]{2,1,0:T(8,128)(2,1)}, u32[]{:S(2)}, u32[]{:S(2)}) collective-permute-start(bf16[2,256,1280]{2,1,0:T(8,128)(2,1)} %get-tuple-element.42), channel_id=1, source_target_pairs={{0,32},{32,64},{64,96},{1,33},{33,65},{65,97},{2,34},{34,66},{66,9... | collective-permute-start | bytes 3932168 | tf_op jit(solution)/shard_map/ppermute | solution.py:106
  275.5 59.4 %collective-permute-start.14 = (bf16[2,256,1280]{2,1,0:T(8,128)(2,1)}, bf16[2,256,1280]{2,1,0:T(8,128)(2,1)}, u32[]{:S(2)}, u32[]{:S(2)}) collective-permute-start(bf16[2,256,1280]{2,1,0:T(8,128)(2,1)} %get-tuple-element.43), channel_id=1, source_target_pairs={{1,0},{2,1},{3,2},{4,3},{5,4},{6,5},{7,6},{8,7},{9,8},{10,9},{11,1... | collective-permute-start | bytes 3932168 | tf_op jit(solution)/shard_map/ppermute | solution.py:106
  276.9 58.1 %collective-permute-start.15 = (bf16[2,256,1280]{2,1,0:T(8,128)(2,1)}, bf16[2,256,1280]{2,1,0:T(8,128)(2,1)}, u32[]{:S(2)}, u32[]{:S(2)}) collective-permute-start(bf16[2,256,1280]{2,1,0:T(8,128)(2,1)} %get-tuple-element.44), channel_id=1, source_target_pairs={{0,1},{1,2},{2,3},{3,4},{4,5},{5,6},{6,7},{7,8},{8,9},{9,10},{10,1... | collective-permute-start | bytes 3932168 | tf_op jit(solution)/shard_map/ppermute | solution.py:106
  287.0 56.5 %all-to-all-start.4 = ((bf16[128,2,2560]{2,1,0:T(2,128)(2,1)}), bf16[128,2,2560]{2,1,0:T(2,128)(2,1)S(1)}, u32[]{:S(2)}, u32[]{:S(2)}) async-start(bf16[128,2,2560]{2,1,0:T(2,128)(2,1)} %all_to_all.58), calls=%async_computation.4 | async-start | bytes 2621440 | tf_op jit(solution)/shard_map/all_to_all | solution.py:170
  293.4 44.7 %copy-start.9 = (f32[256,1280]{1,0:T(8,128)S(1)}, f32[256,1280]{1,0:T(8,128)}, u32[]{:S(2)}) copy-start(f32[256,1280]{1,0:T(8,128)} %get-tuple-element.40) | copy-start | bytes 3932164
  293.4 44.7 %copy-start.10 = (f32[256,1280]{1,0:T(8,128)S(1)}, f32[256,1280]{1,0:T(8,128)}, u32[]{:S(2)}) copy-start(f32[256,1280]{1,0:T(8,128)} %get-tuple-element.45) | copy-start | bytes 3932164
  343.6 30.5 %all-to-all-start.5 = ((bf16[128,2,2560]{2,1,0:T(2,128)(2,1)}), bf16[128,2,2560]{2,1,0:T(2,128)(2,1)}, u32[]{:S(2)}, u32[]{:S(2)}) async-start(bf16[128,2,2560]{2,1,0:T(2,128)(2,1)} %all_to_all.61), calls=%async_computation.5 | async-start | bytes 2621440 | tf_op jit(solution)/shard_map/all_to_all | solution.py:170
  (10 other events, 47.0 us)

commit v6 on v5

--- a/solution.py
+++ b/solution.py
@@ -12,6 +12,7 @@
 TILE = 256
 SETS = 5
 CHUNKS = 2
+HEAD_SPLIT = (8, 12)
 NT_DIMS = (((1,), (1,)), ((), ()))
 TN_DIMS = (((0,), (0,)), ((), ()))
 
@@ -125,11 +126,13 @@
     flags = jnp.stack(
         [own_reach[0] > 0, own_reach[0] >= 0, own_reach[1] > 0, column > 0, column < space_count - 1]
     ).astype(jnp.int32)
-    width = channels // CHUNKS
+    starts = [sum(HEAD_SPLIT[:c]) * HD for c in range(CHUNKS)]
+    widths = [n * HD for n in HEAD_SPLIT]
     backs = []
     gate = None
     for chunk in range(CHUNKS):
-        cols = slice(chunk * width, (chunk + 1) * width)
+        width = widths[chunk]
+        cols = slice(starts[chunk], starts[chunk] + width)
         send = jnp.concatenate([rows[:, cols] for rows in gathered], axis=1)
         recv = lax.all_to_all(send, ("tm", "space"), split_axis=0, concat_axis=0, tiled=True)
         kv_own = jnp.stack([recv[:, width:2 * width], recv[:, 2 * width:3 * width]])
@@ -152,6 +155,7 @@
     prior = None
     for chunk in range(CHUNKS):
         early, key_own, value_own, nb_b, nb_a, nb_l, nb_r = backs[chunk]
+        width = widths[chunk]
         sends = (nb_b, nb_a, nb_l, nb_r)
         if prior is None and CHUNKS > 1:
             sends = lax.optimization_barrier(sends + gate)[:4]
@@ -170,7 +174,9 @@
         late = lax.all_to_all(late, ("tm", "space"), split_axis=0, concat_axis=0, tiled=True)
         outs.append(jnp.concatenate([early, late], axis=1))
     return tuple(
-        jnp.concatenate([outs[chunk][:, i * width:(i + 1) * width] for chunk in range(CHUNKS)], axis=1)[landing]
+        jnp.concatenate(
+            [outs[chunk][:, i * widths[chunk]:(i + 1) * widths[chunk]] for chunk in range(CHUNKS)], axis=1
+        )[landing]
         for i in range(4)
     )
 

time: 386 us -> 418 us (1.083)
  waiting for transfers between devices: 152 us -> 188 us
  starting transfers between devices: 107 us -> 102 us
    all_to_all x2, waiting for transfers between devices: 17.5 us -> 53.5 us  [shards(): lax.all_to_all(early, ('tm', 'space'), split_axis=0, concat_axis=0, tiled...]
    ppermute x16, waiting for transfers between devices: 75.7 us -> 65.1 us  [shifted(): return lax.ppermute(block, axis, route)]
    all_to_all x2, waiting for transfers between devices: 13.1 us -> 23.4 us  [shards(): lax.all_to_all(late, ('tm', 'space'), split_axis=0, concat_axis=0, tiled=...]
  transfers between devices with their start and end apart: 22 -> 22, of which waited for: 9 -> 9; matrix products, arithmetic and copies ran while one was open for 7% -> 6% of each run, Pallas kernels for 12% -> 11%
where the time goes in v6:
time: 418 us; the launch traced here: 417 us
  waiting for transfers between devices  188 us (45%)
  starting transfers between devices  102 us (24%)
  local copies, waits for them, and re-layouts  62.6 us (15%)
  Pallas kernels  44.9 us (11%)
  other arithmetic  15.9 us (4%)
    ppermute x16, waiting for transfers between devices, shifted(): return lax.ppermute(block, axis, route)  65.1 us
    all_to_all x2, waiting for transfers between devices, shards(): lax.all_to_all(early, ('tm', 'space'), split_axis=0, concat_axis=0, tiled...  53.5 us
    ppermute x16, starting transfers between devices, shifted(): return lax.ppermute(block, axis, route)  48.9 us
    all_to_all x2, waiting for transfers between devices, shards(): lax.all_to_all(send, ('tm', 'space'), split_axis=0, concat_axis=0, tiled=...  46.3 us
    pallas_call x2, Pallas kernels, attend_tile(): pl.pallas_call(_attn_kernel, out_shape=out_shape, grid_spec=pltpu.Prefetc...  44.9 us
    all_to_all x2, waiting for transfers between devices, shards(): lax.all_to_all(late, ('tm', 'space'), split_axis=0, concat_axis=0, tiled=...  23.4 us
    all_to_all x2, starting transfers between devices, shards(): lax.all_to_all(early, ('tm', 'space'), split_axis=0, concat_axis=0, tiled...  21.6 us
    all_to_all x2, starting transfers between devices, shards(): lax.all_to_all(send, ('tm', 'space'), split_axis=0, concat_axis=0, tiled=...  16.7 us
  transfers between devices with their start and end apart: 22, of which 9 were waited for; matrix products, arithmetic and copies ran while one was open for 6% of the time, Pallas kernels for 11%

profile of v6, /device:TPU:1, one launch (start us, length us, event | category | flops | bytes accessed | tf_op | source)
XLA Modules:
  0.0 416.6 jit_solution(7918526640008807373)
XLA Ops:
  20.8 11.9 %all-to-all-start = ((bf16[128,2,4096]{2,1,0:T(2,128)(2,1)}), bf16[128,2,4096]{2,1,0:T(2,128)(2,1)}, u32[]{:S(2)}, u32[]{:S(2)}) async-start(bf16[128,2,4096]{2,1,0:T(2,128)(2,1)} %all_to_all.46), calls=%async_computation | async-start | bytes 4194304 | tf_op jit(solution)/shard_map/all_to_all | solution.py:137
  38.3 24.1 %all-to-all-done = bf16[128,2,4096]{2,1,0:T(2,128)(2,1)} async-done(((bf16[128,2,4096]{2,1,0:T(2,128)(2,1)}), bf16[128,2,4096]{2,1,0:T(2,128)(2,1)}, u32[]{:S(2)}, u32[]{:S(2)}) %all-to-all-start) | async-done | bytes 2097184 | tf_op jit(solution)/shard_map/all_to_all | solution.py:137
  62.4 4.7 %all-to-all-start.2 = ((bf16[128,2,6144]{2,1,0:T(2,128)(2,1)}), bf16[128,2,6144]{2,1,0:T(2,128)(2,1)S(1)}, u32[]{:S(2)}, u32[]{:S(2)}) async-start(bf16[128,2,6144]{2,1,0:T(2,128)(2,1)} %all_to_all.52), calls=%async_computation.2 | async-start | bytes 6291456 | tf_op jit(solution)/shard_map/all_to_all | solution.py:137
  67.1 4.1 all_to_all.48.q_ref.g_ref.k_ref.v_ref
  73.6 5.2 %collective-permute-start = (bf16[2,256,1024]{2,1,0:T(8,128)(2,1)}, bf16[2,256,1024]{2,1,0:T(8,128)(2,1)}, u32[]{:S(2)}, u32[]{:S(2)}) collective-permute-start(bf16[2,256,1024]{2,1,0:T(8,128)(2,1)} %pad_maximum_fusion.9), channel_id=1, source_target_pairs={{0,32},{32,64},{64,96},{1,33},{33,65},{65,97},{2,34},{34,66},{66,9... | collective-permute-start | bytes 3145736 | tf_op jit(solution)/shard_map/ppermute | solution.py:107
  80.7 4.4 %collective-permute-start.2 = (bf16[2,256,1024]{2,1,0:T(8,128)(2,1)}, bf16[2,256,1024]{2,1,0:T(8,128)(2,1)}, u32[]{:S(2)}, u32[]{:S(2)}) collective-permute-start(bf16[2,256,1024]{2,1,0:T(8,128)(2,1)} %pad_maximum_fusion.9), channel_id=1, source_target_pairs={{0,1},{1,2},{2,3},{3,4},{4,5},{5,6},{6,7},{7,8},{8,9},{9,10},{10,1... | collective-permute-start | bytes 3145736 | tf_op jit(solution)/shard_map/ppermute | solution.py:107
  86.4 22.2 %all-to-all-done.2 = bf16[128,2,6144]{2,1,0:T(2,128)(2,1)S(1)} async-done(((bf16[128,2,6144]{2,1,0:T(2,128)(2,1)}), bf16[128,2,6144]{2,1,0:T(2,128)(2,1)S(1)}, u32[]{:S(2)}, u32[]{:S(2)}) %all-to-all-start.2) | async-done | bytes 3145760 | tf_op jit(solution)/shard_map/all_to_all | solution.py:137
  112.9 21.9 %collective-permute-done.kb_ref = bf16[2,256,1024]{2,1,0:T(8,128)(2,1)} collective-permute-done((bf16[2,256,1024]{2,1,0:T(8,128)(2,1)}, bf16[2,256,1024]{2,1,0:T(8,128)(2,1)}, u32[]{:S(2)}, u32[]{:S(2)}) %collective-permute-start) | collective-permute-done | bytes 1048608 | tf_op jit(solution)/shard_map/ppermute | solution.py:107
  150.7 18.5 %shard_map.93 = (bf16[256,1024]{1,0:T(8,128)(2,1)}, bf16[256,1024]{1,0:T(8,128)(2,1)}, f32[256,1024]{1,0:T(8,128)}, f32[256,1024]{1,0:T(8,128)}, bf16[2,256,1024...) custom-call(s32[5]{0:T(128)} %convert_element_type.39.flags_ref, ...), custom_call_target="tpu_custom_call" | custom-call | flops 4026531840 | bytes 17825792 | tf_op jit(solution)/shard_map/pallas_call | solution.py:84
  169.2 22.5 %collective-permute-done.4.kb_ref = bf16[2,256,1536]{2,1,0:T(8,128)(2,1)} collective-permute-done((bf16[2,256,1536]{2,1,0:T(8,128)(2,1)S(1)}, bf16[2,256,1536]{2,1,0:T(8,128)(2,1)}, u32[]{:S(2)}, u32[]{:S(2)}) %collective-permute-start.4) | collective-permute-done | bytes 1572896 | tf_op jit(solution)/shard_map/ppermute | solution.py:107
  191.7 17.2 %collective-permute-done.5.ka_ref = bf16[2,256,1536]{2,1,0:T(8,128)(2,1)} collective-permute-done((bf16[2,256,1536]{2,1,0:T(8,128)(2,1)S(1)}, bf16[2,256,1536]{2,1,0:T(8,128)(2,1)}, u32[]{:S(2)}, u32[]{:S(2)}) %collective-permute-start.5) | collective-permute-done | bytes 1572896 | tf_op jit(solution)/shard_map/ppermute | solution.py:107
  210.3 5.0 %collective-permute-start.11 = (bf16[2,256,1024]{2,1,0:T(8,128)(2,1)}, bf16[2,256,1024]{2,1,0:T(8,128)(2,1)}, u32[]{:S(2)}, u32[]{:S(2)}) collective-permute-start(bf16[2,256,1024]{2,1,0:T(8,128)(2,1)} %get-tuple-element.38), channel_id=1, source_target_pairs={{0,1},{1,2},{2,3},{3,4},{4,5},{5,6},{6,7},{7,8},{8,9},{9,10},{10,1... | collective-permute-start | bytes 3145736 | tf_op jit(solution)/shard_map/ppermute | solution.py:107
  220.1 12.8 %all-to-all-start.1 = ((bf16[128,2,2048]{2,1,0:T(2,128)(2,1)}), bf16[128,2,2048]{2,1,0:T(2,128)(2,1)S(1)}, u32[]{:S(2)}, u32[]{:S(2)}) async-start(bf16[128,2,2048]{2,1,0:T(2,128)(2,1)} %all_to_all.49), calls=%async_computation.1 | async-start | bytes 2097152 | tf_op jit(solution)/shard_map/all_to_all | solution.py:152
  233.0 5.1 %collective-permute-start.9 = (bf16[2,256,1024]{2,1,0:T(8,128)(2,1)}, bf16[2,256,1024]{2,1,0:T(8,128)(2,1)}, u32[]{:S(2)}, u32[]{:S(2)}) collective-permute-start(bf16[2,256,1024]{2,1,0:T(8,128)(2,1)} %get-tuple-element.36), channel_id=1, source_target_pairs={{0,32},{32,64},{64,96},{1,33},{33,65},{65,97},{2,34},{34,66},{66,9... | collective-permute-start | bytes 3145736 | tf_op jit(solution)/shard_map/ppermute | solution.py:107
  238.0 26.5 %shard_map.94 = (bf16[256,1536]{1,0:T(8,128)(2,1)}, bf16[256,1536]{1,0:T(8,128)(2,1)}, f32[256,1536]{1,0:T(8,128)}, f32[256,1536]{1,0:T(8,128)}, bf16[2,256,1536...) custom-call(s32[5]{0:T(128)} %convert_element_type.39.flags_ref, ...), custom_call_target="tpu_custom_call" | custom-call | flops 6039797760 | bytes 26738688 | tf_op jit(solution)/shard_map/pallas_call | solution.py:84
  266.4 5.1 %collective-permute-start.13 = (bf16[2,256,1536]{2,1,0:T(8,128)(2,1)}, bf16[2,256,1536]{2,1,0:T(8,128)(2,1)}, u32[]{:S(2)}, u32[]{:S(2)}) collective-permute-start(bf16[2,256,1536]{2,1,0:T(8,128)(2,1)} %get-tuple-element.42), channel_id=1, source_target_pairs={{0,32},{32,64},{64,96},{1,33},{33,65},{65,97},{2,34},{34,66},{66,9... | collective-permute-start | bytes 4718600 | tf_op jit(solution)/shard_map/ppermute | solution.py:107
  272.9 5.2 %collective-permute-start.15 = (bf16[2,256,1536]{2,1,0:T(8,128)(2,1)}, bf16[2,256,1536]{2,1,0:T(8,128)(2,1)}, u32[]{:S(2)}, u32[]{:S(2)}) collective-permute-start(bf16[2,256,1536]{2,1,0:T(8,128)(2,1)} %get-tuple-element.44), channel_id=1, source_target_pairs={{0,1},{1,2},{2,3},{3,4},{4,5},{5,6},{6,7},{7,8},{8,9},{9,10},{10,1... | collective-permute-start | bytes 4718600 | tf_op jit(solution)/shard_map/ppermute | solution.py:107
  282.1 8.8 %all-to-all-start.3 = ((bf16[128,2,3072]{2,1,0:T(2,128)(2,1)}), bf16[128,2,3072]{2,1,0:T(2,128)(2,1)S(1)}, u32[]{:S(2)}, u32[]{:S(2)}) async-start(bf16[128,2,3072]{2,1,0:T(2,128)(2,1)} %all_to_all.55), calls=%async_computation.3 | async-start | bytes 3145728 | tf_op jit(solution)/shard_map/all_to_all | solution.py:152
  296.2 53.5 %all-to-all-done.3 = bf16[128,2,3072]{2,1,0:T(2,128)(2,1)S(1)} async-done(((bf16[128,2,3072]{2,1,0:T(2,128)(2,1)}), bf16[128,2,3072]{2,1,0:T(2,128)(2,1)S(1)}, u32[]{:S(2)}, u32[]{:S(2)}) %all-to-all-start.3) | async-done | bytes 1572896 | tf_op jit(solution)/shard_map/all_to_all | solution.py:152
  349.7 8.6 %all-to-all-start.4 = ((bf16[128,2,2048]{2,1,0:T(2,128)(2,1)}), bf16[128,2,2048]{2,1,0:T(2,128)(2,1)}, u32[]{:S(2)}, u32[]{:S(2)}) async-start(bf16[128,2,2048]{2,1,0:T(2,128)(2,1)} %all_to_all.58), calls=%async_computation.4 | async-start | bytes 2097152 | tf_op jit(solution)/shard_map/all_to_all | solution.py:174
  358.4 3.8 convert_add_fusion
  364.6 12.1 %all-to-all-done.4 = bf16[128,2,2048]{2,1,0:T(2,128)(2,1)} async-done(((bf16[128,2,2048]{2,1,0:T(2,128)(2,1)}), bf16[128,2,2048]{2,1,0:T(2,128)(2,1)}, u32[]{:S(2)}, u32[]{:S(2)}) %all-to-all-start.4) | async-done | bytes 1048608 | tf_op jit(solution)/shard_map/all_to_all | solution.py:174
  376.7 5.8 %all-to-all-start.5 = ((bf16[128,2,3072]{2,1,0:T(2,128)(2,1)}), bf16[128,2,3072]{2,1,0:T(2,128)(2,1)}, u32[]{:S(2)}, u32[]{:S(2)}) async-start(bf16[128,2,3072]{2,1,0:T(2,128)(2,1)} %all_to_all.61), calls=%async_computation.5 | async-start | bytes 3145728 | tf_op jit(solution)/shard_map/all_to_all | solution.py:174
  395.3 11.3 %all-to-all-done.5 = bf16[128,2,3072]{2,1,0:T(2,128)(2,1)} async-done(((bf16[128,2,3072]{2,1,0:T(2,128)(2,1)}), bf16[128,2,3072]{2,1,0:T(2,128)(2,1)}, u32[]{:S(2)}, u32[]{:S(2)}) %all-to-all-start.5) | async-done | bytes 1572896 | tf_op jit(solution)/shard_map/all_to_all | solution.py:174
  (117 shorter events, 93.1 us)
Async XLA Ops:
  20.8 41.6 %all-to-all-start = ((bf16[128,2,4096]{2,1,0:T(2,128)(2,1)}), bf16[128,2,4096]{2,1,0:T(2,128)(2,1)}, u32[]{:S(2)}, u32[]{:S(2)}) async-start(bf16[128,2,4096]{2,1,0:T(2,128)(2,1)} %all_to_all.46), calls=%async_computation | async-start | bytes 4194304 | tf_op jit(solution)/shard_map/all_to_all | solution.py:137
  62.4 46.1 %all-to-all-start.2 = ((bf16[128,2,6144]{2,1,0:T(2,128)(2,1)}), bf16[128,2,6144]{2,1,0:T(2,128)(2,1)S(1)}, u32[]{:S(2)}, u32[]{:S(2)}) async-start(bf16[128,2,6144]{2,1,0:T(2,128)(2,1)} %all_to_all.52), calls=%async_computation.2 | async-start | bytes 6291456 | tf_op jit(solution)/shard_map/all_to_all | solution.py:137
  73.6 61.2 %collective-permute-start = (bf16[2,256,1024]{2,1,0:T(8,128)(2,1)}, bf16[2,256,1024]{2,1,0:T(8,128)(2,1)}, u32[]{:S(2)}, u32[]{:S(2)}) collective-permute-start(bf16[2,256,1024]{2,1,0:T(8,128)(2,1)} %pad_maximum_fusion.9), channel_id=1, source_target_pairs={{0,32},{32,64},{64,96},{1,33},{33,65},{65,97},{2,34},{34,66},{66,9... | collective-permute-start | bytes 3145736 | tf_op jit(solution)/shard_map/ppermute | solution.py:107
  78.8 59.4 %collective-permute-start.1 = (bf16[2,256,1024]{2,1,0:T(8,128)(2,1)}, bf16[2,256,1024]{2,1,0:T(8,128)(2,1)}, u32[]{:S(2)}, u32[]{:S(2)}) collective-permute-start(bf16[2,256,1024]{2,1,0:T(8,128)(2,1)} %pad_maximum_fusion.9), channel_id=1, source_target_pairs={{32,0},{64,32},{96,64},{33,1},{65,33},{97,65},{34,2},{66,34},{98,6... | collective-permute-start | bytes 3145736 | tf_op jit(solution)/shard_map/ppermute | solution.py:107
  80.7 57.4 %collective-permute-start.2 = (bf16[2,256,1024]{2,1,0:T(8,128)(2,1)}, bf16[2,256,1024]{2,1,0:T(8,128)(2,1)}, u32[]{:S(2)}, u32[]{:S(2)}) collective-permute-start(bf16[2,256,1024]{2,1,0:T(8,128)(2,1)} %pad_maximum_fusion.9), channel_id=1, source_target_pairs={{0,1},{1,2},{2,3},{3,4},{4,5},{5,6},{6,7},{7,8},{8,9},{9,10},{10,1... | collective-permute-start | bytes 3145736 | tf_op jit(solution)/shard_map/ppermute | solution.py:107
  85.1 53.1 %collective-permute-start.3 = (bf16[2,256,1024]{2,1,0:T(8,128)(2,1)}, bf16[2,256,1024]{2,1,0:T(8,128)(2,1)}, u32[]{:S(2)}, u32[]{:S(2)}) collective-permute-start(bf16[2,256,1024]{2,1,0:T(8,128)(2,1)} %pad_maximum_fusion.9), channel_id=1, source_target_pairs={{1,0},{2,1},{3,2},{4,3},{5,4},{6,5},{7,6},{8,7},{9,8},{10,9},{11,1... | collective-permute-start | bytes 3145736 | tf_op jit(solution)/shard_map/ppermute | solution.py:107
  112.7 34.8 %copy-start.15 = (s32[4,1,2]{0,2,1:T(2,128)S(1)}, s32[4,1,2]{0,2,1:T(2,128)}, u32[]{:S(2)}) copy-start(s32[4,1,2]{0,2,1:T(2,128)} %param.11) | copy-start | bytes 100
  138.2 53.6 %collective-permute-start.4 = (bf16[2,256,1536]{2,1,0:T(8,128)(2,1)S(1)}, bf16[2,256,1536]{2,1,0:T(8,128)(2,1)}, u32[]{:S(2)}, u32[]{:S(2)}) collective-permute-start(bf16[2,256,1536]{2,1,0:T(8,128)(2,1)S(1)} %pad_maximum_fusion.2), channel_id=1, source_target_pairs={{0,32},{32,64},{64,96},{1,33},{33,65},{65,97},{2,34},{34,66},{66,9... | collective-permute-start | bytes 4718600 | tf_op jit(solution)/shard_map/ppermute | solution.py:107
  140.7 68.3 %collective-permute-start.5 = (bf16[2,256,1536]{2,1,0:T(8,128)(2,1)S(1)}, bf16[2,256,1536]{2,1,0:T(8,128)(2,1)}, u32[]{:S(2)}, u32[]{:S(2)}) collective-permute-start(bf16[2,256,1536]{2,1,0:T(8,128)(2,1)S(1)} %pad_maximum_fusion.2), channel_id=1, source_target_pairs={{32,0},{64,32},{96,64},{33,1},{65,33},{97,65},{34,2},{66,34},{98,6... | collective-permute-start | bytes 4718600 | tf_op jit(solution)/shard_map/ppermute | solution.py:107
  143.7 65.3 %collective-permute-start.6 = (bf16[2,256,1536]{2,1,0:T(8,128)(2,1)S(1)}, bf16[2,256,1536]{2,1,0:T(8,128)(2,1)}, u32[]{:S(2)}, u32[]{:S(2)}) collective-permute-start(bf16[2,256,1536]{2,1,0:T(8,128)(2,1)S(1)} %pad_maximum_fusion.2), channel_id=1, source_target_pairs={{0,1},{1,2},{2,3},{3,4},{4,5},{5,6},{6,7},{7,8},{8,9},{9,10},{10,1... | collective-permute-start | bytes 4718600 | tf_op jit(solution)/shard_map/ppermute | solution.py:107
  146.2 62.8 %collective-permute-start.7 = (bf16[2,256,1536]{2,1,0:T(8,128)(2,1)S(1)}, bf16[2,256,1536]{2,1,0:T(8,128)(2,1)}, u32[]{:S(2)}, u32[]{:S(2)}) collective-permute-start(bf16[2,256,1536]{2,1,0:T(8,128)(2,1)S(1)} %pad_maximum_fusion.2), channel_id=1, source_target_pairs={{1,0},{2,1},{3,2},{4,3},{5,4},{6,5},{7,6},{8,7},{9,8},{10,9},{11,1... | collective-permute-start | bytes 4718600 | tf_op jit(solution)/shard_map/ppermute | solution.py:107
  209.0 57.4 %collective-permute-start.10 = (bf16[2,256,1024]{2,1,0:T(8,128)(2,1)}, bf16[2,256,1024]{2,1,0:T(8,128)(2,1)}, u32[]{:S(2)}, u32[]{:S(2)}) collective-permute-start(bf16[2,256,1024]{2,1,0:T(8,128)(2,1)} %get-tuple-element.37), channel_id=1, source_target_pairs={{1,0},{2,1},{3,2},{4,3},{5,4},{6,5},{7,6},{8,7},{9,8},{10,9},{11,1... | collective-permute-start | bytes 3145736 | tf_op jit(solution)/shard_map/ppermute | solution.py:107
  210.3 61.3 %collective-permute-start.11 = (bf16[2,256,1024]{2,1,0:T(8,128)(2,1)}, bf16[2,256,1024]{2,1,0:T(8,128)(2,1)}, u32[]{:S(2)}, u32[]{:S(2)}) collective-permute-start(bf16[2,256,1024]{2,1,0:T(8,128)(2,1)} %get-tuple-element.38), channel_id=1, source_target_pairs={{0,1},{1,2},{2,3},{3,4},{4,5},{5,6},{6,7},{7,8},{8,9},{9,10},{10,1... | collective-permute-start | bytes 3145736 | tf_op jit(solution)/shard_map/ppermute | solution.py:107
  215.2 57.7 %collective-permute-start.8 = (bf16[2,256,1024]{2,1,0:T(8,128)(2,1)}, bf16[2,256,1024]{2,1,0:T(8,128)(2,1)}, u32[]{:S(2)}, u32[]{:S(2)}) collective-permute-start(bf16[2,256,1024]{2,1,0:T(8,128)(2,1)} %get-tuple-element.35), channel_id=1, source_target_pairs={{32,0},{64,32},{96,64},{33,1},{65,33},{97,65},{34,2},{66,34},{98,6... | collective-permute-start | bytes 3145736 | tf_op jit(solution)/shard_map/ppermute | solution.py:107
  220.1 61.0 %all-to-all-start.1 = ((bf16[128,2,2048]{2,1,0:T(2,128)(2,1)}), bf16[128,2,2048]{2,1,0:T(2,128)(2,1)S(1)}, u32[]{:S(2)}, u32[]{:S(2)}) async-start(bf16[128,2,2048]{2,1,0:T(2,128)(2,1)} %all_to_all.49), calls=%async_computation.1 | async-start | bytes 2097152 | tf_op jit(solution)/shard_map/all_to_all | solution.py:152
  233.0 58.0 %collective-permute-start.9 = (bf16[2,256,1024]{2,1,0:T(8,128)(2,1)}, bf16[2,256,1024]{2,1,0:T(8,128)(2,1)}, u32[]{:S(2)}, u32[]{:S(2)}) collective-permute-start(bf16[2,256,1024]{2,1,0:T(8,128)(2,1)} %get-tuple-element.36), channel_id=1, source_target_pairs={{0,32},{32,64},{64,96},{1,33},{33,65},{65,97},{2,34},{34,66},{66,9... | collective-permute-start | bytes 3145736 | tf_op jit(solution)/shard_map/ppermute | solution.py:107
  264.5 93.8 %collective-permute-start.12 = (bf16[2,256,1536]{2,1,0:T(8,128)(2,1)}, bf16[2,256,1536]{2,1,0:T(8,128)(2,1)}, u32[]{:S(2)}, u32[]{:S(2)}) collective-permute-start(bf16[2,256,1536]{2,1,0:T(8,128)(2,1)} %get-tuple-element.41), channel_id=1, source_target_pairs={{32,0},{64,32},{96,64},{33,1},{65,33},{97,65},{34,2},{66,34},{98,6... | collective-permute-start | bytes 4718600 | tf_op jit(solution)/shard_map/ppermute | solution.py:107
  266.4 91.9 %collective-permute-start.13 = (bf16[2,256,1536]{2,1,0:T(8,128)(2,1)}, bf16[2,256,1536]{2,1,0:T(8,128)(2,1)}, u32[]{:S(2)}, u32[]{:S(2)}) collective-permute-start(bf16[2,256,1536]{2,1,0:T(8,128)(2,1)} %get-tuple-element.42), channel_id=1, source_target_pairs={{0,32},{32,64},{64,96},{1,33},{33,65},{65,97},{2,34},{34,66},{66,9... | collective-permute-start | bytes 4718600 | tf_op jit(solution)/shard_map/ppermute | solution.py:107
  271.6 86.7 %collective-permute-start.14 = (bf16[2,256,1536]{2,1,0:T(8,128)(2,1)}, bf16[2,256,1536]{2,1,0:T(8,128)(2,1)}, u32[]{:S(2)}, u32[]{:S(2)}) collective-permute-start(bf16[2,256,1536]{2,1,0:T(8,128)(2,1)} %get-tuple-element.43), channel_id=1, source_target_pairs={{1,0},{2,1},{3,2},{4,3},{5,4},{6,5},{7,6},{8,7},{9,8},{10,9},{11,1... | collective-permute-start | bytes 4718600 | tf_op jit(solution)/shard_map/ppermute | solution.py:107
  272.9 85.4 %collective-permute-start.15 = (bf16[2,256,1536]{2,1,0:T(8,128)(2,1)}, bf16[2,256,1536]{2,1,0:T(8,128)(2,1)}, u32[]{:S(2)}, u32[]{:S(2)}) collective-permute-start(bf16[2,256,1536]{2,1,0:T(8,128)(2,1)} %get-tuple-element.44), channel_id=1, source_target_pairs={{0,1},{1,2},{2,3},{3,4},{4,5},{5,6},{6,7},{7,8},{8,9},{9,10},{10,1... | collective-permute-start | bytes 4718600 | tf_op jit(solution)/shard_map/ppermute | solution.py:107
  282.1 67.6 %all-to-all-start.3 = ((bf16[128,2,3072]{2,1,0:T(2,128)(2,1)}), bf16[128,2,3072]{2,1,0:T(2,128)(2,1)S(1)}, u32[]{:S(2)}, u32[]{:S(2)}) async-start(bf16[128,2,3072]{2,1,0:T(2,128)(2,1)} %all_to_all.55), calls=%async_computation.3 | async-start | bytes 3145728 | tf_op jit(solution)/shard_map/all_to_all | solution.py:152
  349.7 27.0 %all-to-all-start.4 = ((bf16[128,2,2048]{2,1,0:T(2,128)(2,1)}), bf16[128,2,2048]{2,1,0:T(2,128)(2,1)}, u32[]{:S(2)}, u32[]{:S(2)}) async-start(bf16[128,2,2048]{2,1,0:T(2,128)(2,1)} %all_to_all.58), calls=%async_computation.4 | async-start | bytes 2097152 | tf_op jit(solution)/shard_map/all_to_all | solution.py:174
  364.6 17.9 %copy-start.7 = (bf16[128,2,2048]{2,1,0:T(2,128)(2,1)S(1)}, bf16[128,2,2048]{2,1,0:T(2,128)(2,1)}, u32[]{:S(2)}) copy-start(bf16[128,2,2048]{2,1,0:T(2,128)(2,1)} %copy-done.6) | copy-start | bytes 3145732
  376.7 29.9 %all-to-all-start.5 = ((bf16[128,2,3072]{2,1,0:T(2,128)(2,1)}), bf16[128,2,3072]{2,1,0:T(2,128)(2,1)}, u32[]{:S(2)}, u32[]{:S(2)}) async-start(bf16[128,2,3072]{2,1,0:T(2,128)(2,1)} %all_to_all.61), calls=%async_computation.5 | async-start | bytes 3145728 | tf_op jit(solution)/shard_map/all_to_all | solution.py:174
  (19 other events, 43.9 us)
